TPU v7x, 256 devices: a whole 4x4x8 slice. The times are simulated.
256 devices in a mesh: section: 2 (over core), dp: 4 (over y), ctx: 32 (over x, z).
Axes of the slice: x: 4, y: 4, z: 8, core: 2. Of those that a mesh axis runs over, the one named last changes fastest.
Arguments:
- tokens: bfloat16 [8, 4096, 2048], P('dp', 'ctx'), parts along dimension 0, may hold values from -6 to 6
- w_qkv: bfloat16 [2, 2048, 4096], P('section', 'ctx'), may hold values from -0.125 to 0.125
- w_gate: bfloat16 [2, 2048, 32], P('section', 'ctx'), may hold values from -0.125 to 0.125
- norm_gain: float32 [2, 2048], P('section'), may hold values from 0.5 to 1.5
- conv_weight: bfloat16 [2, 4, 4096], P('section'), may hold values from -3 to 3
- decay_rate: float32 [2, 16], P('section'), may hold values from 2.4414063e-05 to 0.08
- dt_bias: float32 [2, 16], P('section'), may hold values from -1 to 1
- head_gain: float32 [2, 128], P('section'), may hold values from 0.1 to 1.9
Outputs:
- final_hidden: bfloat16 [8, 4096, 2048], P(('dp', 'section'), 'ctx'), parts along dimension 0
There are 4 independent parts, one for each index of `dp`. A program takes and returns all parts, laid end to end along the dimension named above; an argument that names none is the same for every part. Nothing has to cross between parts.
All inputs are finite; a program needn't handle non-finite values.
Results may differ from a plain program's by a relative error of at most 0.022.
Values may be sent and summed in bfloat16 or wider, within the bound.
No kernel may reach another device: no remote copies, remote signals or barrier semaphores. Data moves between devices by JAX's collectives and lax.ppermute only.
A program may use at most 320 MiB of HBM per device.

v0:
```python
import jax
import jax.numpy as jnp
from jax import lax
from jax.sharding import PartitionSpec as P

NK = 8
NV = 16
DK = 128
DV = 128
CONV = 4
BLOCK = 128


PRECISE = lax.Precision.HIGHEST


def from_behind(value, axis, by):
    length = lax.axis_size(axis)
    pairs = [(i, i + by) for i in range(length) if 0 <= i + by < length]
    return lax.ppermute(value, axis, pairs)


def rms_rows(values, gain_row):
    inverse = lax.rsqrt(jnp.mean(values * values, axis=-1, keepdims=True) + 1e-06)
    return values * inverse * gain_row


def unit_rows(values):
    return values * lax.rsqrt(jnp.sum(values * values, axis=-1, keepdims=True) + 1e-06)


def conv_rows(padded, conv_taps):
    tap_count = conv_taps.shape[0]
    length = padded.shape[-2] - tap_count + 1
    running_sum = jnp.zeros(padded.shape[:-2] + (length, padded.shape[-1]), jnp.float32)
    for offset in range(tap_count):
        running_sum = running_sum + conv_taps[offset].astype(jnp.float32) * padded[
            ..., offset : offset + length, :
        ].astype(jnp.float32)
    return jax.nn.silu(running_sum).astype(jnp.bfloat16)


def head_inputs(mixed_rows, gate_raw, decay_rates, biases):
    row_count = mixed_rows.shape[0]
    features = mixed_rows.astype(jnp.float32)
    queries = unit_rows(features[:, : NK * DK].reshape(row_count, NK, DK)) * DK ** (-0.5)
    key_rows = unit_rows(features[:, NK * DK : 2 * NK * DK].reshape(row_count, NK, DK))
    values = features[:, 2 * NK * DK :].reshape(row_count, NV, DV)
    queries = jnp.repeat(queries, NV // NK, axis=1)
    key_rows = jnp.repeat(key_rows, NV // NK, axis=1)
    gate_float = gate_raw.astype(jnp.float32)
    strength = jax.nn.sigmoid(gate_float[:, :NV])
    logdecay = -decay_rates * jax.nn.softplus(gate_float[:, NV:] + biases)
    return (queries, key_rows, values, strength, logdecay)


def block_parts(queries, key_rows, values, strength, logdecay):
    block_len = queries.shape[1]
    cumulative = jnp.swapaxes(jnp.cumsum(logdecay, axis=1), 1, 2)
    beta_heads = jnp.swapaxes(strength, 1, 2)
    query_heads = jnp.swapaxes(queries, 1, 2)
    key_heads = jnp.swapaxes(key_rows, 1, 2)
    value_heads = jnp.swapaxes(values, 1, 2)
    places = jnp.arange(block_len)
    lower_mask = places[:, None] >= places[None, :]
    strict_mask = places[:, None] > places[None, :]
    log_gap = cumulative[..., :, None] - cumulative[..., None, :]
    decay_ratio = jnp.where(lower_mask, jnp.exp(jnp.where(lower_mask, log_gap, 0.0)), 0.0)
    key_inner = jnp.einsum("nhid,nhjd->nhij", key_heads, key_heads, precision=PRECISE)
    system = jnp.where(
        strict_mask, beta_heads[..., :, None] * key_inner * decay_ratio, 0.0
    ) + jnp.eye(block_len, dtype=queries.dtype)
    gamma_rows = jnp.exp(cumulative)
    right_side = jnp.concatenate(
        [beta_heads[..., None] * value_heads, (beta_heads * gamma_rows)[..., None] * key_heads],
        axis=-1,
    )
    solved = lax.linalg.triangular_solve(
        system, right_side, left_side=True, lower=True, unit_diagonal=True
    )
    fresh_rows = solved[..., : value_heads.shape[-1]]
    mixing = solved[..., value_heads.shape[-1] :]
    scores = jnp.einsum("nhid,nhjd->nhij", query_heads, key_heads, precision=PRECISE) * decay_ratio
    qgamma = gamma_rows[..., None] * query_heads
    key_tail = jnp.exp(cumulative[..., -1:] - cumulative)[..., None] * key_heads
    block_decay = gamma_rows[..., -1]
    return (fresh_rows, mixing, scores, qgamma, key_tail, block_decay)


def block_apply(state_now, block_items):
    fresh_rows, mixing, scores, qgamma, key_tail, block_decay = block_items
    update = fresh_rows - jnp.einsum("...cd,...de->...ce", mixing, state_now, precision=PRECISE)
    output = jnp.einsum("...cd,...de->...ce", qgamma, state_now, precision=PRECISE) + jnp.einsum(
        "...ij,...je->...ie", scores, update, precision=PRECISE
    )
    state_next = block_decay[..., None, None] * state_now + jnp.einsum(
        "...cd,...ce->...de", key_tail, update, precision=PRECISE
    )
    return (state_next, output)


def chain_product(left_map, right_map):
    return jnp.einsum("...ij,...jk->...ik", left_map, right_map, precision=PRECISE)


def local(tokens, w_qkv, w_gate, norm_gain, conv_weight, decay_rate, dt_bias, head_gain):
    weight_qkv = w_qkv[0]
    weight_gate = w_gate[0]
    gain_in = norm_gain[0]
    conv_taps = conv_weight[0]
    decay_rates = decay_rate[0]
    biases = dt_bias[0]
    gain_out = head_gain[0]
    full_qkv, full_gate = (
        lax.all_gather(weight_qkv, "ctx", axis=0, tiled=True),
        lax.all_gather(weight_gate, "ctx", axis=0, tiled=True),
    )
    head_section = lax.axis_index("section") == 0
    micro_count = tokens.shape[0]
    passed = jnp.zeros_like(tokens[0:1])
    results = []
    for step_index in range(micro_count + 1):
        section_input = jnp.where(
            head_section, tokens[min(step_index, micro_count - 1)][None], passed
        )
        groups, positions, model_width = section_input.shape
        blocks = positions // BLOCK
        layer_normed = (
            rms_rows(section_input.astype(jnp.float32), gain_in)
            .astype(jnp.bfloat16)
            .reshape(groups * positions, model_width)
        )
        proj_qkv = jnp.dot(layer_normed, full_qkv, preferred_element_type=jnp.float32)
        proj_gate = jnp.dot(layer_normed, full_gate, preferred_element_type=jnp.float32)
        features = proj_qkv.astype(jnp.bfloat16).reshape(groups, positions, proj_qkv.shape[1])
        gate_raw = proj_gate.astype(jnp.bfloat16)
        previous_rows = from_behind(features[:, positions - (CONV - 1) :], "ctx", 1)
        mixed_rows = conv_rows(jnp.concatenate([previous_rows, features], axis=1), conv_taps)
        queries, key_rows, values, strength, logdecay = head_inputs(
            mixed_rows.reshape(groups * positions, mixed_rows.shape[2]),
            gate_raw,
            decay_rates,
            biases,
        )
        count_blocks = groups * blocks
        parts = block_parts(
            queries.reshape(count_blocks, BLOCK, NV, DK),
            key_rows.reshape(count_blocks, BLOCK, NV, DK),
            values.reshape(count_blocks, BLOCK, NV, DV),
            strength.reshape(count_blocks, BLOCK, NV),
            logdecay.reshape(count_blocks, BLOCK, NV),
        )
        parts = tuple(
            (
                jnp.moveaxis(source.reshape((groups, blocks) + source.shape[1:]), 1, 0)
                for source in parts
            )
        )
        fresh_rows, mixing, scores, qgamma, key_tail, block_decay = parts
        identity = jnp.broadcast_to(jnp.eye(DK, dtype=jnp.float32), (groups, NV, DK, DK))
        no_state = jnp.zeros((groups, NV, DK, DV), jnp.float32)
        step_maps = block_decay[..., None, None] * identity - jnp.einsum(
            "...cd,...cf->...df", key_tail, mixing, precision=PRECISE
        )
        step_biases = jnp.einsum("...cd,...ce->...de", key_tail, fresh_rows, precision=PRECISE)

        def compose(running, block_items):
            map_now, bias_now = running
            step_map, step_bias = block_items
            return (
                (chain_product(step_map, map_now), chain_product(step_map, bias_now) + step_bias),
                None,
            )

        (local_map, local_bias), _ = lax.scan(
            compose, (identity, no_state), (step_maps, step_biases)
        )
        ctx_count = lax.axis_size("ctx")
        column_parts = max(1, ctx_count // NV)
        item_count = NV * column_parts
        part_width = DV // column_parts
        sent_maps = jnp.repeat(local_map, column_parts, axis=1)[None]
        sent_bias = jnp.moveaxis(local_bias.reshape(groups, NV, DK, column_parts, part_width), 3, 2)
        sent_bias = sent_bias.reshape(groups, item_count, DK, part_width)[None]
        got_maps = lax.all_to_all(sent_maps, "ctx", split_axis=2, concat_axis=0, tiled=True)
        got_bias = lax.all_to_all(sent_bias, "ctx", split_axis=2, concat_axis=0, tiled=True)

        def chain_step(state_now, incoming):
            return (chain_product(incoming[0], state_now) + incoming[1], state_now)

        _, entering_parts = lax.scan(
            chain_step, jnp.zeros(got_bias.shape[1:], jnp.float32), (got_maps, got_bias)
        )
        returned_states = lax.all_to_all(
            entering_parts, "ctx", split_axis=0, concat_axis=2, tiled=True
        )
        entering = returned_states[0].reshape(groups, NV, column_parts, DK, part_width)
        entering = jnp.moveaxis(entering, 2, 3).reshape(groups, NV, DK, DV)
        _, outputs = lax.scan(block_apply, entering, parts)
        outputs = jnp.transpose(outputs, (1, 0, 3, 2, 4)).reshape(groups, positions, NV, DV)
        normed_out = rms_rows(outputs, gain_out).reshape(groups, positions, NV * DV)
        outcome = (section_input.astype(jnp.float32) + normed_out).astype(jnp.bfloat16)
        results.append(outcome)
        if step_index < micro_count:
            passed = from_behind(outcome, "section", 1)
    first_done = results[1]
    second_done = results[2]
    returned_rows = from_behind(first_done, "section", -1)
    return jnp.where(head_section, returned_rows, second_done)


def solution(mesh):
    return jax.shard_map(
        local,
        mesh=mesh,
        in_specs=(
            P("dp", "ctx", None),
            P("section", "ctx", None),
            P("section", "ctx", None),
            P("section", None),
            P("section", None, None),
            P("section", None),
            P("section", None),
            P("section", None),
        ),
        out_specs=P(("dp", "section"), "ctx", None),
        check_vma=False,
    )
```

profile of v0, /device:TPU:8, one launch (start us, length us, event | category | flops | bytes accessed | tf_op | source)
XLA Modules:
  0.0 1257.0 jit_solution(16439576218833996155)
XLA Ops:
  8.1 53.9 %all-gather = bf16[1,2048,32]{2,0,1:T(2,128)(2,1)S(1)} all-gather(bf16[1,64,32]{2,0,1:T(2,128)(2,1)S(1)} %copy.127), channel_id=2, replica_groups=mesh['section'=2,'dp'=4,'ctx'=32] {'ctx'}, dimensions={1}, use_global_device_ids=true | all-gather | bytes 135168 | tf_op jit(solution)/shard_map/all_gather | solution.py:116
  64.7 89.2 %all-gather.4.cloned.1.call-done = bf16[1,2048,4096]{2,1,0:T(8,128)(2,1)} async-done(((bf16[1,64,4096]{2,1,0:T(8,128)(2,1)}), bf16[1,2048,4096]{2,1,0:T(8,128)(2,1)}) %all-gather.4.cloned.1.call-update) | async-done | bytes 16777232 | tf_op jit(solution)/shard_map/all_gather | solution.py:115
  153.9 8.2 fusion.21
  169.6 3.5 fusion.62
  173.1 158.1 %custom-call.5 = f32[1,16,1,128,128]{3,4,2,1,0:T(8,128)S(1)} custom-call(f32[1,16,1,128,128]{4,3,2,1,0:T(8,128)} %fusion.62), custom_call_target="InvertDiagBlocksLowerTriangular" | custom-call | tf_op jit(solution)/shard_map/triangular_solve/custom-call.1 | solution.py:78
  341.8 9.5 all-to-all-start.1
  353.3 24.8 %all-to-all-done.1 = f32[1,1,32,128,64]{3,4,1,0,2:T(8,128)} async-done(((f32[1,1,32,128,64]{3,4,1,0,2:T(8,128)}), f32[1,1,32,128,64]{3,4,1,0,2:T(8,128)}, u32[]{:S(2)}, u32[]{:S(2)}) %all-to-all-start.1) | async-done | bytes 1048608 | tf_op jit(solution)/shard_map/all_to_all | solution.py:186
  380.9 5.2 all-to-all-start
  386.0 48.2 %all-to-all-done = f32[1,1,32,128,128]{4,3,1,0,2:T(8,128)} async-done(((f32[1,1,32,128,128]{4,3,1,0,2:T(8,128)}), f32[1,1,32,128,128]{4,3,1,0,2:T(8,128)}, u32[]{:S(2)}, u32[]{:S(2)}) %all-to-all-start) | async-done | bytes 2097184 | tf_op jit(solution)/shard_map/all_to_all | solution.py:185
  434.3 36.5 %while.6 = (s32[]{:T(128)}, f32[1,1,128,64]{2,3,1,0:T(8,128)S(1)}, f32[32,1,1,128,64]{3,4,2,1,0:T(8,128)S(1)}, f32[32,1,1,128,128]{4,3,2,1,0:T(8,128)}, f32[32,1,1,128,64]{3,4,2,1,0:T(8,128)}, /*index=5*/s32[]{:T(128)}) while((s32[]{:T(128)}, f32[1,1,128,64]{2,3,1,0:T(8,128)S(1)}, f32[32,1,1,128,64]{3,4,2,1,0:T(8,128)S(1)}, ...), condition=%wide.region_5.7_spmd, body=%wide.region_4.6_spmd.sunk | while | flops 12591106 | bytes 296009 | solution.py:191
  471.8 5.8 all-to-all-start.2
  484.2 19.7 %all-to-all-done.2 = f32[32,1,1,128,64]{3,4,2,1,0:T(8,128)S(1)} async-done(((f32[32,1,1,128,64]{3,4,2,1,0:T(8,128)}), f32[32,1,1,128,64]{3,4,2,1,0:T(8,128)S(1)}, u32[]{:S(2)}, u32[]{:S(2)}) %all-to-all-start.2) | async-done | bytes 1048608 | tf_op jit(solution)/shard_map/all_to_all | solution.py:194
  517.3 8.2 fusion.24
  525.6 3.7 collective-permute-start.2
  535.6 3.5 fusion.59
  539.1 158.0 %custom-call.6 = f32[1,16,1,128,128]{3,4,2,1,0:T(8,128)S(1)} custom-call(f32[1,16,1,128,128]{4,3,2,1,0:T(8,128)} %fusion.59), custom_call_target="InvertDiagBlocksLowerTriangular" | custom-call | tf_op jit(solution)/shard_map/triangular_solve/custom-call.1 | solution.py:78
  707.5 6.3 all-to-all-start.4
  715.8 26.2 %all-to-all-done.4 = f32[1,1,32,128,64]{3,4,1,0,2:T(8,128)} async-done(((f32[1,1,32,128,64]{3,4,1,0,2:T(8,128)}), f32[1,1,32,128,64]{3,4,1,0,2:T(8,128)}, u32[]{:S(2)}, u32[]{:S(2)}) %all-to-all-start.4) | async-done | bytes 1048608 | tf_op jit(solution)/shard_map/all_to_all | solution.py:186
  744.8 5.0 all-to-all-start.3
  749.8 49.6 %all-to-all-done.3 = f32[1,1,32,128,128]{4,3,1,0,2:T(8,128)} async-done(((f32[1,1,32,128,128]{4,3,1,0,2:T(8,128)}), f32[1,1,32,128,128]{4,3,1,0,2:T(8,128)}, u32[]{:S(2)}, u32[]{:S(2)}) %all-to-all-start.3) | async-done | bytes 2097184 | tf_op jit(solution)/shard_map/all_to_all | solution.py:185
  799.5 36.5 %while.7 = (s32[]{:T(128)}, f32[1,1,128,64]{2,3,1,0:T(8,128)S(1)}, f32[32,1,1,128,64]{3,4,2,1,0:T(8,128)S(1)}, f32[32,1,1,128,128]{4,3,2,1,0:T(8,128)}, f32[32,1,1,128,64]{3,4,2,1,0:T(8,128)}, /*index=5*/s32[]{:T(128)}) while((s32[]{:T(128)}, f32[1,1,128,64]{2,3,1,0:T(8,128)S(1)}, f32[32,1,1,128,64]{3,4,2,1,0:T(8,128)S(1)}, ...), condition=%wide.region_12.14_spmd, body=%wide.region_11.13_spmd.sunk | while | flops 12591106 | bytes 296009 | solution.py:191
  837.0 6.4 all-to-all-start.5
  849.9 21.8 %all-to-all-done.5 = f32[32,1,1,128,64]{3,4,2,1,0:T(8,128)S(1)} async-done(((f32[32,1,1,128,64]{3,4,2,1,0:T(8,128)}), f32[32,1,1,128,64]{3,4,2,1,0:T(8,128)S(1)}, u32[]{:S(2)}, u32[]{:S(2)}) %all-to-all-start.5) | async-done | bytes 1048608 | tf_op jit(solution)/shard_map/all_to_all | solution.py:194
  885.2 8.2 fusion.27
  902.9 3.5 fusion.56
  906.4 157.9 %custom-call.7 = f32[1,16,1,128,128]{3,4,2,1,0:T(8,128)S(1)} custom-call(f32[1,16,1,128,128]{4,3,2,1,0:T(8,128)} %fusion.56), custom_call_target="InvertDiagBlocksLowerTriangular" | custom-call | tf_op jit(solution)/shard_map/triangular_solve/custom-call.1 | solution.py:78
  1074.7 6.6 all-to-all-start.7
  1083.3 26.6 %all-to-all-done.7 = f32[1,1,32,128,64]{3,4,1,0,2:T(8,128)} async-done(((f32[1,1,32,128,64]{3,4,1,0,2:T(8,128)}), f32[1,1,32,128,64]{3,4,1,0,2:T(8,128)}, u32[]{:S(2)}, u32[]{:S(2)}) %all-to-all-start.7) | async-done | bytes 1048608 | tf_op jit(solution)/shard_map/all_to_all | solution.py:186
  1111.3 55.7 %all_to_all.99 = f32[1,1,32,128,128]{4,3,1,0,2:T(8,128)} all-to-all(f32[1,1,32,128,128]{4,3,1,0,2:T(8,128)S(1)} %bitcast.533), channel_id=1, replica_groups=mesh['section'=2,'dp'=4,'ctx'=32] {'ctx'}, dimensions={2} | all-to-all | bytes 4194304 | tf_op jit(solution)/shard_map/all_to_all | solution.py:185
  1167.2 36.5 %while.8 = (s32[]{:T(128)}, f32[1,1,128,64]{2,3,1,0:T(8,128)S(1)}, f32[32,1,1,128,64]{3,4,2,1,0:T(8,128)S(1)}, f32[32,1,1,128,128]{4,3,2,1,0:T(8,128)}, f32[32,1,1,128,64]{3,4,2,1,0:T(8,128)}, /*index=5*/s32[]{:T(128)}) while((s32[]{:T(128)}, f32[1,1,128,64]{2,3,1,0:T(8,128)S(1)}, f32[32,1,1,128,64]{3,4,2,1,0:T(8,128)S(1)}, ...), condition=%wide.region_19.21_spmd, body=%wide.region_18.20_spmd.sunk | while | flops 12591106 | bytes 296009 | solution.py:191
  1204.7 4.9 all-to-all-start.8
  1217.6 20.3 %all-to-all-done.8 = f32[32,1,1,128,64]{3,4,2,1,0:T(8,128)S(1)} async-done(((f32[32,1,1,128,64]{3,4,2,1,0:T(8,128)}), f32[32,1,1,128,64]{3,4,2,1,0:T(8,128)S(1)}, u32[]{:S(2)}, u32[]{:S(2)}) %all-to-all-start.8) | async-done | bytes 1048608 | tf_op jit(solution)/shard_map/all_to_all | solution.py:194
  (548 shorter events, 239.7 us)
Async XLA Ops:
  6.5 471.1 %copy-start = (f32[1,128]{1,0:T(1,128)S(1)}, f32[1,128]{1,0:T(1,128)}, u32[]{:S(2)}) copy-start(f32[1,128]{1,0:T(1,128)} %param.23) | copy-start | bytes 1540
  6.5 56.0 %copy-start.2 = (bf16[2,128,2048]{2,1,0:T(8,128)(2,1)S(1)}, bf16[2,128,2048]{2,1,0:T(8,128)(2,1)}, u32[]{:S(2)}) copy-start(bf16[2,128,2048]{2,1,0:T(8,128)(2,1)} %param.16) | copy-start | bytes 3145732
  6.5 56.2 %copy-start.46 = (f32[1,16]{1,0:T(1,128)S(1)}, f32[1,16]{1,0:T(1,128)}, u32[]{:S(2)}) copy-start(f32[1,16]{1,0:T(1,128)} %param.21) | copy-start | bytes 196
  6.5 56.3 %copy-start.25 = (f32[1,2048]{1,0:T(1,128)S(1)}, f32[1,2048]{1,0:T(1,128)}, u32[]{:S(2)}) copy-start(f32[1,2048]{1,0:T(1,128)} %param.19) | copy-start | bytes 24580
  6.5 147.3 %all-gather.4.cloned.1.call-start = ((), (), s32[]{:S(2)}) async-start(), calls=%async_computation.9 | async-start | bytes 17301504 | tf_op jit(solution)/shard_map/all_gather | solution.py:115
  8.1 55.1 %copy-start.41 = (f32[1,16]{1,0:T(1,128)S(1)}, f32[1,16]{1,0:T(1,128)}, u32[]{:S(2)}) copy-start(f32[1,16]{1,0:T(1,128)} %param.22) | copy-start | bytes 196
  63.3 105.4 %copy-start.31 = (f32[16,128]{1,0:T(8,128)}, f32[16,128]{1,0:T(8,128)S(1)}, u32[]{:S(2)}) copy-start(f32[16,128]{1,0:T(8,128)S(1)} %get-tuple-element.300) | copy-start | bytes 24580
  63.9 104.8 %copy-start.35 = (pred[128,128]{1,0:T(8,128)(4,1)}, pred[128,128]{1,0:T(8,128)(4,1)S(1)}, u32[]{:S(2)}) copy-start(pred[128,128]{1,0:T(8,128)(4,1)S(1)} %get-tuple-element.322) | copy-start | bytes 49156
  64.0 104.7 %copy-start.38 = (pred[128,128]{1,0:T(8,128)(4,1)}, pred[128,128]{1,0:T(8,128)(4,1)S(1)}, u32[]{:S(2)}) copy-start(pred[128,128]{1,0:T(8,128)(4,1)S(1)} %get-tuple-element.320) | copy-start | bytes 49156
  162.2 3.3 collective-permute-start
  173.1 158.4 %copy-start.32 = (f32[16,128]{1,0:T(8,128)S(1)}, f32[16,128]{1,0:T(8,128)}, u32[]{:S(2)}) copy-start(f32[16,128]{1,0:T(8,128)} %copy-done.31) | copy-start | bytes 24580
  341.8 36.3 %all-to-all-start.1 = ((f32[1,1,32,128,64]{3,4,1,0,2:T(8,128)}), f32[1,1,32,128,64]{3,4,1,0,2:T(8,128)}, u32[]{:S(2)}, u32[]{:S(2)}) async-start(f32[1,1,32,128,64]{3,4,1,0,2:T(8,128)} %bitcast.556), calls=%async_computation.1 | async-start | bytes 2097152 | tf_op jit(solution)/shard_map/all_to_all | solution.py:186
  380.9 53.3 %all-to-all-start = ((f32[1,1,32,128,128]{4,3,1,0,2:T(8,128)}), f32[1,1,32,128,128]{4,3,1,0,2:T(8,128)}, u32[]{:S(2)}, u32[]{:S(2)}) async-start(f32[1,1,32,128,128]{4,3,1,0,2:T(8,128)} %bitcast.531), calls=%async_computation | async-start | bytes 4194304 | tf_op jit(solution)/shard_map/all_to_all | solution.py:185
  471.8 32.0 %all-to-all-start.2 = ((f32[32,1,1,128,64]{3,4,2,1,0:T(8,128)}), f32[32,1,1,128,64]{3,4,2,1,0:T(8,128)S(1)}, u32[]{:S(2)}, u32[]{:S(2)}) async-start(f32[32,1,1,128,64]{3,4,2,1,0:T(8,128)} %copy-done.22), calls=%async_computation.2 | async-start | bytes 2097152 | tf_op jit(solution)/shard_map/all_to_all | solution.py:194
  513.8 2.8 collective-permute-start.1
  516.9 8.6 copy-start.7
  517.3 12.0 copy-start.43
  525.6 5.6 collective-permute-start.2
  529.4 5.3 copy-start.33
  539.1 158.2 %copy-start.34 = (f32[16,128]{1,0:T(8,128)S(1)}, f32[16,128]{1,0:T(8,128)}, u32[]{:S(2)}) copy-start(f32[16,128]{1,0:T(8,128)} %copy-done.33) | copy-start | bytes 24580
  707.5 34.5 %all-to-all-start.4 = ((f32[1,1,32,128,64]{3,4,1,0,2:T(8,128)}), f32[1,1,32,128,64]{3,4,1,0,2:T(8,128)}, u32[]{:S(2)}, u32[]{:S(2)}) async-start(f32[1,1,32,128,64]{3,4,1,0,2:T(8,128)} %bitcast.557), calls=%async_computation.4 | async-start | bytes 2097152 | tf_op jit(solution)/shard_map/all_to_all | solution.py:186
  744.8 54.7 %all-to-all-start.3 = ((f32[1,1,32,128,128]{4,3,1,0,2:T(8,128)}), f32[1,1,32,128,128]{4,3,1,0,2:T(8,128)}, u32[]{:S(2)}, u32[]{:S(2)}) async-start(f32[1,1,32,128,128]{4,3,1,0,2:T(8,128)} %bitcast.532), calls=%async_computation.3 | async-start | bytes 4194304 | tf_op jit(solution)/shard_map/all_to_all | solution.py:185
  837.0 34.7 %all-to-all-start.5 = ((f32[32,1,1,128,64]{3,4,2,1,0:T(8,128)}), f32[32,1,1,128,64]{3,4,2,1,0:T(8,128)S(1)}, u32[]{:S(2)}, u32[]{:S(2)}) async-start(f32[32,1,1,128,64]{3,4,2,1,0:T(8,128)} %copy-done.23), calls=%async_computation.5 | async-start | bytes 2097152 | tf_op jit(solution)/shard_map/all_to_all | solution.py:194
  881.4 3.2 copy-start.4
  881.6 11.9 copy-start.26
  881.6 2.9 collective-permute-start.4
  884.8 8.6 copy-start.5
  893.5 5.0 collective-permute-start.5
  1074.7 35.1 %all-to-all-start.7 = ((f32[1,1,32,128,64]{3,4,1,0,2:T(8,128)}), f32[1,1,32,128,64]{3,4,1,0,2:T(8,128)}, u32[]{:S(2)}, u32[]{:S(2)}) async-start(f32[1,1,32,128,64]{3,4,1,0,2:T(8,128)} %bitcast.555), calls=%async_computation.7 | async-start | bytes 2097152 | tf_op jit(solution)/shard_map/all_to_all | solution.py:186
  1204.7 33.2 %all-to-all-start.8 = ((f32[32,1,1,128,64]{3,4,2,1,0:T(8,128)}), f32[32,1,1,128,64]{3,4,2,1,0:T(8,128)S(1)}, u32[]{:S(2)}, u32[]{:S(2)}) async-start(f32[32,1,1,128,64]{3,4,2,1,0:T(8,128)} %copy-done.21), calls=%async_computation.8 | async-start | bytes 2097152 | tf_op jit(solution)/shard_map/all_to_all | solution.py:194
  1209.6 37.7 %collective-permute-start.3 = (bf16[1,128,2048]{2,1,0:T(8,128)(2,1)}, bf16[1,128,2048]{2,1,0:T(8,128)(2,1)}, u32[]{:S(2)}, u32[]{:S(2)}) collective-permute-start(bf16[1,128,2048]{2,1,0:T(8,128)(2,1)} %copy-done.26), channel_id=1, source_target_pairs={{128,0},{129,1},{130,2},{131,3},{132,4},{133,5},{134,6},{135,7},{1... | collective-permute-start | bytes 1572872 | tf_op jit(solution)/shard_map/ppermute | solution.py:20
  1246.0 3.9 copy-start.1
  (30 other events, 50.7 us)
Sparse Core Ops, SparseCore 0:
  9.9 143.9 all-gather.3
where the time goes:
time: 1270 us; the launch traced here: 1260 us
  other arithmetic  494 us (39%)
  waiting for transfers between devices  332 us (26%)
  matrix products  205 us (16%)
  blocking collectives  110 us (9%)
  starting transfers between devices  62.8 us (5%)
  local copies, waits for them, and re-layouts  34.5 us (3%)
  between operations  15.1 us (1%)
    another operation x6, other arithmetic, block_parts(): lax.linalg.triangular_solve(system, right_side, left_side=True, lower=Tru...  474 us
    dot_general x102, matrix products, chain_product(): jnp.einsum('...ij,...jk->...ik', left_map, right_map, precision=PRECISE)  117 us
    all_to_all x2, waiting for transfers between devices, local(): lax.all_to_all(sent_maps, 'ctx', split_axis=2, concat_axis=0, tiled=True)  97.8 us
    all_gather x1, waiting for transfers between devices, local(): lax.all_gather(weight_qkv, 'ctx', axis=0, tiled=True)  89.2 us
    all_to_all x3, waiting for transfers between devices, local(): lax.all_to_all(sent_bias, 'ctx', split_axis=2, concat_axis=0, tiled=True)  77.6 us
    all_to_all x3, waiting for transfers between devices, local(): lax.all_to_all(entering_parts, 'ctx', split_axis=0, concat_axis=2, tiled=...  61.8 us
    all_to_all x1, blocking collectives, local(): lax.all_to_all(sent_maps, 'ctx', split_axis=2, concat_axis=0, tiled=True)  55.7 us
    all_gather x1, blocking collectives, local(): lax.all_gather(weight_gate, 'ctx', axis=0, tiled=True)  53.9 us
  transfers between devices with their start and end apart: 15, of which 13 were waited for; matrix products, arithmetic and copies ran while one was open for 3% of the time, Pallas kernels for 0%

commit v1 on v0

v1 whole, which is shorter than its diff:
```python
import jax
import jax.numpy as jnp
from jax import lax
from jax.sharding import PartitionSpec as P

NK = 8
NV = 16
DK = 128
DV = 128
CONV = 4
BLOCK = 128


PRECISE = lax.Precision.HIGHEST


def from_behind(value, axis, by):
    length = lax.axis_size(axis)
    pairs = [(i, i + by) for i in range(length) if 0 <= i + by < length]
    return lax.ppermute(value, axis, pairs)


def rms_rows(values, gain_row):
    inverse = lax.rsqrt(jnp.mean(values * values, axis=-1, keepdims=True) + 1e-06)
    return values * inverse * gain_row


def unit_rows(values):
    return values * lax.rsqrt(jnp.sum(values * values, axis=-1, keepdims=True) + 1e-06)


def conv_rows(padded, conv_taps):
    tap_count = conv_taps.shape[0]
    length = padded.shape[-2] - tap_count + 1
    running_sum = jnp.zeros(padded.shape[:-2] + (length, padded.shape[-1]), jnp.float32)
    for offset in range(tap_count):
        running_sum = running_sum + conv_taps[offset].astype(jnp.float32) * padded[
            ..., offset : offset + length, :
        ].astype(jnp.float32)
    return jax.nn.silu(running_sum).astype(jnp.bfloat16)


def head_inputs(mixed_rows, gate_raw, decay_rates, biases):
    row_count = mixed_rows.shape[0]
    features = mixed_rows.astype(jnp.float32)
    queries = unit_rows(features[:, : NK * DK].reshape(row_count, NK, DK)) * DK ** (-0.5)
    key_rows = unit_rows(features[:, NK * DK : 2 * NK * DK].reshape(row_count, NK, DK))
    values = features[:, 2 * NK * DK :].reshape(row_count, NV, DV)
    queries = jnp.repeat(queries, NV // NK, axis=1)
    key_rows = jnp.repeat(key_rows, NV // NK, axis=1)
    gate_float = gate_raw.astype(jnp.float32)
    strength = jax.nn.sigmoid(gate_float[:, :NV])
    logdecay = -decay_rates * jax.nn.softplus(gate_float[:, NV:] + biases)
    return (queries, key_rows, values, strength, logdecay)


def unit_lower_inverse(strict_part):
    size = strict_part.shape[-1]
    base = min(16, size)
    count = size // base
    lead = strict_part.shape[:-2]
    tiles = strict_part.reshape(lead + (count, base, count, base))
    diag_tiles = jnp.moveaxis(jnp.diagonal(tiles, axis1=-4, axis2=-2), -1, -3)
    inverse = jnp.broadcast_to(jnp.eye(base, dtype=strict_part.dtype), diag_tiles.shape)
    for row in range(1, base):
        new_row = -jnp.einsum(
            "...j,...jk->...k", diag_tiles[..., row, :], inverse, precision=PRECISE
        )
        new_row = new_row.at[..., row].add(1.0)
        inverse = inverse.at[..., row, :].set(new_row)
    width = base
    while width < size:
        pairs = size // (2 * width)
        tiles = strict_part.reshape(lead + (pairs, 2 * width, pairs, 2 * width))
        below = jnp.moveaxis(jnp.diagonal(tiles, axis1=-4, axis2=-2), -1, -3)[
            ..., width:, :width
        ]
        inverse = inverse.reshape(lead + (pairs, 2, width, width))
        upper = inverse[..., 0, :, :]
        lower = inverse[..., 1, :, :]
        corner = -jnp.einsum(
            "...ij,...jk->...ik",
            lower,
            jnp.einsum("...ij,...jk->...ik", below, upper, precision=PRECISE),
            precision=PRECISE,
        )
        zeros = jnp.zeros_like(upper)
        top = jnp.concatenate([upper, zeros], axis=-1)
        bottom = jnp.concatenate([corner, lower], axis=-1)
        inverse = jnp.concatenate([top, bottom], axis=-2)
        width *= 2
    return inverse.reshape(lead + (size, size))


def block_parts(queries, key_rows, values, strength, logdecay):
    block_len = queries.shape[1]
    cumulative = jnp.swapaxes(jnp.cumsum(logdecay, axis=1), 1, 2)
    beta_heads = jnp.swapaxes(strength, 1, 2)
    query_heads = jnp.swapaxes(queries, 1, 2)
    key_heads = jnp.swapaxes(key_rows, 1, 2)
    value_heads = jnp.swapaxes(values, 1, 2)
    places = jnp.arange(block_len)
    lower_mask = places[:, None] >= places[None, :]
    strict_mask = places[:, None] > places[None, :]
    log_gap = cumulative[..., :, None] - cumulative[..., None, :]
    decay_ratio = jnp.where(lower_mask, jnp.exp(jnp.where(lower_mask, log_gap, 0.0)), 0.0)
    key_inner = jnp.einsum("nhid,nhjd->nhij", key_heads, key_heads, precision=PRECISE)
    strict_part = jnp.where(strict_mask, beta_heads[..., :, None] * key_inner * decay_ratio, 0.0)
    gamma_rows = jnp.exp(cumulative)
    right_side = jnp.concatenate(
        [beta_heads[..., None] * value_heads, (beta_heads * gamma_rows)[..., None] * key_heads],
        axis=-1,
    )
    solved = jnp.einsum(
        "...ij,...jk->...ik", unit_lower_inverse(strict_part), right_side, precision=PRECISE
    )
    fresh_rows = solved[..., : value_heads.shape[-1]]
    mixing = solved[..., value_heads.shape[-1] :]
    scores = jnp.einsum("nhid,nhjd->nhij", query_heads, key_heads, precision=PRECISE) * decay_ratio
    qgamma = gamma_rows[..., None] * query_heads
    key_tail = jnp.exp(cumulative[..., -1:] - cumulative)[..., None] * key_heads
    block_decay = gamma_rows[..., -1]
    return (fresh_rows, mixing, scores, qgamma, key_tail, block_decay)


def block_apply(state_now, block_items):
    fresh_rows, mixing, scores, qgamma, key_tail, block_decay = block_items
    update = fresh_rows - jnp.einsum("...cd,...de->...ce", mixing, state_now, precision=PRECISE)
    output = jnp.einsum("...cd,...de->...ce", qgamma, state_now, precision=PRECISE) + jnp.einsum(
        "...ij,...je->...ie", scores, update, precision=PRECISE
    )
    state_next = block_decay[..., None, None] * state_now + jnp.einsum(
        "...cd,...ce->...de", key_tail, update, precision=PRECISE
    )
    return (state_next, output)


def chain_product(left_map, right_map):
    return jnp.einsum("...ij,...jk->...ik", left_map, right_map, precision=PRECISE)


def local(tokens, w_qkv, w_gate, norm_gain, conv_weight, decay_rate, dt_bias, head_gain):
    section = lax.axis_index("section")
    layer_count = lax.axis_size("section")

    def every_layer(value):
        return lax.all_gather(value[0], "section", axis=0, tiled=False)

    all_qkv = every_layer(w_qkv)
    all_gate = every_layer(w_gate)
    all_gain_in = every_layer(norm_gain)
    all_taps = every_layer(conv_weight)
    all_rates = every_layer(decay_rate)
    all_biases = every_layer(dt_bias)
    all_gain_out = every_layer(head_gain)
    hidden = lax.dynamic_slice_in_dim(tokens, section, 1, axis=0)
    for layer_index in range(layer_count):
        full_qkv = lax.all_gather(all_qkv[layer_index], "ctx", axis=0, tiled=True)
        full_gate = lax.all_gather(all_gate[layer_index], "ctx", axis=0, tiled=True)
        hidden = layer_apply(
            hidden,
            full_qkv,
            full_gate,
            all_gain_in[layer_index],
            all_taps[layer_index],
            all_rates[layer_index],
            all_biases[layer_index],
            all_gain_out[layer_index],
        )
    return hidden


def layer_apply(section_input, full_qkv, full_gate, gain_in, conv_taps, decay_rates, biases, gain_out):
    groups, positions, model_width = section_input.shape
    blocks = positions // BLOCK
    layer_normed = (
        rms_rows(section_input.astype(jnp.float32), gain_in)
        .astype(jnp.bfloat16)
        .reshape(groups * positions, model_width)
    )
    proj_qkv = jnp.dot(layer_normed, full_qkv, preferred_element_type=jnp.float32)
    proj_gate = jnp.dot(layer_normed, full_gate, preferred_element_type=jnp.float32)
    features = proj_qkv.astype(jnp.bfloat16).reshape(groups, positions, proj_qkv.shape[1])
    gate_raw = proj_gate.astype(jnp.bfloat16)
    previous_rows = from_behind(features[:, positions - (CONV - 1) :], "ctx", 1)
    mixed_rows = conv_rows(jnp.concatenate([previous_rows, features], axis=1), conv_taps)
    queries, key_rows, values, strength, logdecay = head_inputs(
        mixed_rows.reshape(groups * positions, mixed_rows.shape[2]),
        gate_raw,
        decay_rates,
        biases,
    )
    count_blocks = groups * blocks
    parts = block_parts(
        queries.reshape(count_blocks, BLOCK, NV, DK),
        key_rows.reshape(count_blocks, BLOCK, NV, DK),
        values.reshape(count_blocks, BLOCK, NV, DV),
        strength.reshape(count_blocks, BLOCK, NV),
        logdecay.reshape(count_blocks, BLOCK, NV),
    )
    parts = tuple(
        (
            jnp.moveaxis(source.reshape((groups, blocks) + source.shape[1:]), 1, 0)
            for source in parts
        )
    )
    fresh_rows, mixing, scores, qgamma, key_tail, block_decay = parts
    identity = jnp.broadcast_to(jnp.eye(DK, dtype=jnp.float32), (groups, NV, DK, DK))
    no_state = jnp.zeros((groups, NV, DK, DV), jnp.float32)
    step_maps = block_decay[..., None, None] * identity - jnp.einsum(
        "...cd,...cf->...df", key_tail, mixing, precision=PRECISE
    )
    step_biases = jnp.einsum("...cd,...ce->...de", key_tail, fresh_rows, precision=PRECISE)

    def compose(running, block_items):
        map_now, bias_now = running
        step_map, step_bias = block_items
        return (
            (chain_product(step_map, map_now), chain_product(step_map, bias_now) + step_bias),
            None,
        )

    (local_map, local_bias), _ = lax.scan(
        compose, (identity, no_state), (step_maps, step_biases)
    )
    ctx_count = lax.axis_size("ctx")
    column_parts = max(1, ctx_count // NV)
    item_count = NV * column_parts
    part_width = DV // column_parts
    sent_maps = jnp.repeat(local_map, column_parts, axis=1)[None]
    sent_bias = jnp.moveaxis(local_bias.reshape(groups, NV, DK, column_parts, part_width), 3, 2)
    sent_bias = sent_bias.reshape(groups, item_count, DK, part_width)[None]
    got_maps = lax.all_to_all(sent_maps, "ctx", split_axis=2, concat_axis=0, tiled=True)
    got_bias = lax.all_to_all(sent_bias, "ctx", split_axis=2, concat_axis=0, tiled=True)

    def chain_step(state_now, incoming):
        return (chain_product(incoming[0], state_now) + incoming[1], state_now)

    _, entering_parts = lax.scan(
        chain_step, jnp.zeros(got_bias.shape[1:], jnp.float32), (got_maps, got_bias)
    )
    returned_states = lax.all_to_all(
        entering_parts, "ctx", split_axis=0, concat_axis=2, tiled=True
    )
    entering = returned_states[0].reshape(groups, NV, column_parts, DK, part_width)
    entering = jnp.moveaxis(entering, 2, 3).reshape(groups, NV, DK, DV)
    _, outputs = lax.scan(block_apply, entering, parts)
    outputs = jnp.transpose(outputs, (1, 0, 3, 2, 4)).reshape(groups, positions, NV, DV)
    normed_out = rms_rows(outputs, gain_out).reshape(groups, positions, NV * DV)
    outcome = (section_input.astype(jnp.float32) + normed_out).astype(jnp.bfloat16)
    return outcome


def solution(mesh):
    return jax.shard_map(
        local,
        mesh=mesh,
        in_specs=(
            P("dp", "ctx", None),
            P("section", "ctx", None),
            P("section", "ctx", None),
            P("section", None),
            P("section", None, None),
            P("section", None),
            P("section", None),
            P("section", None),
        ),
        out_specs=P(("dp", "section"), "ctx", None),
        check_vma=False,
    )
```

time: 1270 us -> 874 us (0.69)
  other arithmetic: 494 us -> 47.4 us
  local copies, waits for them, and re-layouts: 34.5 us -> 176 us
  waiting for transfers between devices: 332 us -> 219 us
  blocking collectives: 110 us -> 189 us
  matrix products: 205 us -> 175 us
  starting transfers between devices: 62.8 us -> 41.2 us
    another operation x6 -> x0, other arithmetic: 474 us -> none  [block_parts(): lax.linalg.triangular_solve(system, right_side, left_side=True, lower=Tru...]
    all_to_all x8 -> x5, waiting for transfers between devices: 237 us -> 121 us  [the longest x2 51 us: layer_apply(): lax.all_to_all(sent_bias, 'ctx', split_axis=2, concat_axis=0, tiled=True)]
    all_gather x1 -> x8, blocking collectives: 53.9 us -> 134 us  [the longest x2 123 us: local(): full_gate = lax.all_gather(all_gate[layer_index], 'ctx', axis=0, tiled=True)]
    reshape x6 -> x16, local copies, waits for them, and re-layouts: 4.82 us -> 51.6 us  [the longest x4 26.8 us: unit_lower_inverse(): tiles = strict_part.reshape(lead + (count, base, count, base))]
    scatter x0 -> x30, local copies, waits for them, and re-layouts: none -> 43.4 us  [unit_lower_inverse(): inverse = inverse.at[..., row, :].set(new_row)]
    dot_general x102 -> x68, matrix products: 117 us -> 78.1 us  [chain_product(): jnp.einsum('...ij,...jk->...ik', left_map, right_map, precision=PRECISE)]
    dot_general x12 -> x52, matrix products: 40.4 us -> 70.3 us  [the longest x30 30.1 us: unit_lower_inverse(): jnp.einsum('...j,...jk->...k', diag_tiles[..., row, :], inverse, precisio...]
    scatter-add x0 -> x30, local copies, waits for them, and re-layouts: none -> 24.6 us  [unit_lower_inverse(): new_row = new_row.at[..., row].add(1.0)]
  transfers between devices with their start and end apart: 15 -> 10, of which waited for: 13 -> 8; matrix products, arithmetic and copies ran while one was open for 3% -> 23% of each run, Pallas kernels for 0% -> 0%
where the time goes in v1:
time: 874 us; the launch traced here: 865 us
  waiting for transfers between devices  219 us (25%)
  blocking collectives  189 us (22%)
  local copies, waits for them, and re-layouts  176 us (20%)
  matrix products  175 us (20%)
  other arithmetic  47.4 us (5%)
  starting transfers between devices  41.2 us (5%)
  between operations  15.5 us (2%)
    all_gather x2, blocking collectives, local(): full_gate = lax.all_gather(all_gate[layer_index], 'ctx', axis=0, tiled=True)  123 us
    dot_general x68, matrix products, chain_product(): jnp.einsum('...ij,...jk->...ik', left_map, right_map, precision=PRECISE)  78.1 us
    all_gather x2, waiting for transfers between devices, local(): full_qkv = lax.all_gather(all_qkv[layer_index], 'ctx', axis=0, tiled=True)  76.3 us
    all_to_all x1, blocking collectives, layer_apply(): lax.all_to_all(sent_maps, 'ctx', split_axis=2, concat_axis=0, tiled=True)  55.4 us
    all_to_all x2, waiting for transfers between devices, layer_apply(): lax.all_to_all(sent_bias, 'ctx', split_axis=2, concat_axis=0, tiled=True)  51 us
    all_to_all x1, waiting for transfers between devices, layer_apply(): lax.all_to_all(sent_maps, 'ctx', split_axis=2, concat_axis=0, tiled=True)  48.5 us
    scatter x30, local copies, waits for them, and re-layouts, unit_lower_inverse(): inverse = inverse.at[..., row, :].set(new_row)  43.4 us
    dot_general x30, matrix products, unit_lower_inverse(): jnp.einsum('...j,...jk->...k', diag_tiles[..., row, :], inverse, precisio...  30.1 us
  transfers between devices with their start and end apart: 10, of which 8 were waited for; matrix products, arithmetic and copies ran while one was open for 23% of the time, Pallas kernels for 0%

profile of v1, /device:TPU:8, one launch (start us, length us, event | category | flops | bytes accessed | tf_op | source)
XLA Modules:
  0.0 865.0 jit_solution(9686055204022526432)
XLA Ops:
  7.3 19.1 %all-gather.12.cloned.1.call-done = bf16[2,64,4096]{2,1,0:T(8,128)(2,1)} async-done(((bf16[1,64,4096]{2,1,0:T(8,128)(2,1)}), bf16[2,64,4096]{2,1,0:T(8,128)(2,1)}) %all-gather.12.cloned.1.call-update) | async-done | bytes 1048592 | tf_op jit(solution)/shard_map/all_gather | solution.py:147
  34.3 52.3 %all-gather = bf16[1,2048,32]{2,0,1:T(2,128)(2,1)S(1)} all-gather(bf16[1,64,32]{2,0,1:T(2,128)(2,1)S(1)} %copy.181), channel_id=2, replica_groups=mesh['section'=2,'dp'=4,'ctx'=32] {'ctx'}, dimensions={1}, use_global_device_ids=true | all-gather | bytes 135168 | tf_op jit(solution)/shard_map/all_gather | solution.py:159
  94.7 76.3 %all-gather.14.cloned.1.call-done = bf16[1,2048,4096]{2,1,0:T(8,128)(2,1)} async-done(((bf16[1,64,4096]{2,1,0:T(8,128)(2,1)}), bf16[1,2048,4096]{2,1,0:T(8,128)(2,1)}) %all-gather.14.cloned.1.call-update) | async-done | bytes 16777232 | tf_op jit(solution)/shard_map/all_gather | solution.py:158
  171.0 8.2 fusion.14
  189.3 4.7 reshape.3666
  193.9 3.2 reshape.3713
  199.6 8.8 %copy.422 = f32[1,16,8,16,8,16]{5,3,4,2,1,0:T(8,128)} copy(f32[1,16,8,16,8,16]{5,4,3,2,1,0:T(8,128)} %reshape.3666) | data formatting | bytes 2097152 | tf_op jit(solution)/shard_map/reshape | solution.py:62
  208.4 4.1 gather_fusion
  276.9 4.9 copy.424
  307.0 3.3 convolution_add_fusion.5
  310.2 9.2 %all-to-all-start.1 = ((f32[1,1,32,128,64]{3,4,1,0,2:T(8,128)}), f32[1,1,32,128,64]{3,4,1,0,2:T(8,128)}, u32[]{:S(2)}, u32[]{:S(2)}) async-start(f32[1,1,32,128,64]{3,4,1,0,2:T(8,128)} %bitcast.1069), calls=%async_computation.1 | async-start | bytes 2097152 | tf_op jit(solution)/shard_map/all_to_all | solution.py:234
  321.4 25.0 %all-to-all-done.1 = f32[1,1,32,128,64]{3,4,1,0,2:T(8,128)} async-done(((f32[1,1,32,128,64]{3,4,1,0,2:T(8,128)}), f32[1,1,32,128,64]{3,4,1,0,2:T(8,128)}, u32[]{:S(2)}, u32[]{:S(2)}) %all-to-all-start.1) | async-done | bytes 1048608 | tf_op jit(solution)/shard_map/all_to_all | solution.py:234
  349.2 5.3 all-to-all-start
  354.5 48.5 %all-to-all-done = f32[1,1,32,128,128]{4,3,1,0,2:T(8,128)} async-done(((f32[1,1,32,128,128]{4,3,1,0,2:T(8,128)}), f32[1,1,32,128,128]{4,3,1,0,2:T(8,128)}, u32[]{:S(2)}, u32[]{:S(2)}) %all-to-all-start) | async-done | bytes 2097184 | tf_op jit(solution)/shard_map/all_to_all | solution.py:233
  403.1 36.5 %while.104 = (s32[]{:T(128)}, f32[1,1,128,64]{2,3,1,0:T(8,128)S(1)}, f32[32,1,1,128,64]{3,4,2,1,0:T(8,128)S(1)}, f32[32,1,1,128,128]{4,3,2,1,0:T(8,128)}, f32[32,1,1,128,64]{3,4,2,1,0:T(8,128)}, /*index=5*/s32[]{:T(128)}) while((s32[]{:T(128)}, f32[1,1,128,64]{2,3,1,0:T(8,128)S(1)}, f32[32,1,1,128,64]{3,4,2,1,0:T(8,128)S(1)}, ...), condition=%wide.region_5.6_spmd, body=%wide.region_4.5_spmd.sunk | while | flops 12591106 | bytes 296009 | solution.py:239
  440.6 5.7 all-to-all-start.2
  446.4 70.4 %all-gather.2 = bf16[1,2048,32]{2,0,1:T(2,128)(2,1)} all-gather(bf16[1,64,32]{2,0,1:T(2,128)(2,1)S(1)} %copy.222), channel_id=4, replica_groups=mesh['section'=2,'dp'=4,'ctx'=32] {'ctx'}, dimensions={1}, use_global_device_ids=true | all-gather | bytes 135168 | tf_op jit(solution)/shard_map/all_gather | solution.py:159
  524.6 3.3 convolution_multiply_fusion.2
  539.1 8.4 fusion.17
  547.5 4.2 collective-permute-start.1
  559.8 4.6 reshape.3742
  564.4 3.2 reshape.3789
  570.2 8.7 %copy.421 = f32[1,16,8,16,8,16]{5,3,4,2,1,0:T(8,128)} copy(f32[1,16,8,16,8,16]{5,4,3,2,1,0:T(8,128)} %reshape.3742) | data formatting | bytes 2097152 | tf_op jit(solution)/shard_map/reshape | solution.py:62
  578.9 4.0 gather_fusion.3
  652.9 4.7 copy.423
  681.9 10.0 %all-to-all-start.4 = ((f32[1,1,32,128,64]{3,4,1,0,2:T(8,128)}), f32[1,1,32,128,64]{3,4,1,0,2:T(8,128)}, u32[]{:S(2)}, u32[]{:S(2)}) async-start(f32[1,1,32,128,64]{3,4,1,0,2:T(8,128)} %bitcast.1068), calls=%async_computation.4 | async-start | bytes 2097152 | tf_op jit(solution)/shard_map/all_to_all | solution.py:234
  693.9 26.0 %all-to-all-done.4 = f32[1,1,32,128,64]{3,4,1,0,2:T(8,128)} async-done(((f32[1,1,32,128,64]{3,4,1,0,2:T(8,128)}), f32[1,1,32,128,64]{3,4,1,0,2:T(8,128)}, u32[]{:S(2)}, u32[]{:S(2)}) %all-to-all-start.4) | async-done | bytes 1048608 | tf_op jit(solution)/shard_map/all_to_all | solution.py:234
  721.4 55.4 %all_to_all.66 = f32[1,1,32,128,128]{4,3,1,0,2:T(8,128)} all-to-all(f32[1,1,32,128,128]{4,3,1,0,2:T(8,128)S(1)} %bitcast.1057), channel_id=1, replica_groups=mesh['section'=2,'dp'=4,'ctx'=32] {'ctx'}, dimensions={2} | all-to-all | bytes 4194304 | tf_op jit(solution)/shard_map/all_to_all | solution.py:233
  776.9 36.5 %while.105 = (s32[]{:T(128)}, f32[1,1,128,64]{2,3,1,0:T(8,128)S(1)}, f32[32,1,1,128,64]{3,4,2,1,0:T(8,128)S(1)}, f32[32,1,1,128,128]{4,3,2,1,0:T(8,128)}, f32[32,1,1,128,64]{3,4,2,1,0:T(8,128)}, /*index=5*/s32[]{:T(128)}) while((s32[]{:T(128)}, f32[1,1,128,64]{2,3,1,0:T(8,128)S(1)}, f32[32,1,1,128,64]{3,4,2,1,0:T(8,128)S(1)}, ...), condition=%wide.region_12.13_spmd, body=%wide.region_11.12_spmd.sunk | while | flops 12591106 | bytes 296009 | solution.py:239
  814.4 4.9 all-to-all-start.5
  822.4 3.3 convolution_multiply_fusion
  825.8 21.8 %all-to-all-done.5 = f32[32,1,1,128,64]{3,4,2,1,0:T(8,128)S(1)} async-done(((f32[32,1,1,128,64]{3,4,2,1,0:T(8,128)}), f32[32,1,1,128,64]{3,4,2,1,0:T(8,128)S(1)}, u32[]{:S(2)}, u32[]{:S(2)}) %all-to-all-start.5) | async-done | bytes 1048608 | tf_op jit(solution)/shard_map/all_to_all | solution.py:242
  (633 shorter events, 335.8 us)
Async XLA Ops:
  6.5 22.2 %copy-start.44 = (f32[1,16]{1,0:T(1,128)S(1)}, f32[1,16]{1,0:T(1,128)}, u32[]{:S(2)}) copy-start(f32[1,16]{1,0:T(1,128)} %param.137) | copy-start | bytes 196
  6.5 24.0 %copy-start.45 = (f32[1,16]{1,0:T(1,128)S(1)}, f32[1,16]{1,0:T(1,128)}, u32[]{:S(2)}) copy-start(f32[1,16]{1,0:T(1,128)} %param.138) | copy-start | bytes 196
  6.5 25.8 %copy-start.40 = (bf16[1,64,32]{1,2,0:T(8,128)(2,1)S(1)}, bf16[1,64,32]{1,2,0:T(8,128)(2,1)}, u32[]{:S(2)}) copy-start(bf16[1,64,32]{1,2,0:T(8,128)(2,1)} %param.134) | copy-start | bytes 12292
  6.5 19.9 %all-gather.12.cloned.1.call-start = ((), (), s32[]{:S(2)}) async-start(), calls=%async_computation.6 | async-start | bytes 1572864 | tf_op jit(solution)/shard_map/all_gather | solution.py:147
  7.3 79.9 %copy-start.41 = (f32[1,2048]{1,0:T(1,128)S(1)}, f32[1,2048]{1,0:T(1,128)}, u32[]{:S(2)}) copy-start(f32[1,2048]{1,0:T(1,128)} %param.135) | copy-start | bytes 24580
  7.3 81.7 %copy-start.30 = (bf16[2,128,2048]{2,1,0:T(8,128)(2,1)S(1)}, bf16[2,128,2048]{2,1,0:T(8,128)(2,1)}, u32[]{:S(2)}) copy-start(bf16[2,128,2048]{2,1,0:T(8,128)(2,1)} %param.132) | copy-start | bytes 3145732
  7.3 163.7 %all-gather.14.cloned.1.call-start = ((), (), s32[]{:S(2)}) async-start(), calls=%async_computation.7 | async-start | bytes 17301504 | tf_op jit(solution)/shard_map/all_gather | solution.py:158
  28.7 510.4 %all-gather.16.cloned.1.call-start = ((), (), s32[]{:S(2)}) async-start(), calls=%async_computation.8 | async-start | bytes 17301504 | tf_op jit(solution)/shard_map/all_gather | solution.py:158
  34.3 56.8 %copy-start.37 = (bf16[1,4,4096]{2,1,0:T(4,128)(2,1)S(1)}, bf16[1,4,4096]{2,1,0:T(4,128)(2,1)}, u32[]{:S(2)}) copy-start(bf16[1,4,4096]{2,1,0:T(4,128)(2,1)} %param.136) | copy-start | bytes 98308
  179.2 3.3 collective-permute-start
  181.1 106.0 %copy-start.38 = (s32[2]{0:T(128)}, s32[2]{0:T(128)S(1)}, u32[]{:S(2)}) copy-start(s32[2]{0:T(128)S(1)} %or_bitcast_fusion) | copy-start | bytes 28
  189.2 7.8 copy-start.4
  275.7 6.1 copy-start
  289.8 2.8 copy-start.21
  310.2 36.2 %all-to-all-start.1 = ((f32[1,1,32,128,64]{3,4,1,0,2:T(8,128)}), f32[1,1,32,128,64]{3,4,1,0,2:T(8,128)}, u32[]{:S(2)}, u32[]{:S(2)}) async-start(f32[1,1,32,128,64]{3,4,1,0,2:T(8,128)} %bitcast.1069), calls=%async_computation.1 | async-start | bytes 2097152 | tf_op jit(solution)/shard_map/all_to_all | solution.py:234
  349.2 53.8 %all-to-all-start = ((f32[1,1,32,128,128]{4,3,1,0,2:T(8,128)}), f32[1,1,32,128,128]{4,3,1,0,2:T(8,128)}, u32[]{:S(2)}, u32[]{:S(2)}) async-start(f32[1,1,32,128,128]{4,3,1,0,2:T(8,128)} %bitcast.1056), calls=%async_computation | async-start | bytes 4194304 | tf_op jit(solution)/shard_map/all_to_all | solution.py:233
  440.6 78.5 %copy-start.46 = (f32[1,128]{1,0:T(1,128)S(1)}, f32[1,128]{1,0:T(1,128)}, u32[]{:S(2)}) copy-start(f32[1,128]{1,0:T(1,128)} %param.139) | copy-start | bytes 1540
  440.6 87.4 %all-to-all-start.2 = ((f32[32,1,1,128,64]{3,4,2,1,0:T(8,128)}), f32[32,1,1,128,64]{3,4,2,1,0:T(8,128)S(1)}, u32[]{:S(2)}, u32[]{:S(2)}) async-start(f32[32,1,1,128,64]{3,4,2,1,0:T(8,128)} %copy-done.27), calls=%async_computation.2 | async-start | bytes 2097152 | tf_op jit(solution)/shard_map/all_to_all | solution.py:242
  519.1 4.1 copy-start.35
  528.0 2.3 copy-start.23
  530.3 2.3 copy-start.25
  539.0 12.7 %copy-start.16 = (bf16[1,128,2048]{2,1,0:T(8,128)(2,1)}, bf16[1,128,2048]{2,1,0:T(8,128)(2,1)S(1)}, u32[]{:S(2)}) copy-start(bf16[1,128,2048]{2,1,0:T(8,128)(2,1)S(1)} %get-tuple-element.906) | copy-start | bytes 1572868
  539.1 13.0 %copy-start.42 = (f32[16]{0:T(128)S(1)}, f32[16]{0:T(128)}, u32[]{:S(2)}) copy-start(f32[16]{0:T(128)} %get-tuple-element.1045) | copy-start | bytes 196
  539.1 13.0 %copy-start.43 = (f32[16]{0:T(128)S(1)}, f32[16]{0:T(128)}, u32[]{:S(2)}) copy-start(f32[16]{0:T(128)} %get-tuple-element.1047) | copy-start | bytes 196
  539.1 14.0 %copy-start.34 = (f32[1,1,4096]{2,1,0:T(1,128)S(1)}, f32[1,1,4096]{2,1,0:T(1,128)}, u32[]{:S(2)}) copy-start(f32[1,1,4096]{2,1,0:T(1,128)} %get-tuple-element.992) | copy-start | bytes 49156
  547.5 5.6 collective-permute-start.1
  559.8 7.9 copy-start.2
  661.6 2.1 copy-start.14
  681.9 38.0 %all-to-all-start.4 = ((f32[1,1,32,128,64]{3,4,1,0,2:T(8,128)}), f32[1,1,32,128,64]{3,4,1,0,2:T(8,128)}, u32[]{:S(2)}, u32[]{:S(2)}) async-start(f32[1,1,32,128,64]{3,4,1,0,2:T(8,128)} %bitcast.1068), calls=%async_computation.4 | async-start | bytes 2097152 | tf_op jit(solution)/shard_map/all_to_all | solution.py:234
  814.4 33.1 %all-to-all-start.5 = ((f32[32,1,1,128,64]{3,4,2,1,0:T(8,128)}), f32[32,1,1,128,64]{3,4,2,1,0:T(8,128)S(1)}, u32[]{:S(2)}, u32[]{:S(2)}) async-start(f32[32,1,1,128,64]{3,4,2,1,0:T(8,128)} %copy-done.26), calls=%async_computation.5 | async-start | bytes 2097152 | tf_op jit(solution)/shard_map/all_to_all | solution.py:242
  847.5 2.3 copy-start.22
  849.8 2.3 copy-start.24
  (25 other events, 32.5 us)
Sparse Core Ops, SparseCore 0:
  9.1 17.2 all-gather.11
  29.0 141.9 all-gather.13
  181.3 138.2 all-gather.15

commit v2 on v1

--- a/solution.py
+++ b/solution.py
@@ -56,18 +56,19 @@
 
 def unit_lower_inverse(strict_part):
     size = strict_part.shape[-1]
-    base = min(16, size)
+    base = min(8, size)
     count = size // base
     lead = strict_part.shape[:-2]
     tiles = strict_part.reshape(lead + (count, base, count, base))
     diag_tiles = jnp.moveaxis(jnp.diagonal(tiles, axis1=-4, axis2=-2), -1, -3)
-    inverse = jnp.broadcast_to(jnp.eye(base, dtype=strict_part.dtype), diag_tiles.shape)
-    for row in range(1, base):
-        new_row = -jnp.einsum(
-            "...j,...jk->...k", diag_tiles[..., row, :], inverse, precision=PRECISE
-        )
-        new_row = new_row.at[..., row].add(1.0)
-        inverse = inverse.at[..., row, :].set(new_row)
+    identity = jnp.eye(base, dtype=strict_part.dtype)
+    inverse = identity - diag_tiles
+    power = diag_tiles
+    reach = 2
+    while reach < base:
+        power = jnp.einsum("...ij,...jk->...ik", power, power, precision=PRECISE)
+        inverse = inverse + jnp.einsum("...ij,...jk->...ik", inverse, power, precision=PRECISE)
+        reach *= 2
     width = base
     while width < size:
         pairs = size // (2 * width)
@@ -144,7 +145,18 @@
     layer_count = lax.axis_size("section")
 
     def every_layer(value):
-        return lax.all_gather(value[0], "section", axis=0, tiled=False)
+        held = [value]
+        for offset in range(1, layer_count):
+            pairs = [(i, (i + offset) % layer_count) for i in range(layer_count)]
+            held.append(lax.ppermute(value, "section", pairs))
+        layers = []
+        for layer_index in range(layer_count):
+            owner_offset = (section - layer_index) % layer_count
+            chosen = held[0]
+            for offset in range(1, layer_count):
+                chosen = jnp.where(owner_offset == offset, held[offset], chosen)
+            layers.append(chosen[0])
+        return layers
 
     all_qkv = every_layer(w_qkv)
     all_gate = every_layer(w_gate)

time: 874 us -> 760 us (0.87)
  local copies, waits for them, and re-layouts: 176 us -> 134 us
  other arithmetic: 47.4 us -> 16.4 us
  blocking collectives: 189 us -> 165 us
  waiting for transfers between devices: 219 us -> 205 us
  matrix products: 175 us -> 165 us
    scatter x30 -> x0, local copies, waits for them, and re-layouts: 43.4 us -> none  [unit_lower_inverse(): inverse = inverse.at[..., row, :].set(new_row)]
    reshape x8 -> x12, local copies, waits for them, and re-layouts: 21.6 us -> 46.7 us  [unit_lower_inverse(): tiles = strict_part.reshape(lead + (pairs, 2 * width, pairs, 2 * width))]
    scatter-add x30 -> x0, local copies, waits for them, and re-layouts: 24.6 us -> none  [unit_lower_inverse(): new_row = new_row.at[..., row].add(1.0)]
    all_gather x1 -> x0, waiting for transfers between devices: 19.1 us -> none  [every_layer(): return lax.all_gather(value[0], 'section', axis=0, tiled=False)]
    neg x30 -> x0, other arithmetic: 16.7 us -> none  [unit_lower_inverse(): -jnp.einsum('...j,...jk->...k', diag_tiles[..., row, :], inverse, precisi...]
    scatter-add x30 -> x0, other arithmetic: 15.4 us -> none  [unit_lower_inverse(): new_row = new_row.at[..., row].add(1.0)]
    all_to_all x1, blocking collectives: 55.4 us -> 40.9 us  [layer_apply(): lax.all_to_all(sent_maps, 'ctx', split_axis=2, concat_axis=0, tiled=True)]
    dot_general x30 -> x8, matrix products: 30.1 us -> 15.8 us  [the longest x4 8.47 us: unit_lower_inverse(): jnp.einsum('...ij,...jk->...ik', inverse, power, precision=PRECISE)]
  transfers between devices with their start and end apart: 10 -> 16, of which waited for: 8 -> 11; matrix products, arithmetic and copies ran while one was open for 23% -> 22% of each run, Pallas kernels for 0% -> 0%
where the time goes in v2:
time: 760 us; the launch traced here: 749 us
  waiting for transfers between devices  205 us (27%)
  blocking collectives  165 us (22%)
  matrix products  165 us (22%)
  local copies, waits for them, and re-layouts  134 us (18%)
  starting transfers between devices  46.9 us (6%)
  other arithmetic  16.4 us (2%)
  between operations  15.1 us (2%)
    all_gather x2, blocking collectives, local(): full_gate = lax.all_gather(all_gate[layer_index], 'ctx', axis=0, tiled=True)  124 us
    all_gather x2, waiting for transfers between devices, local(): full_qkv = lax.all_gather(all_qkv[layer_index], 'ctx', axis=0, tiled=True)  85.5 us
    dot_general x68, matrix products, chain_product(): jnp.einsum('...ij,...jk->...ik', left_map, right_map, precision=PRECISE)  78.2 us
    all_to_all x2, waiting for transfers between devices, layer_apply(): lax.all_to_all(sent_bias, 'ctx', split_axis=2, concat_axis=0, tiled=True)  54.2 us
    all_to_all x1, waiting for transfers between devices, layer_apply(): lax.all_to_all(sent_maps, 'ctx', split_axis=2, concat_axis=0, tiled=True)  48 us
    reshape x12, local copies, waits for them, and re-layouts, unit_lower_inverse(): tiles = strict_part.reshape(lead + (pairs, 2 * width, pairs, 2 * width))  46.7 us
    all_to_all x1, blocking collectives, layer_apply(): lax.all_to_all(sent_maps, 'ctx', split_axis=2, concat_axis=0, tiled=True)  40.9 us
    all_to_all x2, starting transfers between devices, layer_apply(): lax.all_to_all(sent_bias, 'ctx', split_axis=2, concat_axis=0, tiled=True)  20.1 us
  transfers between devices with their start and end apart: 16, of which 11 were waited for; matrix products, arithmetic and copies ran while one was open for 22% of the time, Pallas kernels for 0%

profile of v2, /device:TPU:8, one launch (start us, length us, event | category | flops | bytes accessed | tf_op | source)
XLA Modules:
  0.0 749.2 jit_solution(11733509818180095344)
XLA Ops:
  13.6 54.2 %all-gather = bf16[1,2048,32]{2,0,1:T(2,128)(2,1)S(1)} all-gather(bf16[1,64,32]{2,0,1:T(2,128)(2,1)S(1)} %get-tuple-element.214), channel_id=2, replica_groups=mesh['section'=2,'dp'=4,'ctx'=32] {'ctx'}, dimensions={1}, use_global_device_ids=true | all-gather | bytes 135168 | tf_op jit(solution)/shard_map/all_gather | solution.py:171
  69.7 85.5 %all-gather.7.cloned.1.call-done = bf16[1,2048,4096]{2,1,0:T(8,128)(2,1)} async-done(((bf16[1,64,4096]{2,1,0:T(8,128)(2,1)}), bf16[1,2048,4096]{2,1,0:T(8,128)(2,1)}) %all-gather.7.cloned.1.call-update) | async-done | bytes 16777232 | tf_op jit(solution)/shard_map/all_gather | solution.py:170
  155.2 8.2 %fusion.14 = bf16[128,4096]{1,0:T(8,128)(2,1)S(1)} fusion(bf16[1,2048,4096]{2,1,0:T(8,128)(2,1)} %all-gather.7.cloned.1.call-done, f32[2048]{0:T(1024)S(1)} %bitcast.748, f32[128]{0:T(128)S(1)} %add_rsqrt_fusion.7, bf16[2,128,2048]{2,1,0:T(8,128)(2,1)S(1)} %copy-done.31, s32[]{:T(128)S(6)} %select_n.186), kind=kOutput, calls=%fused_computation.30 | convolution fusion | flops 2149056512 | bytes 18358788 | tf_op jit(solution)/shard_map/dot_general | solution.py:193
  173.5 4.7 copy.159
  178.2 4.6 reshape.831
  182.8 3.7 reshape.836
  189.0 7.8 %copy.266 = f32[1,16,16,8,16,8]{1,5,4,2,3,0:T(8,128)} copy(f32[1,16,16,8,16,8]{1,5,4,3,2,0:T(8,128)} %bitcast.682) | data formatting | bytes 2097152 | tf_op jit(solution)/shard_map/reshape | solution.py:62
  196.8 4.0 gather_fusion
  202.6 8.9 %copy.265 = f32[1,16,8,16,8,16]{5,3,4,2,1,0:T(8,128)} copy(f32[1,16,8,16,8,16]{5,4,3,2,1,0:T(8,128)} %reshape.831) | data formatting | bytes 2097152 | tf_op jit(solution)/shard_map/reshape | solution.py:75
  211.5 4.0 gather_fusion.1
  216.6 4.7 copy.268
  256.5 10.1 %all-to-all-start.1 = ((f32[1,1,32,128,64]{3,4,1,0,2:T(8,128)}), f32[1,1,32,128,64]{3,4,1,0,2:T(8,128)}, u32[]{:S(2)}, u32[]{:S(2)}) async-start(f32[1,1,32,128,64]{3,4,1,0,2:T(8,128)} %bitcast.731), calls=%async_computation.1 | async-start | bytes 2097152 | tf_op jit(solution)/shard_map/all_to_all | solution.py:246
  268.7 35.9 %all-to-all-done.1 = f32[1,1,32,128,64]{3,4,1,0,2:T(8,128)} async-done(((f32[1,1,32,128,64]{3,4,1,0,2:T(8,128)}), f32[1,1,32,128,64]{3,4,1,0,2:T(8,128)}, u32[]{:S(2)}, u32[]{:S(2)}) %all-to-all-start.1) | async-done | bytes 1048608 | tf_op jit(solution)/shard_map/all_to_all | solution.py:246
  307.4 6.6 all-to-all-start
  314.1 48.0 %all-to-all-done = f32[1,1,32,128,128]{4,3,1,0,2:T(8,128)} async-done(((f32[1,1,32,128,128]{4,3,1,0,2:T(8,128)}), f32[1,1,32,128,128]{4,3,1,0,2:T(8,128)}, u32[]{:S(2)}, u32[]{:S(2)}) %all-to-all-start) | async-done | bytes 2097184 | tf_op jit(solution)/shard_map/all_to_all | solution.py:245
  362.2 36.5 %while.4 = (s32[]{:T(128)}, f32[1,1,128,64]{2,3,1,0:T(8,128)S(1)}, f32[32,1,1,128,64]{3,4,2,1,0:T(8,128)S(1)}, f32[32,1,1,128,128]{4,3,2,1,0:T(8,128)}, f32[32,1,1,128,64]{3,4,2,1,0:T(8,128)}, /*index=5*/s32[]{:T(128)}) while((s32[]{:T(128)}, f32[1,1,128,64]{2,3,1,0:T(8,128)S(1)}, f32[32,1,1,128,64]{3,4,2,1,0:T(8,128)S(1)}, ...), condition=%wide.region_5.6_spmd, body=%wide.region_4.5_spmd.sunk | while | flops 12591106 | bytes 296009 | solution.py:251
  399.7 6.4 all-to-all-start.2
  407.3 69.8 %all-gather.2 = bf16[1,2048,32]{2,0,1:T(2,128)(2,1)} all-gather(bf16[1,64,32]{2,0,1:T(2,128)(2,1)S(1)} %get-tuple-element.213), channel_id=4, replica_groups=mesh['section'=2,'dp'=4,'ctx'=32] {'ctx'}, dimensions={1}, use_global_device_ids=true | all-gather | bytes 135168 | tf_op jit(solution)/shard_map/all_gather | solution.py:171
  497.3 8.4 %fusion.17 = bf16[128,4096]{1,0:T(8,128)(2,1)S(1)} fusion(bf16[1,2048,4096]{2,1,0:T(8,128)(2,1)} %all-gather.9.cloned.1.call-done, bf16[1,128,2048]{2,1,0:T(8,128)(2,1)S(1)} %get-tuple-element.186, f32[2048]{0:T(1024)S(1)} %bitcast.745, f32[128]{0:T(128)S(1)} %add_rsqrt_fusion.6), kind=kOutput, calls=%fused_computation.31 | convolution fusion | flops 2149056512 | bytes 18358784 | tf_op jit(solution)/shard_map/dot_general | solution.py:193
  505.8 3.9 collective-permute-start.8
  518.1 4.7 copy.191
  522.8 7.8 %copy.264 = f32[1,16,16,8,16,8]{1,5,4,2,3,0:T(8,128)} copy(f32[1,16,16,8,16,8]{1,5,4,3,2,0:T(8,128)} %bitcast.683) | data formatting | bytes 2097152 | tf_op jit(solution)/shard_map/reshape | solution.py:62
  530.5 4.0 gather_fusion.4
  541.9 4.6 reshape.871
  552.4 8.7 %copy.263 = f32[1,16,8,16,8,16]{5,3,4,2,1,0:T(8,128)} copy(f32[1,16,8,16,8,16]{5,4,3,2,1,0:T(8,128)} %reshape.871) | data formatting | bytes 2097152 | tf_op jit(solution)/shard_map/reshape | solution.py:75
  561.0 4.0 gather_fusion.5
  596.8 10.0 %all-to-all-start.4 = ((f32[1,1,32,128,64]{3,4,1,0,2:T(8,128)}), f32[1,1,32,128,64]{3,4,1,0,2:T(8,128)}, u32[]{:S(2)}, u32[]{:S(2)}) async-start(f32[1,1,32,128,64]{3,4,1,0,2:T(8,128)} %bitcast.730), calls=%async_computation.4 | async-start | bytes 2097152 | tf_op jit(solution)/shard_map/all_to_all | solution.py:246
  608.7 18.3 %all-to-all-done.4 = f32[1,1,32,128,64]{3,4,1,0,2:T(8,128)} async-done(((f32[1,1,32,128,64]{3,4,1,0,2:T(8,128)}), f32[1,1,32,128,64]{3,4,1,0,2:T(8,128)}, u32[]{:S(2)}, u32[]{:S(2)}) %all-to-all-start.4) | async-done | bytes 1048608 | tf_op jit(solution)/shard_map/all_to_all | solution.py:246
  628.5 40.9 %all_to_all.66 = f32[1,1,32,128,128]{4,3,1,0,2:T(8,128)} all-to-all(f32[1,1,32,128,128]{4,3,1,0,2:T(8,128)S(1)} %bitcast.719), channel_id=1, replica_groups=mesh['section'=2,'dp'=4,'ctx'=32] {'ctx'}, dimensions={2} | all-to-all | bytes 4194304 | tf_op jit(solution)/shard_map/all_to_all | solution.py:245
  669.6 36.5 %while.5 = (s32[]{:T(128)}, f32[1,1,128,64]{2,3,1,0:T(8,128)S(1)}, f32[32,1,1,128,64]{3,4,2,1,0:T(8,128)S(1)}, f32[32,1,1,128,128]{4,3,2,1,0:T(8,128)}, f32[32,1,1,128,64]{3,4,2,1,0:T(8,128)}, /*index=5*/s32[]{:T(128)}) while((s32[]{:T(128)}, f32[1,1,128,64]{2,3,1,0:T(8,128)S(1)}, f32[32,1,1,128,64]{3,4,2,1,0:T(8,128)S(1)}, ...), condition=%wide.region_12.13_spmd, body=%wide.region_11.12_spmd.sunk | while | flops 12591106 | bytes 296009 | solution.py:251
  707.1 6.4 all-to-all-start.5
  719.9 11.5 %all-to-all-done.5 = f32[32,1,1,128,64]{3,4,2,1,0:T(8,128)S(1)} async-done(((f32[32,1,1,128,64]{3,4,2,1,0:T(8,128)}), f32[32,1,1,128,64]{3,4,2,1,0:T(8,128)S(1)}, u32[]{:S(2)}, u32[]{:S(2)}) %all-to-all-start.5) | async-done | bytes 1048608 | tf_op jit(solution)/shard_map/all_to_all | solution.py:254
  (469 shorter events, 231.5 us)
Async XLA Ops:
  6.5 4.5 copy-start.37
  6.5 4.7 copy-start.35
  6.5 5.1 copy-start.36
  6.5 5.4 copy-start.38
  6.5 5.8 copy-start.39
  6.5 5.9 copy-start.31
  6.6 148.6 %all-gather.7.cloned.1.call-start = ((), (), s32[]{:S(2)}) async-start(), calls=%async_computation.6 | async-start | bytes 17301504 | tf_op jit(solution)/shard_map/all_gather | solution.py:170
  6.6 2.2 collective-permute-start.5
  10.9 486.4 %all-gather.9.cloned.1.call-start = ((), (), s32[]{:S(2)}) async-start(), calls=%async_computation.7 | async-start | bytes 17301504 | tf_op jit(solution)/shard_map/all_gather | solution.py:170
  11.0 57.3 %collective-permute-start.1 = (f32[1,2048]{1,0:T(1,128)S(1)}, f32[1,2048]{1,0:T(1,128)S(1)}, u32[]{:S(2)}, u32[]{:S(2)}) collective-permute-start(f32[1,2048]{1,0:T(1,128)S(1)} %copy-done.37), channel_id=1, source_target_pairs={{0,128},{128,0},{1,129},{129,1},{2,130},{130,2},{3,131},{131,3},{4... | collective-permute-start | bytes 24584 | tf_op jit(solution)/shard_map/ppermute | solution.py:151
  11.2 58.4 %collective-permute-start.4 = (bf16[1,4,4096]{2,1,0:T(4,128)(2,1)S(1)}, bf16[1,4,4096]{2,1,0:T(4,128)(2,1)S(1)}, u32[]{:S(2)}, u32[]{:S(2)}) collective-permute-start(bf16[1,4,4096]{2,1,0:T(4,128)(2,1)S(1)} %copy-done.35), channel_id=1, source_target_pairs={{0,128},{128,0},{1,129},{129,1},{2,130},{130,2},{3,131},{131,3},{4... | collective-permute-start | bytes 98312 | tf_op jit(solution)/shard_map/ppermute | solution.py:151
  11.7 1.8 collective-permute-start.2
  11.9 1.2 collective-permute-start
  12.3 1.2 collective-permute-start.3
  163.4 3.3 collective-permute-start.6
  173.5 13.0 %copy-start = (f32[16,128,128]{2,1,0:T(8,128)}, f32[16,128,128]{2,1,0:T(8,128)S(1)}, u32[]{:S(2)}) copy-start(f32[16,128,128]{2,1,0:T(8,128)S(1)} %fusion.30) | copy-start | bytes 3145732
  256.5 48.1 %all-to-all-start.1 = ((f32[1,1,32,128,64]{3,4,1,0,2:T(8,128)}), f32[1,1,32,128,64]{3,4,1,0,2:T(8,128)}, u32[]{:S(2)}, u32[]{:S(2)}) async-start(f32[1,1,32,128,64]{3,4,1,0,2:T(8,128)} %bitcast.731), calls=%async_computation.1 | async-start | bytes 2097152 | tf_op jit(solution)/shard_map/all_to_all | solution.py:246
  307.4 54.6 %all-to-all-start = ((f32[1,1,32,128,128]{4,3,1,0,2:T(8,128)}), f32[1,1,32,128,128]{4,3,1,0,2:T(8,128)}, u32[]{:S(2)}, u32[]{:S(2)}) async-start(f32[1,1,32,128,128]{4,3,1,0,2:T(8,128)} %bitcast.718), calls=%async_computation | async-start | bytes 4194304 | tf_op jit(solution)/shard_map/all_to_all | solution.py:245
  362.2 43.9 %copy-start.40 = (f32[1,128]{1,0:T(1,128)S(1)}, f32[1,128]{1,0:T(1,128)}, u32[]{:S(2)}) copy-start(f32[1,128]{1,0:T(1,128)} %param.19) | copy-start | bytes 1540
  399.7 86.5 %all-to-all-start.2 = ((f32[32,1,1,128,64]{3,4,2,1,0:T(8,128)}), f32[32,1,1,128,64]{3,4,2,1,0:T(8,128)S(1)}, u32[]{:S(2)}, u32[]{:S(2)}) async-start(f32[32,1,1,128,64]{3,4,2,1,0:T(8,128)} %copy-done.28), calls=%async_computation.2 | async-start | bytes 2097152 | tf_op jit(solution)/shard_map/all_to_all | solution.py:254
  406.1 1.2 collective-permute-start.7
  486.2 2.3 copy-start.23
  488.5 2.3 copy-start.26
  497.3 12.4 %copy-start.16 = (bf16[1,128,2048]{2,1,0:T(8,128)(2,1)}, bf16[1,128,2048]{2,1,0:T(8,128)(2,1)S(1)}, u32[]{:S(2)}) copy-start(bf16[1,128,2048]{2,1,0:T(8,128)(2,1)S(1)} %get-tuple-element.186) | copy-start | bytes 1572868
  505.8 5.5 collective-permute-start.8
  518.1 31.7 %copy-start.2 = (f32[16,128,128]{2,1,0:T(8,128)}, f32[16,128,128]{2,1,0:T(8,128)S(1)}, u32[]{:S(2)}) copy-start(f32[16,128,128]{2,1,0:T(8,128)S(1)} %fusion.31) | copy-start | bytes 3145732
  568.1 2.2 copy-start.4
  577.0 2.1 copy-start.14
  596.8 30.3 %all-to-all-start.4 = ((f32[1,1,32,128,64]{3,4,1,0,2:T(8,128)}), f32[1,1,32,128,64]{3,4,1,0,2:T(8,128)}, u32[]{:S(2)}, u32[]{:S(2)}) async-start(f32[1,1,32,128,64]{3,4,1,0,2:T(8,128)} %bitcast.730), calls=%async_computation.4 | async-start | bytes 2097152 | tf_op jit(solution)/shard_map/all_to_all | solution.py:246
  707.1 24.3 %all-to-all-start.5 = ((f32[32,1,1,128,64]{3,4,2,1,0:T(8,128)}), f32[32,1,1,128,64]{3,4,2,1,0:T(8,128)S(1)}, u32[]{:S(2)}, u32[]{:S(2)}) async-start(f32[32,1,1,128,64]{3,4,2,1,0:T(8,128)} %copy-done.27), calls=%async_computation.5 | async-start | bytes 2097152 | tf_op jit(solution)/shard_map/all_to_all | solution.py:254
  731.4 2.3 copy-start.22
  733.7 2.3 copy-start.25
  (25 other events, 33.2 us)
Sparse Core Ops, SparseCore 0:
  11.1 144.0 all-gather.6
  157.7 164.7 all-gather.8

commit v3 on v2

--- a/solution.py
+++ b/solution.py
@@ -158,8 +158,7 @@
             layers.append(chosen[0])
         return layers
 
-    all_qkv = every_layer(w_qkv)
-    all_gate = every_layer(w_gate)
+    all_weights = every_layer(jnp.concatenate([w_qkv, w_gate], axis=2))
     all_gain_in = every_layer(norm_gain)
     all_taps = every_layer(conv_weight)
     all_rates = every_layer(decay_rate)
@@ -167,12 +166,10 @@
     all_gain_out = every_layer(head_gain)
     hidden = lax.dynamic_slice_in_dim(tokens, section, 1, axis=0)
     for layer_index in range(layer_count):
-        full_qkv = lax.all_gather(all_qkv[layer_index], "ctx", axis=0, tiled=True)
-        full_gate = lax.all_gather(all_gate[layer_index], "ctx", axis=0, tiled=True)
+        full_weights = lax.all_gather(all_weights[layer_index], "ctx", axis=0, tiled=True)
         hidden = layer_apply(
             hidden,
-            full_qkv,
-            full_gate,
+            full_weights,
             all_gain_in[layer_index],
             all_taps[layer_index],
             all_rates[layer_index],
@@ -182,7 +179,7 @@
     return hidden
 
 
-def layer_apply(section_input, full_qkv, full_gate, gain_in, conv_taps, decay_rates, biases, gain_out):
+def layer_apply(section_input, full_weights, gain_in, conv_taps, decay_rates, biases, gain_out):
     groups, positions, model_width = section_input.shape
     blocks = positions // BLOCK
     layer_normed = (
@@ -190,8 +187,10 @@
         .astype(jnp.bfloat16)
         .reshape(groups * positions, model_width)
     )
-    proj_qkv = jnp.dot(layer_normed, full_qkv, preferred_element_type=jnp.float32)
-    proj_gate = jnp.dot(layer_normed, full_gate, preferred_element_type=jnp.float32)
+    projected = jnp.dot(layer_normed, full_weights, preferred_element_type=jnp.float32)
+    qkv_width = full_weights.shape[1] - 2 * NV
+    proj_qkv = projected[:, :qkv_width]
+    proj_gate = projected[:, qkv_width:]
     features = proj_qkv.astype(jnp.bfloat16).reshape(groups, positions, proj_qkv.shape[1])
     gate_raw = proj_gate.astype(jnp.bfloat16)
     previous_rows = from_behind(features[:, positions - (CONV - 1) :], "ctx", 1)
@@ -242,8 +241,15 @@
     sent_maps = jnp.repeat(local_map, column_parts, axis=1)[None]
     sent_bias = jnp.moveaxis(local_bias.reshape(groups, NV, DK, column_parts, part_width), 3, 2)
     sent_bias = sent_bias.reshape(groups, item_count, DK, part_width)[None]
-    got_maps = lax.all_to_all(sent_maps, "ctx", split_axis=2, concat_axis=0, tiled=True)
-    got_bias = lax.all_to_all(sent_bias, "ctx", split_axis=2, concat_axis=0, tiled=True)
+    got_both = lax.all_to_all(
+        jnp.concatenate([sent_maps, sent_bias], axis=-1),
+        "ctx",
+        split_axis=2,
+        concat_axis=0,
+        tiled=True,
+    )
+    got_maps = got_both[..., :DK]
+    got_bias = got_both[..., DK:]
 
     def chain_step(state_now, incoming):
         return (chain_product(incoming[0], state_now) + incoming[1], state_now)

time: 760 us -> 782 us (1.029)
  blocking collectives: 165 us -> 78.3 us
  waiting for transfers between devices: 205 us -> 265 us
  local copies, waits for them, and re-layouts: 134 us -> 184 us
  starting transfers between devices: 46.9 us -> 28 us
  other arithmetic: 16.4 us -> 30.7 us
    all_gather x2 -> x0, blocking collectives: 124 us -> none  [local(): full_gate = lax.all_gather(all_gate[layer_index], 'ctx', axis=0, tiled=True)]
    all_gather x2, waiting for transfers between devices: 85.5 us -> 143 us  [local(): lax.all_gather(all_weights[layer_index], 'ctx', axis=0, tiled=True)]
    dynamic_update_slice x64, local copies, waits for them, and re-layouts: 0.61 us -> 39.6 us  [layer_apply(): lax.scan(chain_step, jnp.zeros(got_bias.shape[1:], jnp.float32), (got_map...]
    all_to_all x1, blocking collectives: 40.9 us -> 78.3 us  [layer_apply(): lax.all_to_all(jnp.concatenate([sent_maps, sent_bias], axis=-1), 'ctx', s...]
    all_to_all x2, waiting for transfers between devices: 11.5 us -> 35.2 us  [layer_apply(): lax.all_to_all(entering_parts, 'ctx', split_axis=0, concat_axis=2, tiled=...]
    all_to_all x3 -> x1, waiting for transfers between devices: 102 us -> 82.1 us  [layer_apply(): lax.all_to_all(jnp.concatenate([sent_maps, sent_bias], axis=-1), 'ctx', s...]
    all_to_all x3 -> x1, starting transfers between devices: 26.7 us -> 9.97 us  [layer_apply(): lax.all_to_all(jnp.concatenate([sent_maps, sent_bias], axis=-1), 'ctx', s...]
    convert_element_type x2, other arithmetic: 3.06 us -> 11.5 us  [head_inputs(): features = mixed_rows.astype(jnp.float32)]
  transfers between devices with their start and end apart: 16 -> 13, of which waited for: 11 -> 10; matrix products, arithmetic and copies ran while one was open for 22% -> 26% of each run, Pallas kernels for 0% -> 0%
where the time goes in v3:
time: 782 us; the launch traced here: 771 us
  waiting for transfers between devices  265 us (34%)
  local copies, waits for them, and re-layouts  184 us (24%)
  matrix products  168 us (21%)
  blocking collectives  78.3 us (10%)
  other arithmetic  30.7 us (4%)
  starting transfers between devices  28 us (4%)
  between operations  14.9 us (2%)
    all_gather x2, waiting for transfers between devices, local(): lax.all_gather(all_weights[layer_index], 'ctx', axis=0, tiled=True)  143 us
    all_to_all x1, waiting for transfers between devices, layer_apply(): lax.all_to_all(jnp.concatenate([sent_maps, sent_bias], axis=-1), 'ctx', s...  82.1 us
    all_to_all x1, blocking collectives, layer_apply(): lax.all_to_all(jnp.concatenate([sent_maps, sent_bias], axis=-1), 'ctx', s...  78.3 us
    dot_general x68, matrix products, chain_product(): jnp.einsum('...ij,...jk->...ik', left_map, right_map, precision=PRECISE)  73.5 us
    reshape x12, local copies, waits for them, and re-layouts, unit_lower_inverse(): tiles = strict_part.reshape(lead + (pairs, 2 * width, pairs, 2 * width))  46.2 us
    dynamic_update_slice x64, local copies, waits for them, and re-layouts, layer_apply(): lax.scan(chain_step, jnp.zeros(got_bias.shape[1:], jnp.float32), (got_map...  39.6 us
    all_to_all x2, waiting for transfers between devices, layer_apply(): lax.all_to_all(entering_parts, 'ctx', split_axis=0, concat_axis=2, tiled=...  35.2 us
    dot_general x2, matrix products, layer_apply(): jnp.dot(layer_normed, full_weights, preferred_element_type=jnp.float32)  21.1 us
  transfers between devices with their start and end apart: 13, of which 10 were waited for; matrix products, arithmetic and copies ran while one was open for 26% of the time, Pallas kernels for 0%

profile of v3, /device:TPU:8, one launch (start us, length us, event | category | flops | bytes accessed | tf_op | source)
XLA Modules:
  0.0 770.9 jit_solution(15352007286744062031)
XLA Ops:
  15.0 142.9 %all-gather.5.cloned.1.call-done = bf16[1,2048,4128]{2,1,0:T(8,128)(2,1)} async-done(((bf16[1,64,4128]{2,1,0:T(8,128)(2,1)}), bf16[1,2048,4128]{2,1,0:T(8,128)(2,1)}) %all-gather.5.cloned.1.call-update) | async-done | bytes 16908304 | tf_op jit(solution)/shard_map/all_gather | solution.py:169
  158.0 10.6 %fusion.14 = bf16[128,4128]{0,1:T(8,128)(2,1)S(1)} fusion(bf16[1,2048,4128]{2,1,0:T(8,128)(2,1)} %all-gather.5.cloned.1.call-done, f32[2048]{0:T(1024)S(1)} %bitcast.723, f32[128]{0:T(128)S(1)} %add_rsqrt_fusion.7, bf16[2,128,2048]{2,1,0:T(8,128)(2,1)S(1)} %copy-done.32, s32[]{:T(128)S(6)} %select_n.168), kind=kOutput, calls=%fused_computation.30 | convolution fusion | flops 2165837824 | bytes 18498052 | tf_op jit(solution)/shard_map/dot_general | solution.py:190
  175.8 7.3 bitcast_convert_fusion.1
  188.1 4.7 copy.106
  192.8 4.7 reshape.825
  203.2 7.8 %copy.211 = f32[1,16,16,8,16,8]{1,5,4,2,3,0:T(8,128)} copy(f32[1,16,16,8,16,8]{1,5,4,3,2,0:T(8,128)} %bitcast.662) | data formatting | bytes 2097152 | tf_op jit(solution)/shard_map/reshape | solution.py:62
  211.0 4.6 gather_fusion
  217.3 8.7 %copy.210 = f32[1,16,8,16,8,16]{5,3,4,2,1,0:T(8,128)} copy(f32[1,16,8,16,8,16]{5,4,3,2,1,0:T(8,128)} %reshape.825) | data formatting | bytes 2097152 | tf_op jit(solution)/shard_map/reshape | solution.py:75
  226.1 4.2 gather_fusion.1
  231.5 4.9 copy.213
  276.2 10.0 %all-to-all-start = ((f32[1,1,32,128,192]{3,4,1,0,2:T(8,128)}), f32[1,1,32,128,192]{3,4,1,0,2:T(8,128)}, u32[]{:S(2)}, u32[]{:S(2)}) async-start(f32[1,1,32,128,192]{3,4,1,0,2:T(8,128)} %pad_maximum_fusion), calls=%async_computation | async-start | bytes 6291456 | tf_op jit(solution)/shard_map/all_to_all | solution.py:244
  286.2 82.1 %all-to-all-done = f32[1,1,32,128,192]{3,4,1,0,2:T(8,128)} async-done(((f32[1,1,32,128,192]{3,4,1,0,2:T(8,128)}), f32[1,1,32,128,192]{3,4,1,0,2:T(8,128)}, u32[]{:S(2)}, u32[]{:S(2)}) %all-to-all-start) | async-done | bytes 3145760 | tf_op jit(solution)/shard_map/all_to_all | solution.py:244
  373.9 53.6 %while.4 = (s32[]{:T(128)}, f32[1,1,128,64]{2,3,1,0:T(8,128)S(1)}, f32[32,1,1,128,64]{3,4,2,1,0:T(8,128)}, f32[32,1,1,128,128]{3,4,0,2,1:T(8,128)}, f32[32,1,1,128,64]{3,4,2,1,0:T(8,128)S(1)}, /*index=5*/s32[]{:T(128)}) while((s32[]{:T(128)}, f32[1,1,128,64]{2,3,1,0:T(8,128)S(1)}, f32[32,1,1,128,64]{3,4,2,1,0:T(8,128)}, ...), condition=%wide.region_5.6_spmd, body=%wide.region_4.5_spmd.sunk | while | flops 12591106 | bytes 296517 | solution.py:257
  427.4 5.4 all-to-all-start.1
  443.5 17.7 %all-to-all-done.1 = f32[32,1,1,128,64]{3,4,2,1,0:T(8,128)} async-done(((f32[32,1,1,128,64]{3,4,2,1,0:T(8,128)}), f32[32,1,1,128,64]{3,4,2,1,0:T(8,128)}, u32[]{:S(2)}, u32[]{:S(2)}) %all-to-all-start.1) | async-done | bytes 1048608 | tf_op jit(solution)/shard_map/all_to_all | solution.py:260
  461.2 3.5 convolution_subtract_fusion.2
  464.7 3.6 fusion.86
  475.6 10.6 %fusion.17 = bf16[128,4128]{0,1:T(8,128)(2,1)S(1)} fusion(bf16[1,2048,4128]{2,1,0:T(8,128)(2,1)} %all-gather.7.cloned.1.call-done, bf16[1,128,2048]{2,1,0:T(8,128)(2,1)S(1)} %get-tuple-element.200, f32[2048]{0:T(1024)S(1)} %bitcast.722, f32[128]{0:T(128)S(1)} %add_rsqrt_fusion.6), kind=kOutput, calls=%fused_computation.31 | convolution fusion | flops 2165837824 | bytes 18498048 | tf_op jit(solution)/shard_map/dot_general | solution.py:190
  487.0 3.4 collective-permute-start.7
  492.5 4.1 bitcast_convert_fusion
  502.7 4.7 copy.139
  507.3 7.8 %copy.209 = f32[1,16,16,8,16,8]{1,5,4,2,3,0:T(8,128)} copy(f32[1,16,16,8,16,8]{1,5,4,3,2,0:T(8,128)} %bitcast.663) | data formatting | bytes 2097152 | tf_op jit(solution)/shard_map/reshape | solution.py:62
  515.1 4.0 gather_fusion.4
  526.4 4.5 reshape.865
  536.9 8.7 %copy.208 = f32[1,16,8,16,8,16]{5,3,4,2,1,0:T(8,128)} copy(f32[1,16,8,16,8,16]{5,4,3,2,1,0:T(8,128)} %reshape.865) | data formatting | bytes 2097152 | tf_op jit(solution)/shard_map/reshape | solution.py:75
  545.6 4.0 gather_fusion.5
  584.3 78.3 %all_to_all.42 = f32[1,1,32,128,192]{3,4,1,0,2:T(8,128)S(1)} all-to-all(f32[1,1,32,128,192]{3,4,1,0,2:T(8,128)S(1)} %pad_maximum_fusion.1), channel_id=1, replica_groups=mesh['section'=2,'dp'=4,'ctx'=32] {'ctx'}, dimensions={2} | all-to-all | bytes 6291456 | tf_op jit(solution)/shard_map/all_to_all | solution.py:244
  665.3 53.5 %while.5 = (s32[]{:T(128)}, f32[1,1,128,64]{2,3,1,0:T(8,128)S(1)}, f32[32,1,1,128,64]{3,4,2,1,0:T(8,128)}, f32[32,1,1,128,128]{3,4,0,2,1:T(8,128)}, f32[32,1,1,128,64]{3,4,2,1,0:T(8,128)S(1)}, /*index=5*/s32[]{:T(128)}) while((s32[]{:T(128)}, f32[1,1,128,64]{2,3,1,0:T(8,128)S(1)}, f32[32,1,1,128,64]{3,4,2,1,0:T(8,128)}, ...), condition=%wide.region_12.13_spmd, body=%wide.region_11.12_spmd.sunk | while | flops 12591106 | bytes 296517 | solution.py:257
  718.8 5.3 all-to-all-start.3
  733.1 17.5 %all-to-all-done.3 = f32[32,1,1,128,64]{3,4,2,1,0:T(8,128)} async-done(((f32[32,1,1,128,64]{3,4,2,1,0:T(8,128)}), f32[32,1,1,128,64]{3,4,2,1,0:T(8,128)}, u32[]{:S(2)}, u32[]{:S(2)}) %all-to-all-start.3) | async-done | bytes 1048608 | tf_op jit(solution)/shard_map/all_to_all | solution.py:260
  750.6 3.5 convolution_subtract_fusion
  754.1 3.6 fusion.79
  (469 shorter events, 271.4 us)
Async XLA Ops:
  6.5 6.4 copy-start.40
  6.5 6.6 copy-start.39
  6.5 7.0 copy-start.41
  6.5 7.1 copy-start.42
  6.5 7.5 copy-start.32
  6.6 151.4 %all-gather.5.cloned.1.call-start = ((), (), s32[]{:S(2)}) async-start(), calls=%async_computation.4 | async-start | bytes 17842176 | tf_op jit(solution)/shard_map/all_gather | solution.py:169
  8.6 2.0 collective-permute-start.2
  12.9 462.0 %all-gather.7.cloned.1.call-start = ((), (), s32[]{:S(2)}) async-start(), calls=%async_computation.5 | async-start | bytes 17842176 | tf_op jit(solution)/shard_map/all_gather | solution.py:169
  12.9 1.9 collective-permute-start.1
  13.1 1.7 collective-permute-start.4
  13.5 1.2 collective-permute-start
  13.7 1.2 collective-permute-start.3
  168.6 4.1 copy-start.11
  170.5 3.9 collective-permute-start.5
  172.7 3.2 copy-start.14
  183.2 20.0 %copy-start.10 = (f32[128,4096]{0,1:T(8,128)}, f32[128,4096]{0,1:T(8,128)S(1)}, u32[]{:S(2)}) copy-start(f32[128,4096]{0,1:T(8,128)S(1)} %bitcast_convert_fusion.1) | copy-start | bytes 6291460
  188.1 12.6 %copy-start = (f32[16,128,128]{2,1,0:T(8,128)}, f32[16,128,128]{2,1,0:T(8,128)S(1)}, u32[]{:S(2)}) copy-start(f32[16,128,128]{2,1,0:T(8,128)S(1)} %fusion.30) | copy-start | bytes 3145732
  276.2 92.1 %all-to-all-start = ((f32[1,1,32,128,192]{3,4,1,0,2:T(8,128)}), f32[1,1,32,128,192]{3,4,1,0,2:T(8,128)}, u32[]{:S(2)}, u32[]{:S(2)}) async-start(f32[1,1,32,128,192]{3,4,1,0,2:T(8,128)} %pad_maximum_fusion), calls=%async_computation | async-start | bytes 6291456 | tf_op jit(solution)/shard_map/all_to_all | solution.py:244
  373.9 59.0 %copy-start.43 = (f32[1,128]{1,0:T(1,128)S(1)}, f32[1,128]{1,0:T(1,128)}, u32[]{:S(2)}) copy-start(f32[1,128]{1,0:T(1,128)} %param.19) | copy-start | bytes 1540
  427.4 33.7 %all-to-all-start.1 = ((f32[32,1,1,128,64]{3,4,2,1,0:T(8,128)}), f32[32,1,1,128,64]{3,4,2,1,0:T(8,128)}, u32[]{:S(2)}, u32[]{:S(2)}) async-start(f32[32,1,1,128,64]{3,4,2,1,0:T(8,128)} %get-tuple-element.123), calls=%async_computation.1 | async-start | bytes 2097152 | tf_op jit(solution)/shard_map/all_to_all | solution.py:260
  432.8 1.7 collective-permute-start.6
  434.5 5.7 copy-start.6
  443.5 21.2 %copy-start.24 = (f32[1,16,128,128]{3,2,1,0:T(8,128)S(1)}, f32[1,16,128,128]{3,2,1,0:T(8,128)}, u32[]{:S(2)}) copy-start(f32[1,16,128,128]{3,2,1,0:T(8,128)} %bitcast_multiply_fusion.8) | copy-start | bytes 3145732
  464.7 3.6 copy-start.28
  487.0 5.0 collective-permute-start.7
  502.7 31.7 %copy-start.2 = (f32[16,128,128]{2,1,0:T(8,128)}, f32[16,128,128]{2,1,0:T(8,128)S(1)}, u32[]{:S(2)}) copy-start(f32[16,128,128]{2,1,0:T(8,128)S(1)} %fusion.31) | copy-start | bytes 3145732
  552.7 2.2 copy-start.4
  561.6 2.1 copy-start.15
  718.8 31.7 %all-to-all-start.3 = ((f32[32,1,1,128,64]{3,4,2,1,0:T(8,128)}), f32[32,1,1,128,64]{3,4,2,1,0:T(8,128)}, u32[]{:S(2)}, u32[]{:S(2)}) async-start(f32[32,1,1,128,64]{3,4,2,1,0:T(8,128)} %get-tuple-element.124), calls=%async_computation.3 | async-start | bytes 2097152 | tf_op jit(solution)/shard_map/all_to_all | solution.py:260
  724.1 5.7 copy-start.8
  733.1 21.0 %copy-start.23 = (f32[1,16,128,128]{3,2,1,0:T(8,128)S(1)}, f32[1,16,128,128]{3,2,1,0:T(8,128)}, u32[]{:S(2)}) copy-start(f32[1,16,128,128]{3,2,1,0:T(8,128)} %bitcast_multiply_fusion.5) | copy-start | bytes 3145732
  754.1 3.6 copy-start.27
  (27 other events, 35.8 us)
Sparse Core Ops, SparseCore 0:
  13.0 144.9 all-gather.4
  160.6 165.8 all-gather.6

commit v4 on v2

--- a/solution.py
+++ b/solution.py
@@ -40,12 +40,12 @@
     return jax.nn.silu(running_sum).astype(jnp.bfloat16)
 
 
-def head_inputs(mixed_rows, gate_raw, decay_rates, biases):
-    row_count = mixed_rows.shape[0]
-    features = mixed_rows.astype(jnp.float32)
+def head_inputs(mixed_qk, mixed_v, gate_raw, decay_rates, biases):
+    row_count = mixed_qk.shape[0]
+    features = mixed_qk.astype(jnp.float32)
     queries = unit_rows(features[:, : NK * DK].reshape(row_count, NK, DK)) * DK ** (-0.5)
     key_rows = unit_rows(features[:, NK * DK : 2 * NK * DK].reshape(row_count, NK, DK))
-    values = features[:, 2 * NK * DK :].reshape(row_count, NV, DV)
+    values = mixed_v.astype(jnp.float32).reshape(row_count, NV, DV)
     queries = jnp.repeat(queries, NV // NK, axis=1)
     key_rows = jnp.repeat(key_rows, NV // NK, axis=1)
     gate_float = gate_raw.astype(jnp.float32)
@@ -108,15 +108,16 @@
     key_inner = jnp.einsum("nhid,nhjd->nhij", key_heads, key_heads, precision=PRECISE)
     strict_part = jnp.where(strict_mask, beta_heads[..., :, None] * key_inner * decay_ratio, 0.0)
     gamma_rows = jnp.exp(cumulative)
-    right_side = jnp.concatenate(
-        [beta_heads[..., None] * value_heads, (beta_heads * gamma_rows)[..., None] * key_heads],
-        axis=-1,
-    )
-    solved = jnp.einsum(
-        "...ij,...jk->...ik", unit_lower_inverse(strict_part), right_side, precision=PRECISE
-    )
-    fresh_rows = solved[..., : value_heads.shape[-1]]
-    mixing = solved[..., value_heads.shape[-1] :]
+    inverse = unit_lower_inverse(strict_part)
+    mixing = jnp.einsum(
+        "...ij,...jk->...ik",
+        inverse,
+        (beta_heads * gamma_rows)[..., None] * key_heads,
+        precision=PRECISE,
+    )
+    fresh_rows = jnp.einsum(
+        "...ij,...jk->...ik", inverse, beta_heads[..., None] * value_heads, precision=PRECISE
+    )
     scores = jnp.einsum("nhid,nhjd->nhij", query_heads, key_heads, precision=PRECISE) * decay_ratio
     qgamma = gamma_rows[..., None] * query_heads
     key_tail = jnp.exp(cumulative[..., -1:] - cumulative)[..., None] * key_heads
@@ -158,21 +159,27 @@
             layers.append(chosen[0])
         return layers
 
-    all_qkv = every_layer(w_qkv)
-    all_gate = every_layer(w_gate)
+    qk_width = 2 * NK * DK
+    all_first = every_layer(jnp.concatenate([w_qkv[..., :qk_width], w_gate], axis=2))
+    all_second = every_layer(w_qkv[..., qk_width:])
     all_gain_in = every_layer(norm_gain)
     all_taps = every_layer(conv_weight)
     all_rates = every_layer(decay_rate)
     all_biases = every_layer(dt_bias)
     all_gain_out = every_layer(head_gain)
     hidden = lax.dynamic_slice_in_dim(tokens, section, 1, axis=0)
+    arrived = None
     for layer_index in range(layer_count):
-        full_qkv = lax.all_gather(all_qkv[layer_index], "ctx", axis=0, tiled=True)
-        full_gate = lax.all_gather(all_gate[layer_index], "ctx", axis=0, tiled=True)
-        hidden = layer_apply(
+        first_shard = all_first[layer_index]
+        if arrived is not None:
+            arrived, first_shard = lax.optimization_barrier((arrived, first_shard))
+        full_first = lax.all_gather(first_shard, "ctx", axis=0, tiled=True)
+        full_first, second_shard = lax.optimization_barrier((full_first, all_second[layer_index]))
+        full_second = lax.all_gather(second_shard, "ctx", axis=0, tiled=True)
+        hidden, arrived = layer_apply(
             hidden,
-            full_qkv,
-            full_gate,
+            full_first,
+            full_second,
             all_gain_in[layer_index],
             all_taps[layer_index],
             all_rates[layer_index],
@@ -182,7 +189,7 @@
     return hidden
 
 
-def layer_apply(section_input, full_qkv, full_gate, gain_in, conv_taps, decay_rates, biases, gain_out):
+def layer_apply(section_input, full_first, full_second, gain_in, conv_taps, decay_rates, biases, gain_out):
     groups, positions, model_width = section_input.shape
     blocks = positions // BLOCK
     layer_normed = (
@@ -190,14 +197,21 @@
         .astype(jnp.bfloat16)
         .reshape(groups * positions, model_width)
     )
-    proj_qkv = jnp.dot(layer_normed, full_qkv, preferred_element_type=jnp.float32)
-    proj_gate = jnp.dot(layer_normed, full_gate, preferred_element_type=jnp.float32)
-    features = proj_qkv.astype(jnp.bfloat16).reshape(groups, positions, proj_qkv.shape[1])
-    gate_raw = proj_gate.astype(jnp.bfloat16)
-    previous_rows = from_behind(features[:, positions - (CONV - 1) :], "ctx", 1)
-    mixed_rows = conv_rows(jnp.concatenate([previous_rows, features], axis=1), conv_taps)
+    projected = jnp.dot(layer_normed, full_first, preferred_element_type=jnp.float32)
+    qk_width = full_first.shape[1] - 2 * NV
+    features_qk = projected[:, :qk_width].astype(jnp.bfloat16).reshape(groups, positions, qk_width)
+    gate_raw = projected[:, qk_width:].astype(jnp.bfloat16)
+    proj_v = jnp.dot(layer_normed, full_second, preferred_element_type=jnp.float32)
+    features_v = proj_v.astype(jnp.bfloat16).reshape(groups, positions, proj_v.shape[1])
+
+    def mixed_part(features, taps):
+        previous_rows = from_behind(features[:, positions - (CONV - 1) :], "ctx", 1)
+        mixed = conv_rows(jnp.concatenate([previous_rows, features], axis=1), taps)
+        return mixed.reshape(groups * positions, mixed.shape[2])
+
     queries, key_rows, values, strength, logdecay = head_inputs(
-        mixed_rows.reshape(groups * positions, mixed_rows.shape[2]),
+        mixed_part(features_qk, conv_taps[:, :qk_width]),
+        mixed_part(features_v, conv_taps[:, qk_width:]),
         gate_raw,
         decay_rates,
         biases,
@@ -260,7 +274,7 @@
     outputs = jnp.transpose(outputs, (1, 0, 3, 2, 4)).reshape(groups, positions, NV, DV)
     normed_out = rms_rows(outputs, gain_out).reshape(groups, positions, NV * DV)
     outcome = (section_input.astype(jnp.float32) + normed_out).astype(jnp.bfloat16)
-    return outcome
+    return outcome, step_biases
 
 
 def solution(mesh):

time: 760 us -> 811 us (1.067)
  blocking collectives: 165 us -> 52.7 us
  waiting for transfers between devices: 205 us -> 307 us
  matrix products: 165 us -> 199 us
  other arithmetic: 16.4 us -> 34.4 us
  starting transfers between devices: 46.9 us -> 56.8 us
    all_gather x2 -> x0, blocking collectives: 124 us -> none  [local(): full_gate = lax.all_gather(all_gate[layer_index], 'ctx', axis=0, tiled=True)]
    ppermute x2 -> x4, waiting for transfers between devices: 1.5 us -> 103 us  [from_behind(): return lax.ppermute(value, axis, pairs)]
    all_to_all x1, waiting for transfers between devices: 48 us -> 0.01 us  [layer_apply(): lax.all_to_all(sent_maps, 'ctx', split_axis=2, concat_axis=0, tiled=True)]
    all_to_all x2, waiting for transfers between devices: 11.5 us -> 43.5 us  [layer_apply(): lax.all_to_all(entering_parts, 'ctx', split_axis=0, concat_axis=2, tiled=...]
    all_gather x2 -> x4, waiting for transfers between devices: 85.5 us -> 103 us  [the longest x2 103 us: local(): full_first = lax.all_gather(first_shard, 'ctx', axis=0, tiled=True)]
    dot_general x6 -> x8, matrix products: 21.2 us -> 36.5 us  [the longest x2 14.5 us: layer_apply(): jnp.dot(layer_normed, full_first, preferred_element_type=jnp.float32)]
    all_to_all x1, blocking collectives: 40.9 us -> 52.7 us  [layer_apply(): lax.all_to_all(sent_maps, 'ctx', split_axis=2, concat_axis=0, tiled=True)]
    unnamed x93 -> x67, local copies, waits for them, and re-layouts: 17.9 us -> 7.71 us
  transfers between devices with their start and end apart: 16 -> 20, of which waited for: 11 -> 11; matrix products, arithmetic and copies ran while one was open for 22% -> 35% of each run, Pallas kernels for 0% -> 0%
where the time goes in v4:
time: 811 us; the launch traced here: 799 us
  waiting for transfers between devices  307 us (38%)
  matrix products  199 us (25%)
  local copies, waits for them, and re-layouts  132 us (16%)
  starting transfers between devices  56.8 us (7%)
  blocking collectives  52.7 us (6%)
  other arithmetic  34.4 us (4%)
  between operations  15 us (2%)
    all_gather x2, waiting for transfers between devices, local(): full_first = lax.all_gather(first_shard, 'ctx', axis=0, tiled=True)  103 us
    ppermute x4, waiting for transfers between devices, from_behind(): return lax.ppermute(value, axis, pairs)  103 us
    dot_general x68, matrix products, chain_product(): jnp.einsum('...ij,...jk->...ik', left_map, right_map, precision=PRECISE)  77.7 us
    all_to_all x2, waiting for transfers between devices, layer_apply(): lax.all_to_all(sent_bias, 'ctx', split_axis=2, concat_axis=0, tiled=True)  53.3 us
    all_to_all x1, blocking collectives, layer_apply(): lax.all_to_all(sent_maps, 'ctx', split_axis=2, concat_axis=0, tiled=True)  52.7 us
    reshape x12, local copies, waits for them, and re-layouts, unit_lower_inverse(): tiles = strict_part.reshape(lead + (pairs, 2 * width, pairs, 2 * width))  47.6 us
    all_to_all x2, waiting for transfers between devices, layer_apply(): lax.all_to_all(entering_parts, 'ctx', split_axis=0, concat_axis=2, tiled=...  43.5 us
    all_to_all x2, starting transfers between devices, layer_apply(): lax.all_to_all(sent_bias, 'ctx', split_axis=2, concat_axis=0, tiled=True)  18.6 us
  transfers between devices with their start and end apart: 20, of which 11 were waited for; matrix products, arithmetic and copies ran while one was open for 35% of the time, Pallas kernels for 0%

profile of v4, /device:TPU:8, one launch (start us, length us, event | category | flops | bytes accessed | tf_op | source)
XLA Modules:
  0.0 799.1 jit_solution(2483379573135600032)
XLA Ops:
  13.7 103.4 %all-gather.12.cloned.1.call-done = bf16[1,2048,2080]{2,1,0:T(8,128)(2,1)} async-done(((bf16[1,64,2080]{2,1,0:T(8,128)(2,1)}), bf16[1,2048,2080]{2,1,0:T(8,128)(2,1)}) %all-gather.12.cloned.1.call-update) | async-done | bytes 8519696 | tf_op jit(solution)/shard_map/all_gather | solution.py:176
  123.2 7.3 convolution_convert_fusion.1
  133.6 15.8 %collective-permute-done.6 = bf16[1,3,2048]{1,2,0:T(8,128)(2,1)S(1)} collective-permute-done((bf16[1,3,2048]{1,2,0:T(8,128)(2,1)S(1)}, bf16[1,3,2048]{1,2,0:T(8,128)(2,1)S(1)}, u32[]{:S(2)}, u32[]{:S(2)}) %collective-permute-start.6) | collective-permute-done | bytes 12320 | tf_op jit(solution)/shard_map/ppermute | solution.py:20
  156.4 4.6 copy.100
  161.0 4.6 reshape.975
  171.3 7.8 copy.201
  185.0 8.7 %copy.200 = f32[1,16,8,16,8,16]{5,3,4,2,1,0:T(8,128)} copy(f32[1,16,8,16,8,16]{5,4,3,2,1,0:T(8,128)} %reshape.975) | data formatting | bytes 2097152 | tf_op jit(solution)/shard_map/reshape | solution.py:75
  199.0 4.8 copy.203
  219.2 10.6 %fusion.15 = f32[1,16,16,8,8]{4,3,2,1,0:T(8,128)S(1)} fusion(f32[1,16,16,8,8]{4,3,2,1,0:T(8,128)S(1)} %fusion.14, f32[16,16,8,8]{3,2,1,0:T(8,128)S(1)} %fusion.179), kind=kOutput, calls=%fused_computation.65 | convolution fusion | flops 1589248 | bytes 196608 | tf_op jit(solution)/shard_map/...ij,...jk->...ik/dot_general | solution.py:70
  243.3 12.0 %all-to-all-start = ((f32[1,1,32,128,128]{4,3,1,0,2:T(8,128)}), f32[1,1,32,128,128]{4,3,1,0,2:T(8,128)}, u32[]{:S(2)}, u32[]{:S(2)}) async-start(f32[1,1,32,128,128]{4,3,1,0,2:T(8,128)} %bitcast.720), calls=%async_computation | async-start | bytes 4194304 | tf_op jit(solution)/shard_map/all_to_all | solution.py:259
  255.3 7.0 convolution_convert_fusion.3
  269.5 70.6 %collective-permute-done.7 = bf16[1,3,2048]{1,2,0:T(8,128)(2,1)S(1)} collective-permute-done((bf16[1,3,2048]{1,2,0:T(8,128)(2,1)S(1)}, bf16[1,3,2048]{1,2,0:T(8,128)(2,1)S(1)}, u32[]{:S(2)}, u32[]{:S(2)}) %collective-permute-start.7) | collective-permute-done | bytes 12320 | tf_op jit(solution)/shard_map/ppermute | solution.py:20
  352.1 11.0 %all-to-all-start.1 = ((f32[1,1,32,128,64]{3,4,1,0,2:T(8,128)}), f32[1,1,32,128,64]{3,4,1,0,2:T(8,128)S(1)}, u32[]{:S(2)}, u32[]{:S(2)}) async-start(f32[1,1,32,128,64]{3,4,1,0,2:T(8,128)} %bitcast.728), calls=%async_computation.1 | async-start | bytes 2097152 | tf_op jit(solution)/shard_map/all_to_all | solution.py:260
  363.7 28.5 %all-to-all-done.1 = f32[1,1,32,128,64]{3,4,1,0,2:T(8,128)S(1)} async-done(((f32[1,1,32,128,64]{3,4,1,0,2:T(8,128)}), f32[1,1,32,128,64]{3,4,1,0,2:T(8,128)S(1)}, u32[]{:S(2)}, u32[]{:S(2)}) %all-to-all-start.1) | async-done | bytes 1048608 | tf_op jit(solution)/shard_map/all_to_all | solution.py:260
  393.3 36.5 %while.4 = (s32[]{:T(128)}, f32[1,1,128,64]{2,3,1,0:T(8,128)S(1)}, f32[32,1,1,128,64]{3,4,2,1,0:T(8,128)S(1)}, f32[32,1,1,128,128]{4,3,2,1,0:T(8,128)}, f32[32,1,1,128,64]{3,4,2,1,0:T(8,128)}, /*index=5*/s32[]{:T(128)}) while((s32[]{:T(128)}, f32[1,1,128,64]{2,3,1,0:T(8,128)S(1)}, f32[32,1,1,128,64]{3,4,2,1,0:T(8,128)S(1)}, ...), condition=%wide.region_5.6_spmd, body=%wide.region_4.5_spmd.sunk | while | flops 12591106 | bytes 296009 | solution.py:265
  430.8 6.4 all-to-all-start.2
  447.5 28.0 %all-to-all-done.2 = f32[32,1,1,128,64]{3,4,2,1,0:T(8,128)S(1)} async-done(((f32[32,1,1,128,64]{3,4,2,1,0:T(8,128)}), f32[32,1,1,128,64]{3,4,2,1,0:T(8,128)S(1)}, u32[]{:S(2)}, u32[]{:S(2)}) %all-to-all-start.2) | async-done | bytes 1048608 | tf_op jit(solution)/shard_map/all_to_all | solution.py:268
  490.3 7.3 convolution_convert_fusion
  497.6 7.2 convolution_convert_fusion.2
  506.6 5.7 collective-permute-start.10
  515.1 16.7 %collective-permute-done.9 = bf16[1,3,2048]{1,2,0:T(8,128)(2,1)S(1)} collective-permute-done((bf16[1,3,2048]{1,2,0:T(8,128)(2,1)S(1)}, bf16[1,3,2048]{1,2,0:T(8,128)(2,1)S(1)}, u32[]{:S(2)}, u32[]{:S(2)}) %collective-permute-start.9) | collective-permute-done | bytes 12320 | tf_op jit(solution)/shard_map/ppermute | solution.py:20
  538.7 4.7 copy.131
  543.4 7.8 copy.199
  561.5 4.6 reshape.1015
  572.0 8.7 %copy.198 = f32[1,16,8,16,8,16]{5,3,4,2,1,0:T(8,128)} copy(f32[1,16,8,16,8,16]{5,4,3,2,1,0:T(8,128)} %reshape.1015) | data formatting | bytes 2097152 | tf_op jit(solution)/shard_map/reshape | solution.py:75
  604.0 4.6 multiply_convert_fusion
  624.2 7.6 all-to-all-start.4
  632.8 24.9 %all-to-all-done.4 = f32[1,1,32,128,64]{3,4,1,0,2:T(8,128)} async-done(((f32[1,1,32,128,64]{3,4,1,0,2:T(8,128)}), f32[1,1,32,128,64]{3,4,1,0,2:T(8,128)}, u32[]{:S(2)}, u32[]{:S(2)}) %all-to-all-start.4) | async-done | bytes 1048608 | tf_op jit(solution)/shard_map/all_to_all | solution.py:260
  657.9 52.7 %all_to_all.66 = f32[1,1,32,128,128]{4,3,1,0,2:T(8,128)} all-to-all(f32[1,1,32,128,128]{4,3,1,0,2:T(8,128)S(1)} %bitcast.721), channel_id=1, replica_groups=mesh['section'=2,'dp'=4,'ctx'=32] {'ctx'}, dimensions={2} | all-to-all | bytes 4194304 | tf_op jit(solution)/shard_map/all_to_all | solution.py:259
  710.7 36.5 %while.5 = (s32[]{:T(128)}, f32[1,1,128,64]{2,3,1,0:T(8,128)S(1)}, f32[32,1,1,128,64]{3,4,2,1,0:T(8,128)S(1)}, f32[32,1,1,128,128]{4,3,2,1,0:T(8,128)}, f32[32,1,1,128,64]{3,4,2,1,0:T(8,128)}, /*index=5*/s32[]{:T(128)}) while((s32[]{:T(128)}, f32[1,1,128,64]{2,3,1,0:T(8,128)S(1)}, f32[32,1,1,128,64]{3,4,2,1,0:T(8,128)S(1)}, ...), condition=%wide.region_12.13_spmd, body=%wide.region_11.12_spmd.sunk | while | flops 12591106 | bytes 296009 | solution.py:265
  748.2 5.0 all-to-all-start.5
  762.1 15.5 %all-to-all-done.5 = f32[32,1,1,128,64]{3,4,2,1,0:T(8,128)S(1)} async-done(((f32[32,1,1,128,64]{3,4,2,1,0:T(8,128)}), f32[32,1,1,128,64]{3,4,2,1,0:T(8,128)S(1)}, u32[]{:S(2)}, u32[]{:S(2)}) %all-to-all-start.5) | async-done | bytes 1048608 | tf_op jit(solution)/shard_map/all_to_all | solution.py:268
  (457 shorter events, 277.9 us)
Async XLA Ops:
  6.5 110.5 %all-gather.12.cloned.1.call-start = ((), (), s32[]{:S(2)}) async-start(), calls=%async_computation.9 | async-start | bytes 9191424 | tf_op jit(solution)/shard_map/all_gather | solution.py:176
  7.5 1.6 collective-permute-start.3
  11.0 1.6 collective-permute-start.2
  13.6 241.7 %all-gather.6.cloned.1.call-start = ((), (), s32[]{:S(2)}) async-start(), calls=%async_computation.6 | async-start | bytes 8650752 | tf_op jit(solution)/shard_map/all_gather | solution.py:178
  117.1 246.1 %all-gather.8.cloned.1.call-start = ((), (), s32[]{:S(2)}) async-start(), calls=%async_computation.7 | async-start | bytes 9191424 | tf_op jit(solution)/shard_map/all_gather | solution.py:176
  117.1 3.8 collective-permute-start.1
  117.2 4.4 collective-permute-start.5
  117.7 1.9 collective-permute-start
  117.8 2.5 collective-permute-start.4
  130.7 18.7 %collective-permute-start.6 = (bf16[1,3,2048]{1,2,0:T(8,128)(2,1)S(1)}, bf16[1,3,2048]{1,2,0:T(8,128)(2,1)S(1)}, u32[]{:S(2)}, u32[]{:S(2)}) collective-permute-start(bf16[1,3,2048]{1,2,0:T(8,128)(2,1)S(1)} %slice.342), channel_id=1, source_target_pairs={{0,1},{1,2},{2,3},{3,4},{4,5},{5,6},{6,7},{7,8},{8,9},{9,10},{10,1... | collective-permute-start | bytes 36872 | tf_op jit(solution)/shard_map/ppermute | solution.py:20
  156.4 12.5 %copy-start = (f32[16,128,128]{2,1,0:T(8,128)}, f32[16,128,128]{2,1,0:T(8,128)S(1)}, u32[]{:S(2)}) copy-start(f32[16,128,128]{2,1,0:T(8,128)S(1)} %fusion.12) | copy-start | bytes 3145732
  210.3 7.1 copy-start.9
  210.3 19.5 %copy-start.26 = (f32[8,16,16,16]{3,2,0,1:T(8,128)S(1)}, f32[8,16,16,16]{3,2,0,1:T(8,128)}, u32[]{:S(2)}) copy-start(f32[8,16,16,16]{3,2,0,1:T(8,128)} %copy.211) | copy-start | bytes 393220
  215.5 16.7 %copy-start.25 = (f32[4,16,32,32]{3,2,0,1:T(8,128)S(1)}, f32[4,16,32,32]{3,2,0,1:T(8,128)}, u32[]{:S(2)}) copy-start(f32[4,16,32,32]{3,2,0,1:T(8,128)} %copy.210) | copy-start | bytes 786436
  243.3 108.8 %all-to-all-start = ((f32[1,1,32,128,128]{4,3,1,0,2:T(8,128)}), f32[1,1,32,128,128]{4,3,1,0,2:T(8,128)}, u32[]{:S(2)}, u32[]{:S(2)}) async-start(f32[1,1,32,128,128]{4,3,1,0,2:T(8,128)} %bitcast.720), calls=%async_computation | async-start | bytes 4194304 | tf_op jit(solution)/shard_map/all_to_all | solution.py:259
  262.5 77.5 %collective-permute-start.7 = (bf16[1,3,2048]{1,2,0:T(8,128)(2,1)S(1)}, bf16[1,3,2048]{1,2,0:T(8,128)(2,1)S(1)}, u32[]{:S(2)}, u32[]{:S(2)}) collective-permute-start(bf16[1,3,2048]{1,2,0:T(8,128)(2,1)S(1)} %slice.368), channel_id=1, source_target_pairs={{0,1},{1,2},{2,3},{3,4},{4,5},{5,6},{6,7},{7,8},{8,9},{9,10},{10,1... | collective-permute-start | bytes 36872 | tf_op jit(solution)/shard_map/ppermute | solution.py:20
  342.9 94.2 %copy-start.32 = (f32[1,128]{1,0:T(1,128)S(1)}, f32[1,128]{1,0:T(1,128)}, u32[]{:S(2)}) copy-start(f32[1,128]{1,0:T(1,128)} %param.19) | copy-start | bytes 1540
  347.9 96.3 %copy-start.6 = (f32[128,8,2,128]{3,0,2,1:T(8,128)S(1)}, f32[128,8,2,128]{3,0,2,1:T(8,128)}, u32[]{:S(2)}) copy-start(f32[128,8,2,128]{3,0,2,1:T(8,128)} %copy-done.5) | copy-start | bytes 3145732
  352.1 40.0 %all-to-all-start.1 = ((f32[1,1,32,128,64]{3,4,1,0,2:T(8,128)}), f32[1,1,32,128,64]{3,4,1,0,2:T(8,128)S(1)}, u32[]{:S(2)}, u32[]{:S(2)}) async-start(f32[1,1,32,128,64]{3,4,1,0,2:T(8,128)} %bitcast.728), calls=%async_computation.1 | async-start | bytes 2097152 | tf_op jit(solution)/shard_map/all_to_all | solution.py:260
  363.1 134.5 %all-gather.10.cloned.1.call-start = ((), (), s32[]{:S(2)}) async-start(), calls=%async_computation.8 | async-start | bytes 8650752 | tf_op jit(solution)/shard_map/all_gather | solution.py:178
  430.8 44.7 %all-to-all-start.2 = ((f32[32,1,1,128,64]{3,4,2,1,0:T(8,128)}), f32[32,1,1,128,64]{3,4,2,1,0:T(8,128)S(1)}, u32[]{:S(2)}, u32[]{:S(2)}) async-start(f32[32,1,1,128,64]{3,4,2,1,0:T(8,128)} %copy-done.24), calls=%async_computation.2 | async-start | bytes 2097152 | tf_op jit(solution)/shard_map/all_to_all | solution.py:268
  437.2 1.4 collective-permute-start.8
  490.2 14.6 %copy-start.13 = (bf16[1,128,2048]{2,1,0:T(8,128)(2,1)}, bf16[1,128,2048]{2,1,0:T(8,128)(2,1)S(1)}, u32[]{:S(2)}) copy-start(bf16[1,128,2048]{2,1,0:T(8,128)(2,1)S(1)} %get-tuple-element.188) | copy-start | bytes 1572868
  506.6 97.3 %collective-permute-start.10 = (bf16[1,3,2048]{1,2,0:T(8,128)(2,1)}, bf16[1,3,2048]{1,2,0:T(8,128)(2,1)}, u32[]{:S(2)}, u32[]{:S(2)}) collective-permute-start(bf16[1,3,2048]{1,2,0:T(8,128)(2,1)} %slice.406), channel_id=1, source_target_pairs={{0,1},{1,2},{2,3},{3,4},{4,5},{5,6},{6,7},{7,8},{8,9},{9,10},{10,1... | collective-permute-start | bytes 36872 | tf_op jit(solution)/shard_map/ppermute | solution.py:20
  512.5 19.2 %collective-permute-start.9 = (bf16[1,3,2048]{1,2,0:T(8,128)(2,1)S(1)}, bf16[1,3,2048]{1,2,0:T(8,128)(2,1)S(1)}, u32[]{:S(2)}, u32[]{:S(2)}) collective-permute-start(bf16[1,3,2048]{1,2,0:T(8,128)(2,1)S(1)} %slice.380), channel_id=1, source_target_pairs={{0,1},{1,2},{2,3},{3,4},{4,5},{5,6},{6,7},{7,8},{8,9},{9,10},{10,1... | collective-permute-start | bytes 36872 | tf_op jit(solution)/shard_map/ppermute | solution.py:20
  538.7 30.8 %copy-start.2 = (f32[16,128,128]{2,1,0:T(8,128)}, f32[16,128,128]{2,1,0:T(8,128)S(1)}, u32[]{:S(2)}) copy-start(f32[16,128,128]{2,1,0:T(8,128)S(1)} %fusion.13) | copy-start | bytes 3145732
  600.4 12.1 %copy-start.19 = (f32[128,8,128]{2,0,1:T(8,128)S(1)}, f32[128,8,128]{2,0,1:T(8,128)}, u32[]{:S(2)}) copy-start(f32[128,8,128]{2,0,1:T(8,128)} %copy-done.18) | copy-start | bytes 1572868
  615.6 5.6 copy-start.11
  624.2 33.5 %all-to-all-start.4 = ((f32[1,1,32,128,64]{3,4,1,0,2:T(8,128)}), f32[1,1,32,128,64]{3,4,1,0,2:T(8,128)}, u32[]{:S(2)}, u32[]{:S(2)}) async-start(f32[1,1,32,128,64]{3,4,1,0,2:T(8,128)} %bitcast.247), calls=%async_computation.4 | async-start | bytes 2097152 | tf_op jit(solution)/shard_map/all_to_all | solution.py:260
  632.8 126.1 %copy-start.8 = (f32[128,8,2,128]{3,0,2,1:T(8,128)S(1)}, f32[128,8,2,128]{3,0,2,1:T(8,128)}, u32[]{:S(2)}) copy-start(f32[128,8,2,128]{3,0,2,1:T(8,128)} %copy-done.7) | copy-start | bytes 3145732
  748.2 29.5 %all-to-all-start.5 = ((f32[32,1,1,128,64]{3,4,2,1,0:T(8,128)}), f32[32,1,1,128,64]{3,4,2,1,0:T(8,128)S(1)}, u32[]{:S(2)}, u32[]{:S(2)}) async-start(f32[32,1,1,128,64]{3,4,2,1,0:T(8,128)} %copy-done.23), calls=%async_computation.5 | async-start | bytes 2097152 | tf_op jit(solution)/shard_map/all_to_all | solution.py:268
  777.6 13.4 %copy-start.14 = (bf16[1,128,2048]{2,1,0:T(8,128)(2,1)S(1)}, bf16[1,128,2048]{2,1,0:T(8,128)(2,1)}, u32[]{:S(2)}) copy-start(bf16[1,128,2048]{2,1,0:T(8,128)(2,1)} %copy-done.13) | copy-start | bytes 1572868
  (21 other events, 55.8 us)
Sparse Core Ops, SparseCore 0:
  13.7 103.2 all-gather.11
  119.7 95.8 all-gather.5
  218.2 138.5 all-gather.7
  366.2 122.6 all-gather.9

commit v5 on v4

--- a/solution.py
+++ b/solution.py
@@ -192,21 +192,21 @@
 def layer_apply(section_input, full_first, full_second, gain_in, conv_taps, decay_rates, biases, gain_out):
     groups, positions, model_width = section_input.shape
     blocks = positions // BLOCK
-    layer_normed = (
-        rms_rows(section_input.astype(jnp.float32), gain_in)
-        .astype(jnp.bfloat16)
-        .reshape(groups * positions, model_width)
-    )
+    own_normed = rms_rows(section_input.astype(jnp.float32), gain_in).astype(jnp.bfloat16)
+    previous_normed = from_behind(own_normed[:, positions - (CONV - 1) :], "ctx", 1)
+    extended = jnp.concatenate([previous_normed, own_normed], axis=1)
+    extended_rows = extended.shape[1]
+    layer_normed = extended.reshape(groups * extended_rows, model_width)
     projected = jnp.dot(layer_normed, full_first, preferred_element_type=jnp.float32)
     qk_width = full_first.shape[1] - 2 * NV
-    features_qk = projected[:, :qk_width].astype(jnp.bfloat16).reshape(groups, positions, qk_width)
-    gate_raw = projected[:, qk_width:].astype(jnp.bfloat16)
+    projected = projected.reshape(groups, extended_rows, projected.shape[1])
+    features_qk = projected[:, :, :qk_width].astype(jnp.bfloat16)
+    gate_raw = projected[:, CONV - 1 :, qk_width:].astype(jnp.bfloat16).reshape(groups * positions, 2 * NV)
     proj_v = jnp.dot(layer_normed, full_second, preferred_element_type=jnp.float32)
-    features_v = proj_v.astype(jnp.bfloat16).reshape(groups, positions, proj_v.shape[1])
+    features_v = proj_v.astype(jnp.bfloat16).reshape(groups, extended_rows, proj_v.shape[1])
 
     def mixed_part(features, taps):
-        previous_rows = from_behind(features[:, positions - (CONV - 1) :], "ctx", 1)
-        mixed = conv_rows(jnp.concatenate([previous_rows, features], axis=1), taps)
+        mixed = conv_rows(features, taps)
         return mixed.reshape(groups * positions, mixed.shape[2])
 
     queries, key_rows, values, strength, logdecay = head_inputs(

time: 811 us -> 787 us (0.970)
  local copies, waits for them, and re-layouts: 132 us -> 178 us
  waiting for transfers between devices: 307 us -> 280 us
  matrix products: 199 us -> 179 us
  starting transfers between devices: 56.8 us -> 44.1 us
    ppermute x4 -> x2, waiting for transfers between devices: 103 us -> 1.52 us  [from_behind(): return lax.ppermute(value, axis, pairs)]
    all_gather x2, waiting for transfers between devices: 103 us -> 163 us  [local(): full_first = lax.all_gather(first_shard, 'ctx', axis=0, tiled=True)]
    dynamic_update_slice x64, local copies, waits for them, and re-layouts: 0.61 us -> 39 us  [layer_apply(): lax.scan(chain_step, jnp.zeros(got_bias.shape[1:], jnp.float32), (got_map...]
    all_to_all x1, waiting for transfers between devices: 0.01 us -> 37.7 us  [layer_apply(): lax.all_to_all(sent_maps, 'ctx', split_axis=2, concat_axis=0, tiled=True)]
    all_to_all x2, waiting for transfers between devices: 53.3 us -> 27 us  [layer_apply(): lax.all_to_all(sent_bias, 'ctx', split_axis=2, concat_axis=0, tiled=True)]
  transfers between devices with their start and end apart: 20 -> 18, of which waited for: 11 -> 13; matrix products, arithmetic and copies ran while one was open for 35% -> 35% of each run, Pallas kernels for 0% -> 0%
where the time goes in v5:
time: 787 us; the launch traced here: 779 us
  waiting for transfers between devices  280 us (36%)
  matrix products  179 us (23%)
  local copies, waits for them, and re-layouts  178 us (23%)
  blocking collectives  55.4 us (7%)
  starting transfers between devices  44.1 us (6%)
  other arithmetic  26.6 us (3%)
  between operations  14.8 us (2%)
    all_gather x2, waiting for transfers between devices, local(): full_first = lax.all_gather(first_shard, 'ctx', axis=0, tiled=True)  163 us
    dot_general x68, matrix products, chain_product(): jnp.einsum('...ij,...jk->...ik', left_map, right_map, precision=PRECISE)  76.9 us
    all_to_all x1, blocking collectives, layer_apply(): lax.all_to_all(sent_maps, 'ctx', split_axis=2, concat_axis=0, tiled=True)  55.4 us
    reshape x12, local copies, waits for them, and re-layouts, unit_lower_inverse(): tiles = strict_part.reshape(lead + (pairs, 2 * width, pairs, 2 * width))  48.7 us
    all_to_all x2, waiting for transfers between devices, layer_apply(): lax.all_to_all(entering_parts, 'ctx', split_axis=0, concat_axis=2, tiled=...  46.5 us
    dynamic_update_slice x64, local copies, waits for them, and re-layouts, layer_apply(): lax.scan(chain_step, jnp.zeros(got_bias.shape[1:], jnp.float32), (got_map...  39 us
    all_to_all x1, waiting for transfers between devices, layer_apply(): lax.all_to_all(sent_maps, 'ctx', split_axis=2, concat_axis=0, tiled=True)  37.7 us
    all_to_all x2, waiting for transfers between devices, layer_apply(): lax.all_to_all(sent_bias, 'ctx', split_axis=2, concat_axis=0, tiled=True)  27 us
  transfers between devices with their start and end apart: 18, of which 13 were waited for; matrix products, arithmetic and copies ran while one was open for 35% of the time, Pallas kernels for 0%

profile of v5, /device:TPU:8, one launch (start us, length us, event | category | flops | bytes accessed | tf_op | source)
XLA Modules:
  0.0 778.6 jit_solution(13696277895296583959)
XLA Ops:
  13.8 103.4 %all-gather.12.cloned.1.call-done = bf16[1,2048,2080]{2,1,0:T(8,128)(2,1)} async-done(((bf16[1,64,2080]{2,1,0:T(8,128)(2,1)}), bf16[1,2048,2080]{2,1,0:T(8,128)(2,1)}) %all-gather.12.cloned.1.call-update) | async-done | bytes 8519696 | tf_op jit(solution)/shard_map/all_gather | solution.py:176
  122.7 7.1 fusion.10
  137.0 4.7 copy.253
  141.7 4.6 reshape.973
  152.1 7.8 %copy.357 = f32[1,16,16,8,16,8]{1,5,4,2,3,0:T(8,128)} copy(f32[1,16,16,8,16,8]{1,5,4,3,2,0:T(8,128)} %bitcast.679) | data formatting | bytes 2097152 | tf_op jit(solution)/shard_map/reshape | solution.py:62
  160.0 4.0 gather_fusion
  165.7 9.2 %copy.356 = f32[1,16,8,16,8,16]{5,3,4,2,1,0:T(8,128)} copy(f32[1,16,8,16,8,16]{5,4,3,2,1,0:T(8,128)} %reshape.973) | data formatting | bytes 2097152 | tf_op jit(solution)/shard_map/reshape | solution.py:75
  174.9 4.1 gather_fusion.1
  180.1 4.9 copy.359
  215.3 9.5 %all-to-all-start = ((f32[1,1,32,128,128]{4,3,1,0,2:T(8,128)}), f32[1,1,32,128,128]{4,3,1,0,2:T(8,128)}, u32[]{:S(2)}, u32[]{:S(2)}) async-start(f32[1,1,32,128,128]{4,3,1,0,2:T(8,128)} %bitcast.711), calls=%async_computation | async-start | bytes 4194304 | tf_op jit(solution)/shard_map/all_to_all | solution.py:259
  228.1 7.0 fusion.12
  246.7 37.7 %all-to-all-done = f32[1,1,32,128,128]{4,3,1,0,2:T(8,128)} async-done(((f32[1,1,32,128,128]{4,3,1,0,2:T(8,128)}), f32[1,1,32,128,128]{4,3,1,0,2:T(8,128)}, u32[]{:S(2)}, u32[]{:S(2)}) %all-to-all-start) | async-done | bytes 2097184 | tf_op jit(solution)/shard_map/all_to_all | solution.py:259
  284.4 6.0 all-to-all-start.1
  290.4 59.7 %all-gather.8.cloned.1.call-done = bf16[2048,2080]{1,0:T(8,128)(2,1)} async-done(((bf16[64,2080]{1,0:T(8,128)(2,1)}), bf16[2048,2080]{1,0:T(8,128)(2,1)}) %all-gather.8.cloned.1.call-update) | async-done | bytes 8519696 | tf_op jit(solution)/shard_map/all_gather | solution.py:176
  351.3 55.1 %while.4 = (s32[]{:T(128)}, f32[1,1,128,64]{2,3,1,0:T(8,128)S(1)}, f32[32,1,1,128,64]{3,4,2,1,0:T(8,128)}, f32[32,1,1,128,128]{4,3,2,1,0:T(8,128)}, f32[32,1,1,128,64]{3,4,2,1,0:T(8,128)S(1)}, /*index=5*/s32[]{:T(128)}) while((s32[]{:T(128)}, f32[1,1,128,64]{2,3,1,0:T(8,128)S(1)}, f32[32,1,1,128,64]{3,4,2,1,0:T(8,128)}, ...), condition=%wide.region_5.6_spmd, body=%wide.region_4.5_spmd.sunk | while | flops 12591106 | bytes 296517 | solution.py:265
  406.4 7.2 all-to-all-start.2
  424.1 27.4 %all-to-all-done.2 = f32[32,1,1,128,64]{3,4,2,1,0:T(8,128)S(1)} async-done(((f32[32,1,1,128,64]{3,4,2,1,0:T(8,128)}), f32[32,1,1,128,64]{3,4,2,1,0:T(8,128)S(1)}, u32[]{:S(2)}, u32[]{:S(2)}) %all-to-all-start.2) | async-done | bytes 1048608 | tf_op jit(solution)/shard_map/all_to_all | solution.py:268
  462.7 5.8 collective-permute-start.8
  469.6 7.1 fusion.11
  483.9 4.7 copy.285
  488.6 4.5 reshape.1013
  498.9 7.7 copy.355
  512.5 8.7 %copy.354 = f32[1,16,8,16,8,16]{5,3,4,2,1,0:T(8,128)} copy(f32[1,16,8,16,8,16]{5,4,3,2,1,0:T(8,128)} %reshape.1013) | data formatting | bytes 2097152 | tf_op jit(solution)/shard_map/reshape | solution.py:75
  521.2 4.0 gather_fusion.5
  526.3 4.7 copy.358
  554.6 7.0 fusion.13
  579.8 6.8 all-to-all-start.4
  587.6 27.0 %all-to-all-done.4 = f32[1,1,32,128,64]{3,4,1,0,2:T(8,128)} async-done(((f32[1,1,32,128,64]{3,4,1,0,2:T(8,128)}), f32[1,1,32,128,64]{3,4,1,0,2:T(8,128)}, u32[]{:S(2)}, u32[]{:S(2)}) %all-to-all-start.4) | async-done | bytes 1048608 | tf_op jit(solution)/shard_map/all_to_all | solution.py:260
  614.9 55.4 %all_to_all.66 = f32[1,1,32,128,128]{4,3,1,0,2:T(8,128)} all-to-all(f32[1,1,32,128,128]{4,3,1,0,2:T(8,128)S(1)} %bitcast.712), channel_id=1, replica_groups=mesh['section'=2,'dp'=4,'ctx'=32] {'ctx'}, dimensions={2} | all-to-all | bytes 4194304 | tf_op jit(solution)/shard_map/all_to_all | solution.py:259
  671.5 55.2 %while.5 = (s32[]{:T(128)}, f32[1,1,128,64]{2,3,1,0:T(8,128)S(1)}, f32[32,1,1,128,64]{3,4,2,1,0:T(8,128)}, f32[32,1,1,128,128]{4,3,2,1,0:T(8,128)}, f32[32,1,1,128,64]{3,4,2,1,0:T(8,128)}, /*index=5*/s32[]{:T(128)}) while((s32[]{:T(128)}, f32[1,1,128,64]{2,3,1,0:T(8,128)S(1)}, f32[32,1,1,128,64]{3,4,2,1,0:T(8,128)}, ...), condition=%wide.region_12.13_spmd, body=%wide.region_11.12_spmd.sunk | while | flops 12591106 | bytes 296517 | solution.py:265
  726.7 5.1 all-to-all-start.5
  740.8 19.1 %all-to-all-done.5 = f32[32,1,1,128,64]{3,4,2,1,0:T(8,128)S(1)} async-done(((f32[32,1,1,128,64]{3,4,2,1,0:T(8,128)}), f32[32,1,1,128,64]{3,4,2,1,0:T(8,128)S(1)}, u32[]{:S(2)}, u32[]{:S(2)}) %all-to-all-start.5) | async-done | bytes 1048608 | tf_op jit(solution)/shard_map/all_to_all | solution.py:268
  (479 shorter events, 289.9 us)
Async XLA Ops:
  6.5 110.8 %copy-start.43 = (f32[1,2048]{1,0:T(1,128)S(1)}, f32[1,2048]{1,0:T(1,128)}, u32[]{:S(2)}) copy-start(f32[1,2048]{1,0:T(1,128)} %param.15) | copy-start | bytes 24580
  6.5 110.9 %copy-start.38 = (bf16[1,4,4096]{2,1,0:T(4,128)(2,1)S(1)}, bf16[1,4,4096]{2,1,0:T(4,128)(2,1)}, u32[]{:S(2)}) copy-start(bf16[1,4,4096]{2,1,0:T(4,128)(2,1)} %param.16) | copy-start | bytes 98308
  6.5 111.4 %copy-start.44 = (f32[1,16]{1,0:T(1,128)S(1)}, f32[1,16]{1,0:T(1,128)}, u32[]{:S(2)}) copy-start(f32[1,16]{1,0:T(1,128)} %param.17) | copy-start | bytes 196
  6.5 111.5 %copy-start.45 = (f32[1,16]{1,0:T(1,128)S(1)}, f32[1,16]{1,0:T(1,128)}, u32[]{:S(2)}) copy-start(f32[1,16]{1,0:T(1,128)} %param.18) | copy-start | bytes 196
  6.5 111.9 %copy-start.35 = (bf16[2,128,2048]{2,1,0:T(8,128)(2,1)S(1)}, bf16[2,128,2048]{2,1,0:T(8,128)(2,1)}, u32[]{:S(2)}) copy-start(bf16[2,128,2048]{2,1,0:T(8,128)(2,1)} %param.12) | copy-start | bytes 3145732
  6.6 110.7 %all-gather.12.cloned.1.call-start = ((), (), s32[]{:S(2)}) async-start(), calls=%async_computation.9 | async-start | bytes 9191424 | tf_op jit(solution)/shard_map/all_gather | solution.py:176
  7.7 1.6 collective-permute-start.4
  11.2 1.6 collective-permute-start.3
  13.8 214.3 %all-gather.6.cloned.1.call-start = ((), (), s32[]{:S(2)}) async-start(), calls=%async_computation.6 | async-start | bytes 8650752 | tf_op jit(solution)/shard_map/all_gather | solution.py:178
  117.2 232.9 %all-gather.8.cloned.1.call-start = ((), (), s32[]{:S(2)}) async-start(), calls=%async_computation.7 | async-start | bytes 9191424 | tf_op jit(solution)/shard_map/all_gather | solution.py:176
  117.3 2.0 collective-permute-start.1
  117.4 4.0 collective-permute-start.6
  117.9 1.2 collective-permute-start
  118.0 1.2 collective-permute-start.5
  119.5 10.3 %copy-start.36 = (bf16[1,128,2048]{2,1,0:T(8,128)(2,1)}, bf16[1,128,2048]{2,1,0:T(8,128)(2,1)S(1)}, u32[]{:S(2)}) copy-start(bf16[1,128,2048]{2,1,0:T(8,128)(2,1)S(1)} %fusion.32) | copy-start | bytes 1572868
  119.5 3.1 collective-permute-start.2
  137.0 12.7 %copy-start = (f32[16,128,128]{2,1,0:T(8,128)}, f32[16,128,128]{2,1,0:T(8,128)S(1)}, u32[]{:S(2)}) copy-start(f32[16,128,128]{2,1,0:T(8,128)S(1)} %fusion.16) | copy-start | bytes 3145732
  215.3 69.0 %all-to-all-start = ((f32[1,1,32,128,128]{4,3,1,0,2:T(8,128)}), f32[1,1,32,128,128]{4,3,1,0,2:T(8,128)}, u32[]{:S(2)}, u32[]{:S(2)}) async-start(f32[1,1,32,128,128]{4,3,1,0,2:T(8,128)} %bitcast.711), calls=%async_computation | async-start | bytes 4194304 | tf_op jit(solution)/shard_map/all_to_all | solution.py:259
  284.4 65.8 %all-to-all-start.1 = ((f32[1,1,32,128,64]{3,4,1,0,2:T(8,128)}), f32[1,1,32,128,64]{3,4,1,0,2:T(8,128)S(1)}, u32[]{:S(2)}, u32[]{:S(2)}) async-start(f32[1,1,32,128,64]{3,4,1,0,2:T(8,128)} %bitcast.122), calls=%async_computation.1 | async-start | bytes 2097152 | tf_op jit(solution)/shard_map/all_to_all | solution.py:260
  290.4 264.2 %all-gather.10.cloned.1.call-start = ((), (), s32[]{:S(2)}) async-start(), calls=%async_computation.8 | async-start | bytes 8650752 | tf_op jit(solution)/shard_map/all_gather | solution.py:178
  350.2 63.4 %copy-start.46 = (f32[1,128]{1,0:T(1,128)S(1)}, f32[1,128]{1,0:T(1,128)}, u32[]{:S(2)}) copy-start(f32[1,128]{1,0:T(1,128)} %param.19) | copy-start | bytes 1540
  406.4 45.1 %all-to-all-start.2 = ((f32[32,1,1,128,64]{3,4,2,1,0:T(8,128)}), f32[32,1,1,128,64]{3,4,2,1,0:T(8,128)S(1)}, u32[]{:S(2)}, u32[]{:S(2)}) async-start(f32[32,1,1,128,64]{3,4,2,1,0:T(8,128)} %get-tuple-element.138), calls=%async_computation.2 | async-start | bytes 2097152 | tf_op jit(solution)/shard_map/all_to_all | solution.py:268
  413.6 7.1 copy-start.5
  413.6 1.5 collective-permute-start.7
  424.1 31.0 %copy-start.11 = (f32[16,128,128]{2,1,0:T(8,128)S(1)}, f32[16,128,128]{2,1,0:T(8,128)}, u32[]{:S(2)}) copy-start(f32[16,128,128]{2,1,0:T(8,128)} %copy-done.10) | copy-start | bytes 3145732
  462.7 14.0 %copy-start.37 = (bf16[1,128,2048]{2,1,0:T(8,128)(2,1)}, bf16[1,128,2048]{2,1,0:T(8,128)(2,1)S(1)}, u32[]{:S(2)}) copy-start(bf16[1,128,2048]{2,1,0:T(8,128)(2,1)S(1)} %fusion.36) | copy-start | bytes 1572868
  462.7 6.9 collective-permute-start.8
  483.9 12.6 %copy-start.2 = (f32[16,128,128]{2,1,0:T(8,128)}, f32[16,128,128]{2,1,0:T(8,128)S(1)}, u32[]{:S(2)}) copy-start(f32[16,128,128]{2,1,0:T(8,128)S(1)} %fusion.17) | copy-start | bytes 3145732
  554.5 7.1 copy-start.39
  579.8 34.8 %all-to-all-start.4 = ((f32[1,1,32,128,64]{3,4,1,0,2:T(8,128)}), f32[1,1,32,128,64]{3,4,1,0,2:T(8,128)}, u32[]{:S(2)}, u32[]{:S(2)}) async-start(f32[1,1,32,128,64]{3,4,1,0,2:T(8,128)} %bitcast.247), calls=%async_computation.4 | async-start | bytes 2097152 | tf_op jit(solution)/shard_map/all_to_all | solution.py:260
  726.7 33.2 %all-to-all-start.5 = ((f32[32,1,1,128,64]{3,4,2,1,0:T(8,128)}), f32[32,1,1,128,64]{3,4,2,1,0:T(8,128)S(1)}, u32[]{:S(2)}, u32[]{:S(2)}) async-start(f32[32,1,1,128,64]{3,4,2,1,0:T(8,128)} %get-tuple-element.141), calls=%async_computation.5 | async-start | bytes 2097152 | tf_op jit(solution)/shard_map/all_to_all | solution.py:268
  740.8 22.6 %copy-start.27 = (f32[1,16,128,128]{3,2,1,0:T(8,128)S(1)}, f32[1,16,128,128]{3,2,1,0:T(8,128)}, u32[]{:S(2)}) copy-start(f32[1,16,128,128]{3,2,1,0:T(8,128)} %bitcast_multiply_fusion.5) | copy-start | bytes 3145732
  (33 other events, 90.5 us)
Sparse Core Ops, SparseCore 0:
  13.9 103.2 all-gather.11
  119.8 94.9 all-gather.5
  217.3 132.7 all-gather.7
  352.6 116.9 all-gather.9

commit v6 on v5

--- a/solution.py
+++ b/solution.py
@@ -168,15 +168,18 @@
     all_biases = every_layer(dt_bias)
     all_gain_out = every_layer(head_gain)
     hidden = lax.dynamic_slice_in_dim(tokens, section, 1, axis=0)
-    arrived = None
+    gathered_next = None
     for layer_index in range(layer_count):
-        first_shard = all_first[layer_index]
-        if arrived is not None:
-            arrived, first_shard = lax.optimization_barrier((arrived, first_shard))
-        full_first = lax.all_gather(first_shard, "ctx", axis=0, tiled=True)
-        full_first, second_shard = lax.optimization_barrier((full_first, all_second[layer_index]))
-        full_second = lax.all_gather(second_shard, "ctx", axis=0, tiled=True)
-        hidden, arrived = layer_apply(
+        full_first = lax.all_gather(all_first[layer_index], "ctx", axis=0, tiled=True)
+        if gathered_next is None:
+            full_first, second_shard = lax.optimization_barrier(
+                (full_first, all_second[layer_index])
+            )
+            full_second = lax.all_gather(second_shard, "ctx", axis=0, tiled=True)
+        else:
+            full_second = gathered_next
+        tie = all_second[layer_index + 1] if layer_index + 1 < layer_count else None
+        hidden, tied = layer_apply(
             hidden,
             full_first,
             full_second,
@@ -185,11 +188,16 @@
             all_rates[layer_index],
             all_biases[layer_index],
             all_gain_out[layer_index],
+            tie,
         )
+        if tied is not None:
+            gathered_next = lax.all_gather(tied, "ctx", axis=0, tiled=True)
     return hidden
 
 
-def layer_apply(section_input, full_first, full_second, gain_in, conv_taps, decay_rates, biases, gain_out):
+def layer_apply(
+    section_input, full_first, full_second, gain_in, conv_taps, decay_rates, biases, gain_out, tie
+):
     groups, positions, model_width = section_input.shape
     blocks = positions // BLOCK
     own_normed = rms_rows(section_input.astype(jnp.float32), gain_in).astype(jnp.bfloat16)
@@ -270,11 +278,13 @@
     )
     entering = returned_states[0].reshape(groups, NV, column_parts, DK, part_width)
     entering = jnp.moveaxis(entering, 2, 3).reshape(groups, NV, DK, DV)
+    if tie is not None:
+        entering, tie = lax.optimization_barrier((entering, tie))
     _, outputs = lax.scan(block_apply, entering, parts)
     outputs = jnp.transpose(outputs, (1, 0, 3, 2, 4)).reshape(groups, positions, NV, DV)
     normed_out = rms_rows(outputs, gain_out).reshape(groups, positions, NV * DV)
     outcome = (section_input.astype(jnp.float32) + normed_out).astype(jnp.bfloat16)
-    return outcome, step_biases
+    return outcome, tie
 
 
 def solution(mesh):

time: 787 us -> 719 us (0.914)
  waiting for transfers between devices: 280 us -> 229 us
  local copies, waits for them, and re-layouts: 178 us -> 160 us
  blocking collectives: 55.4 us -> 66.3 us
    all_gather x2 -> x3, waiting for transfers between devices: 163 us -> 103 us  [the longest x2 103 us: local(): lax.all_gather(all_first[layer_index], 'ctx', axis=0, tiled=True)]
    all_to_all x2 -> x1, waiting for transfers between devices: 46.5 us -> 19.2 us  [layer_apply(): lax.all_to_all(entering_parts, 'ctx', split_axis=0, concat_axis=2, tiled=...]
    all_to_all x1 -> x2, waiting for transfers between devices: 37.7 us -> 63.7 us  [layer_apply(): lax.all_to_all(sent_maps, 'ctx', split_axis=2, concat_axis=0, tiled=True)]
    dynamic_update_slice x64, local copies, waits for them, and re-layouts: 39 us -> 19.8 us  [layer_apply(): lax.scan(chain_step, jnp.zeros(got_bias.shape[1:], jnp.float32), (got_map...]
    all_to_all x1 -> x2, blocking collectives: 55.4 us -> 66.3 us  [the longest x1 33.9 us: layer_apply(): lax.all_to_all(sent_bias, 'ctx', split_axis=2, concat_axis=0, tiled=True)]
    all_to_all x2 -> x1, waiting for transfers between devices: 27 us -> 36.6 us  [layer_apply(): lax.all_to_all(sent_bias, 'ctx', split_axis=2, concat_axis=0, tiled=True)]
    all_to_all x1 -> x2, starting transfers between devices: 9.47 us -> 16.2 us  [layer_apply(): lax.all_to_all(sent_maps, 'ctx', split_axis=2, concat_axis=0, tiled=True)]
  transfers between devices with their start and end apart: 18 -> 17, of which waited for: 13 -> 12; matrix products, arithmetic and copies ran while one was open for 35% -> 39% of each run, Pallas kernels for 0% -> 0%
where the time goes in v6:
time: 719 us; the launch traced here: 710 us
  waiting for transfers between devices  229 us (32%)
  matrix products  176 us (24%)
  local copies, waits for them, and re-layouts  160 us (22%)
  blocking collectives  66.3 us (9%)
  starting transfers between devices  36.5 us (5%)
  other arithmetic  25.2 us (4%)
  between operations  14.8 us (2%)
    all_gather x2, waiting for transfers between devices, local(): lax.all_gather(all_first[layer_index], 'ctx', axis=0, tiled=True)  103 us
    dot_general x68, matrix products, chain_product(): jnp.einsum('...ij,...jk->...ik', left_map, right_map, precision=PRECISE)  78.4 us
    all_to_all x2, waiting for transfers between devices, layer_apply(): lax.all_to_all(sent_maps, 'ctx', split_axis=2, concat_axis=0, tiled=True)  63.7 us
    reshape x12, local copies, waits for them, and re-layouts, unit_lower_inverse(): tiles = strict_part.reshape(lead + (pairs, 2 * width, pairs, 2 * width))  48.7 us
    all_to_all x1, waiting for transfers between devices, layer_apply(): lax.all_to_all(sent_bias, 'ctx', split_axis=2, concat_axis=0, tiled=True)  36.6 us
    all_to_all x1, blocking collectives, layer_apply(): lax.all_to_all(sent_bias, 'ctx', split_axis=2, concat_axis=0, tiled=True)  33.9 us
    all_to_all x1, blocking collectives, layer_apply(): lax.all_to_all(entering_parts, 'ctx', split_axis=0, concat_axis=2, tiled=...  32.4 us
    dynamic_update_slice x64, local copies, waits for them, and re-layouts, layer_apply(): lax.scan(chain_step, jnp.zeros(got_bias.shape[1:], jnp.float32), (got_map...  19.8 us
  transfers between devices with their start and end apart: 17, of which 12 were waited for; matrix products, arithmetic and copies ran while one was open for 39% of the time, Pallas kernels for 0%

profile of v6, /device:TPU:8, one launch (start us, length us, event | category | flops | bytes accessed | tf_op | source)
XLA Modules:
  0.0 710.2 jit_solution(12149222869636067893)
XLA Ops:
  13.8 103.4 %all-gather.11.cloned.1.call-done = bf16[1,2048,2080]{2,1,0:T(8,128)(2,1)} async-done(((bf16[1,64,2080]{2,1,0:T(8,128)(2,1)}), bf16[1,2048,2080]{2,1,0:T(8,128)(2,1)}) %all-gather.11.cloned.1.call-update) | async-done | bytes 8519696 | tf_op jit(solution)/shard_map/all_gather | solution.py:173
  122.6 7.1 fusion.15
  136.9 4.7 copy.325
  141.6 4.6 reshape.973
  152.0 7.8 %copy.429 = f32[1,16,16,8,16,8]{1,5,4,2,3,0:T(8,128)} copy(f32[1,16,16,8,16,8]{1,5,4,3,2,0:T(8,128)} %bitcast.686) | data formatting | bytes 2097152 | tf_op jit(solution)/shard_map/reshape | solution.py:62
  159.8 4.0 gather_fusion
  165.6 9.2 %copy.428 = f32[1,16,8,16,8,16]{5,3,4,2,1,0:T(8,128)} copy(f32[1,16,8,16,8,16]{5,4,3,2,1,0:T(8,128)} %reshape.973) | data formatting | bytes 2097152 | tf_op jit(solution)/shard_map/reshape | solution.py:75
  174.8 4.1 gather_fusion.1
  180.1 4.8 copy.431
  215.2 9.4 %all-to-all-start = ((f32[1,1,32,128,128]{4,3,1,0,2:T(8,128)}), f32[1,1,32,128,128]{4,3,1,0,2:T(8,128)}, u32[]{:S(2)}, u32[]{:S(2)}) async-start(f32[1,1,32,128,128]{4,3,1,0,2:T(8,128)} %bitcast.718), calls=%async_computation | async-start | bytes 4194304 | tf_op jit(solution)/shard_map/all_to_all | solution.py:267
  228.6 7.0 fusion.19
  247.4 35.3 %all-to-all-done = f32[1,1,32,128,128]{4,3,1,0,2:T(8,128)} async-done(((f32[1,1,32,128,128]{4,3,1,0,2:T(8,128)}), f32[1,1,32,128,128]{4,3,1,0,2:T(8,128)}, u32[]{:S(2)}, u32[]{:S(2)}) %all-to-all-start) | async-done | bytes 2097184 | tf_op jit(solution)/shard_map/all_to_all | solution.py:267
  282.7 7.5 %all-to-all-start.1 = ((f32[1,1,32,128,64]{3,4,1,0,2:T(8,128)}), f32[1,1,32,128,64]{3,4,1,0,2:T(8,128)S(1)}, u32[]{:S(2)}, u32[]{:S(2)}) async-start(f32[1,1,32,128,64]{3,4,1,0,2:T(8,128)} %bitcast.122), calls=%async_computation.1 | async-start | bytes 2097152 | tf_op jit(solution)/shard_map/all_to_all | solution.py:268
  290.2 36.6 %all-to-all-done.1 = f32[1,1,32,128,64]{3,4,1,0,2:T(8,128)S(1)} async-done(((f32[1,1,32,128,64]{3,4,1,0,2:T(8,128)}), f32[1,1,32,128,64]{3,4,1,0,2:T(8,128)S(1)}, u32[]{:S(2)}, u32[]{:S(2)}) %all-to-all-start.1) | async-done | bytes 1048608 | tf_op jit(solution)/shard_map/all_to_all | solution.py:268
  326.9 36.4 %while.4 = (s32[]{:T(128)}, f32[1,1,128,64]{2,3,1,0:T(8,128)S(1)}, f32[32,1,1,128,64]{3,4,2,1,0:T(8,128)S(1)}, f32[32,1,1,128,128]{4,3,2,1,0:T(8,128)}, f32[32,1,1,128,64]{3,4,2,1,0:T(8,128)S(1)}, /*index=5*/s32[]{:T(128)}) while((s32[]{:T(128)}, f32[1,1,128,64]{2,3,1,0:T(8,128)S(1)}, f32[32,1,1,128,64]{3,4,2,1,0:T(8,128)S(1)}, ...), condition=%wide.region_5.6_spmd, body=%wide.region_4.5_spmd.sunk | while | flops 12591106 | bytes 296009 | solution.py:273
  363.4 32.4 %all_to_all.66 = f32[32,1,1,128,64]{3,4,2,1,0:T(8,128)S(1)} all-to-all(f32[32,1,1,128,64]{3,4,2,1,0:T(8,128)S(1)} %get-tuple-element.138), channel_id=1, replica_groups=mesh['section'=2,'dp'=4,'ctx'=32] {'ctx'}, dimensions={0} | all-to-all | bytes 2097152 | tf_op jit(solution)/shard_map/all_to_all | solution.py:276
  414.1 4.0 collective-permute-start.8
  419.1 7.2 %fusion.16 = bf16[1,131,2080]{1,2,0:T(8,128)(2,1)S(1)} fusion(bf16[1,2048,2080]{2,1,0:T(8,128)(2,1)} %all-gather.13.cloned.1.call-done, bf16[1,128,2048]{2,1,0:T(8,128)(2,1)S(1)} %fusion.43, bf16[1,3,2048]{2,1,0:T(4,128)(2,1)S(1)} %collective-permute-done.8), kind=kOutput, calls=%fused_computation.33 | convolution fusion | flops 1117423744 | bytes 9601216 | tf_op jit(solution)/shard_map/dot_general | solution.py:208
  433.6 4.7 copy.357
  438.3 4.6 reshape.1014
  448.6 7.9 %copy.427 = f32[1,16,16,8,16,8]{1,5,4,2,3,0:T(8,128)} copy(f32[1,16,16,8,16,8]{1,5,4,3,2,0:T(8,128)} %bitcast.687) | data formatting | bytes 2097152 | tf_op jit(solution)/shard_map/reshape | solution.py:62
  456.5 4.2 gather_fusion.4
  462.5 8.7 %copy.426 = f32[1,16,8,16,8,16]{5,3,4,2,1,0:T(8,128)} copy(f32[1,16,8,16,8,16]{5,4,3,2,1,0:T(8,128)} %reshape.1014) | data formatting | bytes 2097152 | tf_op jit(solution)/shard_map/reshape | solution.py:75
  471.2 4.1 gather_fusion.5
  476.5 4.8 copy.430
  511.6 6.8 all-to-all-start.3
  521.8 7.0 fusion.20
  539.5 28.4 %all-to-all-done.3 = f32[1,1,32,128,128]{4,3,1,0,2:T(8,128)} async-done(((f32[1,1,32,128,128]{4,3,1,0,2:T(8,128)}), f32[1,1,32,128,128]{4,3,1,0,2:T(8,128)}, u32[]{:S(2)}, u32[]{:S(2)}) %all-to-all-start.3) | async-done | bytes 2097184 | tf_op jit(solution)/shard_map/all_to_all | solution.py:267
  567.9 33.9 %all_to_all.67 = f32[1,1,32,128,64]{3,4,1,0,2:T(8,128)S(1)} all-to-all(f32[1,1,32,128,64]{3,4,1,0,2:T(8,128)S(1)} %bitcast.724), channel_id=1, replica_groups=mesh['section'=2,'dp'=4,'ctx'=32] {'ctx'}, dimensions={2} | all-to-all | bytes 2097152 | tf_op jit(solution)/shard_map/all_to_all | solution.py:268
  603.0 55.1 %while.5 = (s32[]{:T(128)}, f32[1,1,128,64]{2,3,1,0:T(8,128)S(1)}, f32[32,1,1,128,64]{3,4,2,1,0:T(8,128)}, f32[32,1,1,128,128]{4,3,2,1,0:T(8,128)}, f32[32,1,1,128,64]{3,4,2,1,0:T(8,128)S(1)}, /*index=5*/s32[]{:T(128)}) while((s32[]{:T(128)}, f32[1,1,128,64]{2,3,1,0:T(8,128)S(1)}, f32[32,1,1,128,64]{3,4,2,1,0:T(8,128)}, ...), condition=%wide.region_12.13_spmd, body=%wide.region_11.12_spmd.sunk | while | flops 12591106 | bytes 296517 | solution.py:273
  658.1 5.1 all-to-all-start.5
  672.2 19.2 %all-to-all-done.5 = f32[32,1,1,128,64]{3,4,2,1,0:T(8,128)S(1)} async-done(((f32[32,1,1,128,64]{3,4,2,1,0:T(8,128)}), f32[32,1,1,128,64]{3,4,2,1,0:T(8,128)S(1)}, u32[]{:S(2)}, u32[]{:S(2)}) %all-to-all-start.5) | async-done | bytes 1048608 | tf_op jit(solution)/shard_map/all_to_all | solution.py:276
  (486 shorter events, 264.7 us)
Async XLA Ops:
  6.5 110.7 %copy-start.47 = (f32[1,2048]{1,0:T(1,128)S(1)}, f32[1,2048]{1,0:T(1,128)}, u32[]{:S(2)}) copy-start(f32[1,2048]{1,0:T(1,128)} %param.15) | copy-start | bytes 24580
  6.5 110.8 %copy-start.42 = (bf16[1,4,4096]{2,1,0:T(4,128)(2,1)S(1)}, bf16[1,4,4096]{2,1,0:T(4,128)(2,1)}, u32[]{:S(2)}) copy-start(bf16[1,4,4096]{2,1,0:T(4,128)(2,1)} %param.16) | copy-start | bytes 98308
  6.5 111.3 %copy-start.48 = (f32[1,16]{1,0:T(1,128)S(1)}, f32[1,16]{1,0:T(1,128)}, u32[]{:S(2)}) copy-start(f32[1,16]{1,0:T(1,128)} %param.17) | copy-start | bytes 196
  6.5 111.4 %copy-start.49 = (f32[1,16]{1,0:T(1,128)S(1)}, f32[1,16]{1,0:T(1,128)}, u32[]{:S(2)}) copy-start(f32[1,16]{1,0:T(1,128)} %param.18) | copy-start | bytes 196
  6.5 111.8 %copy-start.39 = (bf16[2,128,2048]{2,1,0:T(8,128)(2,1)S(1)}, bf16[2,128,2048]{2,1,0:T(8,128)(2,1)}, u32[]{:S(2)}) copy-start(bf16[2,128,2048]{2,1,0:T(8,128)(2,1)} %param.12) | copy-start | bytes 3145732
  6.6 110.7 %all-gather.11.cloned.1.call-start = ((), (), s32[]{:S(2)}) async-start(), calls=%async_computation.8 | async-start | bytes 9191424 | tf_op jit(solution)/shard_map/all_gather | solution.py:173
  7.7 1.6 collective-permute-start.4
  11.2 1.6 collective-permute-start.3
  13.8 214.9 %all-gather.7.cloned.1.call-start = ((), (), s32[]{:S(2)}) async-start(), calls=%async_computation.6 | async-start | bytes 8650752 | tf_op jit(solution)/shard_map/all_gather | solution.py:178
  117.3 1.9 collective-permute-start.1
  117.4 4.0 collective-permute-start.6
  117.9 1.2 collective-permute-start
  118.0 1.2 collective-permute-start.5
  119.4 10.3 %copy-start.40 = (bf16[1,128,2048]{2,1,0:T(8,128)(2,1)}, bf16[1,128,2048]{2,1,0:T(8,128)(2,1)S(1)}, u32[]{:S(2)}) copy-start(bf16[1,128,2048]{2,1,0:T(8,128)(2,1)S(1)} %fusion.39) | copy-start | bytes 1572868
  119.4 3.1 collective-permute-start.2
  136.9 12.6 %copy-start.2 = (f32[16,128,128]{2,1,0:T(8,128)}, f32[16,128,128]{2,1,0:T(8,128)S(1)}, u32[]{:S(2)}) copy-start(f32[16,128,128]{2,1,0:T(8,128)S(1)} %fusion.23) | copy-start | bytes 3145732
  215.2 67.5 %all-to-all-start = ((f32[1,1,32,128,128]{4,3,1,0,2:T(8,128)}), f32[1,1,32,128,128]{4,3,1,0,2:T(8,128)}, u32[]{:S(2)}, u32[]{:S(2)}) async-start(f32[1,1,32,128,128]{4,3,1,0,2:T(8,128)} %bitcast.718), calls=%async_computation | async-start | bytes 4194304 | tf_op jit(solution)/shard_map/all_to_all | solution.py:267
  224.7 193.5 %all-gather.13.cloned.1.call-start = ((), (), s32[]{:S(2)}) async-start(), calls=%async_computation.9 | async-start | bytes 9191424 | tf_op jit(solution)/shard_map/all_gather | solution.py:173
  282.7 44.1 %all-to-all-start.1 = ((f32[1,1,32,128,64]{3,4,1,0,2:T(8,128)}), f32[1,1,32,128,64]{3,4,1,0,2:T(8,128)S(1)}, u32[]{:S(2)}, u32[]{:S(2)}) async-start(f32[1,1,32,128,64]{3,4,1,0,2:T(8,128)} %bitcast.122), calls=%async_computation.1 | async-start | bytes 2097152 | tf_op jit(solution)/shard_map/all_to_all | solution.py:268
  290.2 231.6 %all-gather.9.cloned.1.call-start = ((), (), s32[]{:S(2)}) async-start(), calls=%async_computation.7 | async-start | bytes 8650752 | tf_op jit(solution)/shard_map/all_gather | solution.py:194
  326.9 68.9 %copy-start.50 = (f32[1,128]{1,0:T(1,128)S(1)}, f32[1,128]{1,0:T(1,128)}, u32[]{:S(2)}) copy-start(f32[1,128]{1,0:T(1,128)} %param.19) | copy-start | bytes 1540
  395.8 1.5 collective-permute-start.7
  414.1 12.2 %copy-start.41 = (bf16[1,128,2048]{2,1,0:T(8,128)(2,1)}, bf16[1,128,2048]{2,1,0:T(8,128)(2,1)S(1)}, u32[]{:S(2)}) copy-start(bf16[1,128,2048]{2,1,0:T(8,128)(2,1)S(1)} %fusion.43) | copy-start | bytes 1572868
  414.1 5.0 collective-permute-start.8
  433.6 12.6 %copy-start = (f32[16,128,128]{2,1,0:T(8,128)}, f32[16,128,128]{2,1,0:T(8,128)S(1)}, u32[]{:S(2)}) copy-start(f32[16,128,128]{2,1,0:T(8,128)S(1)} %fusion.24) | copy-start | bytes 3145732
  511.6 56.3 %all-to-all-start.3 = ((f32[1,1,32,128,128]{4,3,1,0,2:T(8,128)}), f32[1,1,32,128,128]{4,3,1,0,2:T(8,128)}, u32[]{:S(2)}, u32[]{:S(2)}) async-start(f32[1,1,32,128,128]{4,3,1,0,2:T(8,128)} %bitcast.719), calls=%async_computation.3 | async-start | bytes 4194304 | tf_op jit(solution)/shard_map/all_to_all | solution.py:267
  521.7 7.1 copy-start.43
  521.7 7.1 copy-start.44
  521.7 7.1 copy-start.45
  521.7 7.1 %copy-start.46 = (f32[1,2048]{1,0:T(1,128)S(1)}, f32[1,2048]{1,0:T(1,128)}, u32[]{:S(2)}) copy-start(f32[1,2048]{1,0:T(1,128)} %get-tuple-element.253) | copy-start | bytes 24580
  658.1 33.4 %all-to-all-start.5 = ((f32[32,1,1,128,64]{3,4,2,1,0:T(8,128)}), f32[32,1,1,128,64]{3,4,2,1,0:T(8,128)S(1)}, u32[]{:S(2)}, u32[]{:S(2)}) async-start(f32[32,1,1,128,64]{3,4,2,1,0:T(8,128)} %get-tuple-element.141), calls=%async_computation.5 | async-start | bytes 2097152 | tf_op jit(solution)/shard_map/all_to_all | solution.py:276
  672.2 22.8 %copy-start.31 = (f32[1,16,128,128]{3,2,1,0:T(8,128)S(1)}, f32[1,16,128,128]{3,2,1,0:T(8,128)}, u32[]{:S(2)}) copy-start(f32[1,16,128,128]{3,2,1,0:T(8,128)} %bitcast_multiply_fusion.5) | copy-start | bytes 3145732
  (36 other events, 87.3 us)
Sparse Core Ops, SparseCore 0:
  13.9 103.2 all-gather.10
  119.8 94.8 all-gather.6
  228.0 129.0 all-gather.12
  395.9 94.6 all-gather.8

commit v7 on v6

--- a/solution.py
+++ b/solution.py
@@ -271,7 +271,7 @@
         return (chain_product(incoming[0], state_now) + incoming[1], state_now)
 
     _, entering_parts = lax.scan(
-        chain_step, jnp.zeros(got_bias.shape[1:], jnp.float32), (got_maps, got_bias)
+        chain_step, jnp.zeros(got_bias.shape[1:], jnp.float32), (got_maps, got_bias), unroll=4
     )
     returned_states = lax.all_to_all(
         entering_parts, "ctx", split_axis=0, concat_axis=2, tiled=True

time: 719 us -> 700 us (0.974)
  blocking collectives: 66.3 us -> 33.7 us
  waiting for transfers between devices: 229 us -> 261 us
  local copies, waits for them, and re-layouts: 160 us -> 137 us
    all_to_all x1 -> x0, blocking collectives: 33.9 us -> none  [layer_apply(): lax.all_to_all(sent_bias, 'ctx', split_axis=2, concat_axis=0, tiled=True)]
    all_to_all x1 -> x2, waiting for transfers between devices: 36.6 us -> 66.9 us  [layer_apply(): lax.all_to_all(sent_bias, 'ctx', split_axis=2, concat_axis=0, tiled=True)]
    dynamic_update_slice x64 -> x0, local copies, waits for them, and re-layouts: 19.8 us -> none  [layer_apply(): lax.scan(chain_step, jnp.zeros(got_bias.shape[1:], jnp.float32), (got_map...]
    unnamed x103 -> x113, local copies, waits for them, and re-layouts: 12.4 us -> 14.7 us
  transfers between devices with their start and end apart: 17 -> 18, of which waited for: 12 -> 13; matrix products, arithmetic and copies ran while one was open for 39% -> 40% of each run, Pallas kernels for 0% -> 0%
where the time goes in v7:
time: 700 us; the launch traced here: 692 us
  waiting for transfers between devices  261 us (37%)
  matrix products  178 us (25%)
  local copies, waits for them, and re-layouts  137 us (20%)
  starting transfers between devices  41.3 us (6%)
  blocking collectives  33.7 us (5%)
  other arithmetic  25.3 us (4%)
  between operations  14.9 us (2%)
    all_gather x2, waiting for transfers between devices, local(): lax.all_gather(all_first[layer_index], 'ctx', axis=0, tiled=True)  103 us
    dot_general x68, matrix products, chain_product(): jnp.einsum('...ij,...jk->...ik', left_map, right_map, precision=PRECISE)  78.7 us
    all_to_all x2, waiting for transfers between devices, layer_apply(): lax.all_to_all(sent_bias, 'ctx', split_axis=2, concat_axis=0, tiled=True)  66.9 us
    all_to_all x2, waiting for transfers between devices, layer_apply(): lax.all_to_all(sent_maps, 'ctx', split_axis=2, concat_axis=0, tiled=True)  65.7 us
    reshape x12, local copies, waits for them, and re-layouts, unit_lower_inverse(): tiles = strict_part.reshape(lead + (pairs, 2 * width, pairs, 2 * width))  46.4 us
    all_to_all x1, blocking collectives, layer_apply(): lax.all_to_all(entering_parts, 'ctx', split_axis=0, concat_axis=2, tiled=...  33.7 us
    all_to_all x1, waiting for transfers between devices, layer_apply(): lax.all_to_all(entering_parts, 'ctx', split_axis=0, concat_axis=2, tiled=...  19.3 us
    gather x12, local copies, waits for them, and re-layouts, unit_lower_inverse(): jnp.diagonal(tiles, axis1=-4, axis2=-2)  17.8 us
  transfers between devices with their start and end apart: 18, of which 13 were waited for; matrix products, arithmetic and copies ran while one was open for 40% of the time, Pallas kernels for 0%

profile of v7, /device:TPU:8, one launch (start us, length us, event | category | flops | bytes accessed | tf_op | source)
XLA Modules:
  0.0 692.2 jit_solution(13838442034782544299)
XLA Ops:
  13.8 103.4 %all-gather.11.cloned.1.call-done = bf16[1,2048,2080]{2,1,0:T(8,128)(2,1)} async-done(((bf16[1,64,2080]{2,1,0:T(8,128)(2,1)}), bf16[1,2048,2080]{2,1,0:T(8,128)(2,1)}) %all-gather.11.cloned.1.call-update) | async-done | bytes 8519696 | tf_op jit(solution)/shard_map/all_gather | solution.py:173
  122.6 7.1 %fusion.19 = bf16[1,131,2080]{1,2,0:T(8,128)(2,1)S(1)} fusion(bf16[2048,2080]{1,0:T(8,128)(2,1)} %bitcast.886, bf16[1,128,2048]{2,1,0:T(8,128)(2,1)S(1)} %fusion.43, bf16[1,3,2048]{2,1,0:T(4,128)(2,1)S(1)} %collective-permute-done.2), kind=kOutput, calls=%fused_computation.58 | convolution fusion | flops 1117423744 | bytes 9601216 | tf_op jit(solution)/shard_map/dot_general | solution.py:208
  136.9 4.7 copy.325
  141.6 4.6 reshape.1087
  152.3 7.9 %copy.429 = f32[1,16,16,8,16,8]{1,5,4,2,3,0:T(8,128)} copy(f32[1,16,16,8,16,8]{1,5,4,3,2,0:T(8,128)} %bitcast.804) | data formatting | bytes 2097152 | tf_op jit(solution)/shard_map/reshape | solution.py:62
  160.2 4.0 gather_fusion
  170.6 8.6 %copy.428 = f32[1,16,8,16,8,16]{5,3,4,2,1,0:T(8,128)} copy(f32[1,16,8,16,8,16]{5,4,3,2,1,0:T(8,128)} %reshape.1087) | data formatting | bytes 2097152 | tf_op jit(solution)/shard_map/reshape | solution.py:75
  179.2 4.1 gather_fusion.1
  210.0 9.5 %all-to-all-start = ((f32[1,1,32,128,128]{4,3,1,0,2:T(8,128)}), f32[1,1,32,128,128]{4,3,1,0,2:T(8,128)}, u32[]{:S(2)}, u32[]{:S(2)}) async-start(f32[1,1,32,128,128]{4,3,1,0,2:T(8,128)} %bitcast.837), calls=%async_computation | async-start | bytes 4194304 | tf_op jit(solution)/shard_map/all_to_all | solution.py:267
  222.7 7.0 %fusion.23 = bf16[1,131,2048]{1,2,0:T(8,128)(2,1)S(1)} fusion(bf16[2048,2048]{1,0:T(8,128)(2,1)} %all-gather.7.cloned.1.call-done, bf16[1,128,2048]{2,1,0:T(8,128)(2,1)} %copy-done.45, bf16[1,3,2048]{2,1,0:T(4,128)(2,1)S(1)} %collective-permute-done.2), kind=kOutput, calls=%fused_computation.62 | convolution fusion | flops 1100249088 | bytes 9461760 | tf_op jit(solution)/shard_map/dot_general | solution.py:213
  241.4 38.1 %all-to-all-done = f32[1,1,32,128,128]{4,3,1,0,2:T(8,128)} async-done(((f32[1,1,32,128,128]{4,3,1,0,2:T(8,128)}), f32[1,1,32,128,128]{4,3,1,0,2:T(8,128)}, u32[]{:S(2)}, u32[]{:S(2)}) %all-to-all-start) | async-done | bytes 2097184 | tf_op jit(solution)/shard_map/all_to_all | solution.py:267
  279.5 5.8 all-to-all-start.1
  285.4 38.5 %all-to-all-done.1 = f32[1,1,32,128,64]{3,4,1,0,2:T(8,128)S(1)} async-done(((f32[1,1,32,128,64]{3,4,1,0,2:T(8,128)}), f32[1,1,32,128,64]{3,4,1,0,2:T(8,128)S(1)}, u32[]{:S(2)}, u32[]{:S(2)}) %all-to-all-start.1) | async-done | bytes 1048608 | tf_op jit(solution)/shard_map/all_to_all | solution.py:268
  325.0 35.4 %while.4 = (s32[]{:T(128)}, f32[1,1,128,64]{2,3,1,0:T(8,128)S(1)}, f32[8,4,1,1,128,64]{4,5,1,3,2,0:T(8,128)S(1)}, f32[8,4,1,1,128,128]{5,4,3,2,1,0:T(8,128)}, f3...) while((s32[]{:T(128)}, f32[1,1,128,64]{2,3,1,0:T(8,128)S(1)}, ...), condition=%wide.region_5.6_spmd, body=%wide.region_4.5_spmd.sunk | while | flops 50462724 | bytes 924813 | solution.py:273
  361.4 33.7 %all_to_all.24 = f32[32,1,1,128,64]{3,4,2,1,0:T(8,128)S(1)} all-to-all(f32[32,1,1,128,64]{3,4,2,1,0:T(8,128)} %bitcast.847), channel_id=1, replica_groups=mesh['section'=2,'dp'=4,'ctx'=32] {'ctx'}, dimensions={0} | all-to-all | bytes 2097152 | tf_op jit(solution)/shard_map/all_to_all | solution.py:276
  413.8 3.9 collective-permute-start.8
  419.0 7.1 %fusion.20 = bf16[1,131,2080]{1,2,0:T(8,128)(2,1)S(1)} fusion(bf16[1,2048,2080]{2,1,0:T(8,128)(2,1)} %all-gather.13.cloned.1.call-done, bf16[1,128,2048]{2,1,0:T(8,128)(2,1)S(1)} %fusion.47, bf16[1,3,2048]{2,1,0:T(4,128)(2,1)S(1)} %collective-permute-done.8), kind=kOutput, calls=%fused_computation.59 | convolution fusion | flops 1117423744 | bytes 9601216 | tf_op jit(solution)/shard_map/dot_general | solution.py:208
  433.3 4.7 copy.357
  438.0 4.6 reshape.1131
  448.4 7.9 %copy.427 = f32[1,16,16,8,16,8]{1,5,4,2,3,0:T(8,128)} copy(f32[1,16,16,8,16,8]{1,5,4,3,2,0:T(8,128)} %bitcast.805) | data formatting | bytes 2097152 | tf_op jit(solution)/shard_map/reshape | solution.py:62
  456.3 4.2 gather_fusion.4
  462.3 8.8 %copy.426 = f32[1,16,8,16,8,16]{5,3,4,2,1,0:T(8,128)} copy(f32[1,16,8,16,8,16]{5,4,3,2,1,0:T(8,128)} %reshape.1131) | data formatting | bytes 2097152 | tf_op jit(solution)/shard_map/reshape | solution.py:75
  471.0 4.1 gather_fusion.5
  476.3 4.8 copy.430
  511.5 6.8 all-to-all-start.3
  521.6 7.0 %fusion.24 = bf16[1,131,2048]{1,2,0:T(8,128)(2,1)S(1)} fusion(bf16[2048,2048]{1,0:T(8,128)(2,1)} %all-gather.9.cloned.1.call-done, bf16[1,128,2048]{2,1,0:T(8,128)(2,1)} %copy-done.46, bf16[1,3,2048]{2,1,0:T(4,128)(2,1)S(1)} %collective-permute-done.8), kind=kOutput, calls=%fused_computation.63 | convolution fusion | flops 1100249088 | bytes 9461760 | tf_op jit(solution)/shard_map/dot_general | solution.py:213
  540.3 27.6 %all-to-all-done.3 = f32[1,1,32,128,128]{4,3,1,0,2:T(8,128)} async-done(((f32[1,1,32,128,128]{4,3,1,0,2:T(8,128)}), f32[1,1,32,128,128]{4,3,1,0,2:T(8,128)}, u32[]{:S(2)}, u32[]{:S(2)}) %all-to-all-start.3) | async-done | bytes 2097184 | tf_op jit(solution)/shard_map/all_to_all | solution.py:267
  567.9 6.1 all-to-all-start.4
  574.1 28.4 %all-to-all-done.4 = f32[1,1,32,128,64]{3,4,1,0,2:T(8,128)S(1)} async-done(((f32[1,1,32,128,64]{3,4,1,0,2:T(8,128)}), f32[1,1,32,128,64]{3,4,1,0,2:T(8,128)S(1)}, u32[]{:S(2)}, u32[]{:S(2)}) %all-to-all-start.4) | async-done | bytes 1048608 | tf_op jit(solution)/shard_map/all_to_all | solution.py:268
  603.6 35.4 %while.5 = (s32[]{:T(128)}, f32[1,1,128,64]{2,3,1,0:T(8,128)S(1)}, f32[8,4,1,1,128,64]{4,5,1,3,2,0:T(8,128)S(1)}, f32[8,4,1,1,128,128]{5,4,3,2,1,0:T(8,128)}, f3...) while((s32[]{:T(128)}, f32[1,1,128,64]{2,3,1,0:T(8,128)S(1)}, ...), condition=%wide.region_12.13_spmd, body=%wide.region_11.12_spmd.sunk | while | flops 50462724 | bytes 924813 | solution.py:273
  640.0 5.1 all-to-all-start.5
  654.1 19.3 %all-to-all-done.5 = f32[32,1,1,128,64]{3,4,2,1,0:T(8,128)S(1)} async-done(((f32[32,1,1,128,64]{3,4,2,1,0:T(8,128)}), f32[32,1,1,128,64]{3,4,2,1,0:T(8,128)S(1)}, u32[]{:S(2)}, u32[]{:S(2)}) %all-to-all-start.5) | async-done | bytes 1048608 | tf_op jit(solution)/shard_map/all_to_all | solution.py:276
  (385 shorter events, 249.0 us)
Async XLA Ops:
  6.5 110.8 %copy-start.52 = (f32[1,2048]{1,0:T(1,128)S(1)}, f32[1,2048]{1,0:T(1,128)}, u32[]{:S(2)}) copy-start(f32[1,2048]{1,0:T(1,128)} %param.15) | copy-start | bytes 24580
  6.5 110.9 %copy-start.47 = (bf16[1,4,4096]{2,1,0:T(4,128)(2,1)S(1)}, bf16[1,4,4096]{2,1,0:T(4,128)(2,1)}, u32[]{:S(2)}) copy-start(bf16[1,4,4096]{2,1,0:T(4,128)(2,1)} %param.16) | copy-start | bytes 98308
  6.5 111.4 %copy-start.53 = (f32[1,16]{1,0:T(1,128)S(1)}, f32[1,16]{1,0:T(1,128)}, u32[]{:S(2)}) copy-start(f32[1,16]{1,0:T(1,128)} %param.17) | copy-start | bytes 196
  6.5 111.5 %copy-start.54 = (f32[1,16]{1,0:T(1,128)S(1)}, f32[1,16]{1,0:T(1,128)}, u32[]{:S(2)}) copy-start(f32[1,16]{1,0:T(1,128)} %param.18) | copy-start | bytes 196
  6.5 111.9 %copy-start.41 = (bf16[2,128,2048]{2,1,0:T(8,128)(2,1)S(1)}, bf16[2,128,2048]{2,1,0:T(8,128)(2,1)}, u32[]{:S(2)}) copy-start(bf16[2,128,2048]{2,1,0:T(8,128)(2,1)} %param.12) | copy-start | bytes 3145732
  6.6 110.7 %all-gather.11.cloned.1.call-start = ((), (), s32[]{:S(2)}) async-start(), calls=%async_computation.8 | async-start | bytes 9191424 | tf_op jit(solution)/shard_map/all_gather | solution.py:173
  7.7 1.6 collective-permute-start.4
  11.2 1.6 collective-permute-start.3
  13.8 209.0 %all-gather.7.cloned.1.call-start = ((), (), s32[]{:S(2)}) async-start(), calls=%async_computation.6 | async-start | bytes 8650752 | tf_op jit(solution)/shard_map/all_gather | solution.py:178
  117.2 300.5 %all-gather.13.cloned.1.call-start = ((), (), s32[]{:S(2)}) async-start(), calls=%async_computation.9 | async-start | bytes 9191424 | tf_op jit(solution)/shard_map/all_gather | solution.py:173
  117.3 1.9 collective-permute-start.1
  117.4 4.1 collective-permute-start.6
  117.9 1.2 collective-permute-start
  118.0 1.2 collective-permute-start.5
  119.5 10.3 %copy-start.45 = (bf16[1,128,2048]{2,1,0:T(8,128)(2,1)}, bf16[1,128,2048]{2,1,0:T(8,128)(2,1)S(1)}, u32[]{:S(2)}) copy-start(bf16[1,128,2048]{2,1,0:T(8,128)(2,1)S(1)} %fusion.43) | copy-start | bytes 1572868
  119.5 3.1 collective-permute-start.2
  136.9 13.0 %copy-start.2 = (f32[16,128,128]{2,1,0:T(8,128)}, f32[16,128,128]{2,1,0:T(8,128)S(1)}, u32[]{:S(2)}) copy-start(f32[16,128,128]{2,1,0:T(8,128)S(1)} %fusion.27) | copy-start | bytes 3145732
  210.0 69.5 %all-to-all-start = ((f32[1,1,32,128,128]{4,3,1,0,2:T(8,128)}), f32[1,1,32,128,128]{4,3,1,0,2:T(8,128)}, u32[]{:S(2)}, u32[]{:S(2)}) async-start(f32[1,1,32,128,128]{4,3,1,0,2:T(8,128)} %bitcast.837), calls=%async_computation | async-start | bytes 4194304 | tf_op jit(solution)/shard_map/all_to_all | solution.py:267
  279.5 44.3 %all-to-all-start.1 = ((f32[1,1,32,128,64]{3,4,1,0,2:T(8,128)}), f32[1,1,32,128,64]{3,4,1,0,2:T(8,128)S(1)}, u32[]{:S(2)}, u32[]{:S(2)}) async-start(f32[1,1,32,128,64]{3,4,1,0,2:T(8,128)} %bitcast.142), calls=%async_computation.1 | async-start | bytes 2097152 | tf_op jit(solution)/shard_map/all_to_all | solution.py:268
  285.3 236.2 %all-gather.9.cloned.1.call-start = ((), (), s32[]{:S(2)}) async-start(), calls=%async_computation.7 | async-start | bytes 8650752 | tf_op jit(solution)/shard_map/all_gather | solution.py:194
  360.4 34.7 %copy-start.55 = (f32[1,128]{1,0:T(1,128)S(1)}, f32[1,128]{1,0:T(1,128)}, u32[]{:S(2)}) copy-start(f32[1,128]{1,0:T(1,128)} %param.19) | copy-start | bytes 1540
  395.1 1.7 collective-permute-start.7
  413.7 12.3 %copy-start.46 = (bf16[1,128,2048]{2,1,0:T(8,128)(2,1)}, bf16[1,128,2048]{2,1,0:T(8,128)(2,1)S(1)}, u32[]{:S(2)}) copy-start(bf16[1,128,2048]{2,1,0:T(8,128)(2,1)S(1)} %fusion.47) | copy-start | bytes 1572868
  413.8 5.2 collective-permute-start.8
  433.3 12.7 %copy-start = (f32[16,128,128]{2,1,0:T(8,128)}, f32[16,128,128]{2,1,0:T(8,128)S(1)}, u32[]{:S(2)}) copy-start(f32[16,128,128]{2,1,0:T(8,128)S(1)} %fusion.28) | copy-start | bytes 3145732
  511.5 56.5 %all-to-all-start.3 = ((f32[1,1,32,128,128]{4,3,1,0,2:T(8,128)}), f32[1,1,32,128,128]{4,3,1,0,2:T(8,128)}, u32[]{:S(2)}, u32[]{:S(2)}) async-start(f32[1,1,32,128,128]{4,3,1,0,2:T(8,128)} %bitcast.836), calls=%async_computation.3 | async-start | bytes 4194304 | tf_op jit(solution)/shard_map/all_to_all | solution.py:267
  521.5 7.1 %copy-start.48 = (f32[1,2048]{1,0:T(1,128)S(1)}, f32[1,2048]{1,0:T(1,128)}, u32[]{:S(2)}) copy-start(f32[1,2048]{1,0:T(1,128)} %get-tuple-element.250) | copy-start | bytes 24580
  521.5 7.1 %copy-start.49 = (f32[1,2048]{1,0:T(1,128)S(1)}, f32[1,2048]{1,0:T(1,128)}, u32[]{:S(2)}) copy-start(f32[1,2048]{1,0:T(1,128)} %get-tuple-element.251) | copy-start | bytes 24580
  521.5 7.1 %copy-start.50 = (f32[1,2048]{1,0:T(1,128)S(1)}, f32[1,2048]{1,0:T(1,128)}, u32[]{:S(2)}) copy-start(f32[1,2048]{1,0:T(1,128)} %get-tuple-element.252) | copy-start | bytes 24580
  521.5 7.1 %copy-start.51 = (f32[1,2048]{1,0:T(1,128)S(1)}, f32[1,2048]{1,0:T(1,128)}, u32[]{:S(2)}) copy-start(f32[1,2048]{1,0:T(1,128)} %get-tuple-element.253) | copy-start | bytes 24580
  567.9 34.5 %all-to-all-start.4 = ((f32[1,1,32,128,64]{3,4,1,0,2:T(8,128)}), f32[1,1,32,128,64]{3,4,1,0,2:T(8,128)S(1)}, u32[]{:S(2)}, u32[]{:S(2)}) async-start(f32[1,1,32,128,64]{3,4,1,0,2:T(8,128)} %bitcast.267), calls=%async_computation.4 | async-start | bytes 2097152 | tf_op jit(solution)/shard_map/all_to_all | solution.py:268
  640.0 33.4 %all-to-all-start.5 = ((f32[32,1,1,128,64]{3,4,2,1,0:T(8,128)}), f32[32,1,1,128,64]{3,4,2,1,0:T(8,128)S(1)}, u32[]{:S(2)}, u32[]{:S(2)}) async-start(f32[32,1,1,128,64]{3,4,2,1,0:T(8,128)} %bitcast.846), calls=%async_computation.5 | async-start | bytes 2097152 | tf_op jit(solution)/shard_map/all_to_all | solution.py:276
  (42 other events, 94.6 us)
Sparse Core Ops, SparseCore 0:
  13.9 103.2 all-gather.10
  119.8 94.8 all-gather.6
  217.3 135.7 all-gather.12
  395.3 94.6 all-gather.8
